TPU v7x, 128 devices: a whole 4x4x4 slice. The times are simulated.
128 devices in a mesh: tm: 4 (over y_hi, core), row: 8 (over y_lo, z), col: 4 (over x).
Axes of the slice: x: 4, y: 4 (y_hi: 2, y_lo: 2; y = y_hi * 2 + y_lo), z: 4, core: 2. Of those that a mesh axis runs over, the one named last changes fastest.
Arguments:
- latent: bfloat16 [16, 64, 32, 256], P('tm', 'row', 'col'), may hold values from -6 to 6
- w_first: bfloat16 [3, 3, 3, 256, 256], replicated, may hold values from -0.078125 to 0.078125
- b_first: float32 [256], replicated, may hold values from -3 to 3
- w_second: bfloat16 [3, 3, 3, 256, 256], replicated, may hold values from -0.078125 to 0.078125
- b_second: float32 [256], replicated, may hold values from -3 to 3
- upstream: bfloat16 [16, 128, 64, 256], P('tm', 'row', 'col'), may hold values from -6 to 6
- dropout_key: int32 [2], replicated, may hold values from 0 to 1073741823
Outputs:
- mixed: bfloat16 [16, 128, 64, 256], P('tm', 'row', 'col')
- grad_latent: bfloat16 [16, 64, 32, 256], P('tm', 'row', 'col')
- grad_first: float32 [3, 3, 3, 256, 256], replicated
- grad_second: float32 [3, 3, 3, 256, 256], replicated
All inputs are finite; a program needn't handle non-finite values.
Results may differ from a plain program's by a relative error of at most 0.0032.
Values may be sent and summed in bfloat16 or wider, within the bound.
No kernel may reach another device: no remote copies, remote signals or barrier semaphores. Data moves between devices by JAX's collectives and lax.ppermute only.
A program may use at most 128 MiB of HBM per device.

v0:
```python
import jax
import jax.numpy as jnp
from jax import lax
from jax.sharding import PartitionSpec as P

KEEP_LEVEL = 6554
KEEP_SCALE = 65536.0 / 58982.0


def shifted(block, axis, distance):
    devices = range(lax.axis_size(axis))
    route = [(i - distance, i) for i in devices if i - distance in devices]
    return lax.ppermute(block, axis, route)


def extended_2(cells, sides, width):
    for axis, dim in sides:
        count = lax.axis_size(axis)
        ends = count - 1
        head = lax.slice_in_dim(cells, 0, width, axis=dim)
        tail = lax.slice_in_dim(cells, cells.shape[dim] - width, cells.shape[dim], axis=dim)
        cells = jnp.concatenate(
            [
                lax.ppermute(tail, axis, [(i, (i + 1) % count) for i in range(ends)]),
                cells,
                lax.ppermute(head, axis, [((i + 1) % count, i) for i in range(ends)]),
            ],
            axis=dim,
        )
    return cells


def keep_mask(dropout_key, frame_start, row_start, col_start, shape, height_all, width_all):
    frame_idx = lax.broadcasted_iota(jnp.int32, shape, 0) + frame_start
    row_idx = lax.broadcasted_iota(jnp.int32, shape, 1) + row_start
    col_idx = lax.broadcasted_iota(jnp.int32, shape, 2) + col_start
    chan_idx = lax.broadcasted_iota(jnp.int32, shape, 3)
    linear = ((frame_idx * height_all + row_idx) * width_all + col_idx) * shape[3] + chan_idx
    state = linear * jnp.int32(-1640531535) + dropout_key[0]
    state = state ^ lax.shift_right_logical(state, jnp.full(shape, 16, jnp.int32))
    state = state * jnp.int32(-2048144789) + dropout_key[1]
    state = state ^ lax.shift_right_logical(state, jnp.full(shape, 13, jnp.int32))
    state = state * jnp.int32(-1028477387)
    state = state ^ lax.shift_right_logical(state, jnp.full(shape, 16, jnp.int32))
    kept = state & 65535 >= KEEP_LEVEL
    return jnp.where(kept, jnp.float32(KEEP_SCALE), jnp.float32(0.0))


def upsample(field):
    return jnp.repeat(jnp.repeat(field, 2, axis=1), 2, axis=2)


def unfold(extended):
    frames_out = extended.shape[0] - 2
    height = extended.shape[1] - 2
    width = extended.shape[2] - 2
    pieces = [
        extended[a : a + frames_out, b : b + height, c : c + width]
        for a in range(3)
        for b in range(3)
        for c in range(3)
    ]
    return jnp.concatenate(pieces, axis=-1).reshape(frames_out * height * width, -1)


def convolve(patches, weight, shape):
    matrix = weight.reshape(-1, weight.shape[-1])
    return jnp.dot(patches, matrix, preferred_element_type=jnp.float32).reshape(shape)


def flipped(weight):
    return jnp.swapaxes(weight[::-1, ::-1, ::-1], 3, 4)


def weight_gradient(patches, grad):
    channels = grad.shape[-1]
    summed = lax.dot_general(
        patches,
        grad.reshape(-1, channels),
        (((0,), (0,)), ((), ())),
        preferred_element_type=jnp.float32,
    )
    return summed.reshape(3, 3, 3, channels, channels)


def with_earlier(field):
    frames_here = field.shape[0]
    tail = shifted(field[frames_here - 2 :], "tm", 1)
    return jnp.concatenate([tail, field], axis=0)


def with_later(field):
    head = shifted(field[:2], "tm", -1)
    return jnp.concatenate([field, head], axis=0)


def face_cells(field):
    return extended_2(field, (("row", 1), ("col", 2)), 1)


def local(latent, w_first, b_first, w_second, b_second, upstream, dropout_key):
    frames_here, low_rows, low_cols, channels = latent.shape
    high_rows = 2 * low_rows
    high_cols = 2 * low_cols
    cell_shape = (frames_here, high_rows, high_cols, channels)
    frame_start = lax.axis_index("tm") * frames_here
    row_start = lax.axis_index("row") * high_rows
    col_start = lax.axis_index("col") * high_cols
    height_all = high_rows * lax.axis_size("row")
    width_all = high_cols * lax.axis_size("col")
    latent_ext = with_earlier(latent)
    cells_ext = face_cells(upsample(latent_ext))
    cells_here = cells_ext[2:, 1:-1, 1:-1]
    cells_patches = unfold(cells_ext)
    pre_first = convolve(cells_patches, w_first, cell_shape) + b_first
    scaling = keep_mask(
        dropout_key, frame_start, row_start, col_start, cell_shape, height_all, width_all
    )
    dropped = (jax.nn.silu(pre_first) * scaling).astype(jnp.bfloat16)
    dropped_patches = unfold(face_cells(with_earlier(dropped)))
    mixed = (
        cells_here.astype(jnp.float32) + convolve(dropped_patches, w_second, cell_shape) + b_second
    ).astype(jnp.bfloat16)
    upstream_patches = unfold(face_cells(with_later(upstream)))
    grad_dropped = convolve(upstream_patches, flipped(w_second), cell_shape)
    grad_second = weight_gradient(dropped_patches, upstream)
    sigma = jax.nn.sigmoid(pre_first)
    grad_pre = (grad_dropped * scaling * sigma * (1.0 + pre_first * (1.0 - sigma))).astype(
        jnp.bfloat16
    )
    grad_first = weight_gradient(cells_patches, grad_pre)
    grad_cells = upstream.astype(jnp.float32) + convolve(
        unfold(face_cells(with_later(grad_pre))), flipped(w_first), cell_shape
    )
    grad_latent = (
        grad_cells.reshape(frames_here, low_rows, 2, low_cols, 2, channels)
        .sum(axis=(2, 4))
        .astype(jnp.bfloat16)
    )
    grad_first, grad_second = lax.psum((grad_first, grad_second), ("tm", "row", "col"))
    return (mixed, grad_latent, grad_first, grad_second)


def solution(mesh):
    placed = (P("tm", "row", "col", None), P(), P(), P(), P(), P("tm", "row", "col", None), P())
    return jax.shard_map(
        local,
        mesh=mesh,
        in_specs=placed,
        out_specs=(P("tm", "row", "col", None), P("tm", "row", "col", None), P(), P()),
        check_vma=False,
    )
```

profile of v0, /device:TPU:1, one launch (start us, length us, event | category | flops | bytes accessed | tf_op | source)
XLA Modules:
  0.0 432.8 jit_solution(13995282956736010397)
XLA Ops:
  8.1 6.2 %collective-permute-start = (bf16[2,8,8,256]{3,2,1,0:T(8,128)(2,1)S(1)}, bf16[2,8,8,256]{3,2,1,0:T(8,128)(2,1)S(1)}, u32[]{:S(2)}, u32[]{:S(2)}) collective-permute-start(bf16[2,8,8,256]{3,2,1,0:T(8,128)(2,1)S(1)} %slice.498), channel_id=1, source_target_pairs={{0,32},{32,64},{64,96},{1,33},{33,65},{65,97},{2,34},{34,66},{66,9... | collective-permute-start | bytes 196616 | tf_op jit(solution)/shard_map/ppermute | solution.py:13
  22.8 3.5 collective-permute-start.1
  29.7 6.0 %copy.13 = bf16[3,3,3,256,256]{3,4,2,1,0:T(8,128)(2,1)} copy(bf16[3,3,3,256,256]{4,3,2,1,0:T(8,128)(2,1)} %param.10) | data formatting | bytes 7077888 | tf_op args[3]
  35.7 4.2 rev.6
  39.9 6.0 %copy.14 = bf16[3,3,3,256,256]{3,4,2,1,0:T(8,128)(2,1)} copy(bf16[3,3,3,256,256]{4,3,2,1,0:T(8,128)(2,1)} %param.8) | data formatting | bytes 7077888 | tf_op args[1]
  45.9 4.1 rev.7
  52.7 2.4 collective-permute-done.2
  55.9 3.1 collective-permute-start.3
  75.0 2.8 collective-permute-done.4
  102.6 6.7 %fusion.5 = (bf16[4,16,16,256]{3,2,1,0:T(8,128)(2,1)S(1)}, f32[4,16,16,256]{3,2,1,0:T(8,128)}) fusion(s32[]{:T(128)} %bitcast.8, s32[]{:T(128)} %bitcast.7, s32[16]{0:T(128)S(1)} %get-tuple-element.89, s32[16]{0:T(128)S(1)} %get-tuple-element.90, s32[4]{0:T(128)S(1)} %add_multiply_fusion, f32[256]{0:T(256)S(1)} %copy-done.14, ...), kind=kOutput, calls=%fused_computation.55 | convolution fusion | flops 3630694400 | bytes 19268760 | tf_op jit(solution)/shard_map/dot_general | solution.py:68
  113.1 3.4 collective-permute-start.11
  118.7 3.4 collective-permute-done.12
  122.3 3.1 collective-permute-start.13
  127.6 18.7 %copy.15 = bf16[6912,1024]{1,0:T(8,128)(2,1)} copy(bf16[6912,1024]{0,1:T(8,128)(2,1)} %bitcast.44) | data formatting | bytes 28311552 | tf_op jit(solution)/shard_map/dot_general | solution.py:77
  146.4 9.4 %collective-permute-start.5 = (bf16[2,16,16,256]{3,2,1,0:T(8,128)(2,1)S(1)}, bf16[2,16,16,256]{3,2,1,0:T(8,128)(2,1)S(1)}, u32[]{:S(2)}, u32[]{:S(2)}) collective-permute-start(bf16[2,16,16,256]{3,2,1,0:T(8,128)(2,1)S(1)} %slice.670), channel_id=1, source_target_pairs={{0,32},{32,64},{64,96},{1,33},{33,65},{65,97},{2,34},{34,66},{66,9... | collective-permute-start | bytes 786440 | tf_op jit(solution)/shard_map/ppermute | solution.py:13
  159.4 5.9 %copy-done.13 = bf16[4,16,16,6912]{3,2,1,0:T(8,128)(2,1)} copy-done((bf16[4,16,16,6912]{3,2,1,0:T(8,128)(2,1)}, bf16[4,16,16,6912]{3,2,1,0:T(8,128)(2,1)S(1)}, u32[]{:S(2)}) %copy-start.13) | copy-done | bytes 14155800
  165.4 12.1 %fusion.4 = bf16[4,16,16,256]{3,2,1,0:T(8,128)(2,1)S(1)} fusion(bf16[4,16,16,6912]{3,2,1,0:T(8,128)(2,1)} %copy-done.13, bf16[6912,256,1,1]{1,0,3,2:T(8,128)(2,1)S(1)} %bitcast.95, f32[4,16,16,256]{3,2,1,0:T(8,128)S(1)} %copy-done.16, s32[]{:T(128)} %bitcast.8, s32[]{:T(128)} %bitcast.7, s32[16]{0:T(128)S(1)} %get-tuple-element.89, ...), kind=kOutput, calls=%fused_computation.50 | convolution fusion | flops 3631480832 | bytes 19267736 | tf_op jit(solution)/shard_map/dot_general | solution.py:68
  179.4 3.4 collective-permute-start.6
  184.2 6.1 %fusion.66 = f32[3,3,3,256,256]{4,3,2,1,0:T(8,128)} fusion(bf16[3,3,3,256,1024]{4,3,2,1,0:T(8,128)(2,1)S(1)} %bitcast.88, bf16[1024,256,1,1,1]{1,0,4,3,2:T(8,128)(2,1)S(1)} %bitcast.84), kind=kOutput, calls=%fused_computation.273 | convolution fusion | flops 3623878656 | bytes 21757952 | tf_op jit(solution)/shard_map/dot_general | solution.py:77
  190.5 4.3 collective-permute-start.8
  196.5 3.8 collective-permute-done.9
  203.8 5.0 %copy-done = bf16[4,16,16,6912]{3,2,1,0:T(8,128)(2,1)} copy-done((bf16[4,16,16,6912]{3,2,1,0:T(8,128)(2,1)}, bf16[4,16,16,6912]{3,2,1,0:T(8,128)(2,1)S(1)}, u32[]{:S(2)}) %copy-start) | copy-done | bytes 14155800
  208.9 18.6 %copy.16 = bf16[6912,1024]{1,0:T(8,128)(2,1)} copy(bf16[6912,1024]{0,1:T(8,128)(2,1)} %bitcast.85) | data formatting | bytes 28311552 | tf_op jit(solution)/shard_map/dot_general | solution.py:77
  227.5 11.9 %fusion.67 = f32[3,3,3,256,256]{4,3,2,1,0:T(8,128)} fusion(bf16[3,3,3,256,1024]{4,3,2,1,0:T(8,128)(2,1)} %bitcast.89, bf16[1024,256,1,1,1]{1,0,4,3,2:T(8,128)(2,1)S(1)} %bitcast.96), kind=kOutput, calls=%fused_computation.274 | convolution fusion | flops 3623878656 | bytes 21757952 | tf_op jit(solution)/shard_map/dot_general | solution.py:77
  239.4 4.3 collective-permute-start.16
  245.0 10.6 %fusion.3 = bf16[4,16,16,256]{3,2,1,0:T(8,128)(2,1)} fusion(bf16[4,16,16,6912]{3,2,1,0:T(8,128)(2,1)} %copy-done, bf16[6912,256,1,1]{1,0,3,2:T(8,128)(2,1)} %bitcast.93, bf16[4,16,16,256]{3,2,1,0:T(8,128)(2,1)S(1)} %copy-done.7, f32[256]{0:T(256)S(1)} %copy-done.15), kind=kOutput, calls=%fused_computation.49 | convolution fusion | flops 3624927232 | bytes 18744320 | tf_op jit(solution)/shard_map/dot_general | solution.py:68
  255.9 2.8 collective-permute-start.18
  260.6 4.3 collective-permute-done.19
  268.5 3.8 convolution_add_fusion
  274.6 141.3 %all-reduce.3.cloned.1.call-done = (f32[3,3,3,256,256]{4,3,2,1,0:T(8,128)}, f32[3,3,3,256,256]{4,3,2,1,0:T(8,128)}) async-done(((f32[3,3,3,256,256]{4,3,2,1,0:T(8,128)}, f32[3,3,3,256,256]{4,3,2,1,0:T(8,128)}), (f32[3,3,3,256,256]{4,3,2,1,0:T(8,128)}, f32[3,3,3,256,256]{4,3,2,1,0:T(8,128)})) %all-reduce.3.cloned.1.call-update) | async-done | bytes 14155792 | tf_op jit(solution)/shard_map/psum | solution.py:140
  415.8 6.9 %copy.161 = f32[3,3,3,256,256]{4,3,2,1,0:T(8,128)} copy(f32[3,3,3,256,256]{4,3,2,1,0:T(8,128)} %get-tuple-element.93) | data formatting | bytes 14155776
  422.7 3.0 copy.162
  (253 shorter events, 86.0 us)
Async XLA Ops:
  7.2 408.7 %all-reduce.3.cloned.1.call-start = ((), (), s32[]{:S(2)}) async-start(), calls=%async_computation | async-start | bytes 28311552 | tf_op jit(solution)/shard_map/psum | solution.py:140
  8.1 12.2 %collective-permute-start = (bf16[2,8,8,256]{3,2,1,0:T(8,128)(2,1)S(1)}, bf16[2,8,8,256]{3,2,1,0:T(8,128)(2,1)S(1)}, u32[]{:S(2)}, u32[]{:S(2)}) collective-permute-start(bf16[2,8,8,256]{3,2,1,0:T(8,128)(2,1)S(1)} %slice.498), channel_id=1, source_target_pairs={{0,32},{32,64},{64,96},{1,33},{33,65},{65,97},{2,34},{34,66},{66,9... | collective-permute-start | bytes 196616 | tf_op jit(solution)/shard_map/ppermute | solution.py:13
  15.9 96.2 %collective-permute-start.10 = (bf16[2,16,16,256]{3,2,1,0:T(8,128)(2,1)}, bf16[2,16,16,256]{3,2,1,0:T(8,128)(2,1)}, u32[]{:S(2)}, u32[]{:S(2)}) collective-permute-start(bf16[2,16,16,256]{3,2,1,0:T(8,128)(2,1)} %slice.564), channel_id=1, source_target_pairs={{32,0},{64,32},{96,64},{33,1},{65,33},{97,65},{34,2},{66,34},{98,6... | collective-permute-start | bytes 786440 | tf_op jit(solution)/shard_map/ppermute | solution.py:13
  22.8 28.5 %collective-permute-start.1 = (bf16[6,1,16,256]{3,2,1,0:T(8,128)(2,1)S(1)}, bf16[6,1,16,256]{3,2,1,0:T(8,128)(2,1)S(1)}, u32[]{:S(2)}, u32[]{:S(2)}) collective-permute-start(bf16[6,1,16,256]{3,2,1,0:T(8,128)(2,1)S(1)} %get-tuple-element.78), channel_id=1, source_target_pairs={{0,4},{4,8},{8,12},{12,16},{16,20},{20,24},{24,28},{1,5},{5,9},{9,... | collective-permute-start | bytes 147464 | tf_op jit(solution)/shard_map/ppermute | solution.py:24
  50.0 5.0 %collective-permute-start.2 = (bf16[6,1,16,256]{3,2,1,0:T(8,128)(2,1)S(1)}, bf16[6,1,16,256]{3,2,1,0:T(8,128)(2,1)S(1)}, u32[]{:S(2)}, u32[]{:S(2)}) collective-permute-start(bf16[6,1,16,256]{3,2,1,0:T(8,128)(2,1)S(1)} %get-tuple-element.77), channel_id=1, source_target_pairs={{4,0},{8,4},{12,8},{16,12},{20,16},{24,20},{28,24},{5,1},{9,5},{13... | collective-permute-start | bytes 147464 | tf_op jit(solution)/shard_map/ppermute | solution.py:26
  55.9 17.9 %collective-permute-start.3 = (bf16[6,18,1,256]{3,2,1,0:T(2,128)(2,1)}, bf16[6,18,1,256]{3,2,1,0:T(2,128)(2,1)S(1)}, u32[]{:S(2)}, u32[]{:S(2)}) collective-permute-start(bf16[6,18,1,256]{3,2,1,0:T(2,128)(2,1)} %get-tuple-element.55), channel_id=1, source_target_pairs={{0,1},{1,2},{2,3},{4,5},{5,6},{6,7},{8,9},{9,10},{10,11},{12,13},{... | collective-permute-start | bytes 165896 | tf_op jit(solution)/shard_map/ppermute | solution.py:24
  72.1 9.3 %copy-start.11 = (bf16[4,16,16,256]{3,2,1,0:T(8,128)(2,1)S(1)}, bf16[4,16,16,256]{3,2,1,0:T(8,128)(2,1)}, u32[]{:S(2)}) copy-start(bf16[4,16,16,256]{3,2,1,0:T(8,128)(2,1)} %concatenate.237) | copy-start | bytes 1572868
  72.1 5.8 %collective-permute-start.4 = (bf16[6,18,1,256]{3,2,1,0:T(2,128)(2,1)}, bf16[6,18,1,256]{3,2,1,0:T(2,128)(2,1)S(1)}, u32[]{:S(2)}, u32[]{:S(2)}) collective-permute-start(bf16[6,18,1,256]{3,2,1,0:T(2,128)(2,1)} %get-tuple-element.54), channel_id=1, source_target_pairs={{1,0},{2,1},{3,2},{5,4},{6,5},{7,6},{9,8},{10,9},{11,10},{13,12},{... | collective-permute-start | bytes 165896 | tf_op jit(solution)/shard_map/ppermute | solution.py:26
  82.0 12.3 %copy-start.9 = (bf16[1024,256]{1,0:T(8,128)(2,1)S(1)}, bf16[1024,256]{1,0:T(8,128)(2,1)}, u32[]{:S(2)}) copy-start(bf16[1024,256]{1,0:T(8,128)(2,1)} %concatenate.273) | copy-start | bytes 1572868
  83.2 19.4 %copy-start.2 = (bf16[3,3,3,256,256]{4,3,2,1,0:T(8,128)(2,1)S(1)}, bf16[3,3,3,256,256]{4,3,2,1,0:T(8,128)(2,1)}, u32[]{:S(2)}) copy-start(bf16[3,3,3,256,256]{4,3,2,1,0:T(8,128)(2,1)} %param.8) | copy-start | bytes 10616836
  83.2 19.4 %copy-start.14 = (f32[256]{0:T(256)S(1)}, f32[256]{0:T(256)}, u32[]{:S(2)}) copy-start(f32[256]{0:T(256)} %param.9) | copy-start | bytes 3076
  113.1 5.6 %collective-permute-start.11 = (bf16[6,1,16,256]{3,2,1,0:T(8,128)(2,1)S(1)}, bf16[6,1,16,256]{3,2,1,0:T(8,128)(2,1)S(1)}, u32[]{:S(2)}, u32[]{:S(2)}) collective-permute-start(bf16[6,1,16,256]{3,2,1,0:T(8,128)(2,1)S(1)} %get-tuple-element.68), channel_id=1, source_target_pairs={{0,4},{4,8},{8,12},{12,16},{16,20},{20,24},{24,28},{1,5},{5,9},{9,... | collective-permute-start | bytes 147464 | tf_op jit(solution)/shard_map/ppermute | solution.py:24
  116.5 5.7 %collective-permute-start.12 = (bf16[6,1,16,256]{3,2,1,0:T(8,128)(2,1)S(1)}, bf16[6,1,16,256]{3,2,1,0:T(8,128)(2,1)S(1)}, u32[]{:S(2)}, u32[]{:S(2)}) collective-permute-start(bf16[6,1,16,256]{3,2,1,0:T(8,128)(2,1)S(1)} %get-tuple-element.69), channel_id=1, source_target_pairs={{4,0},{8,4},{12,8},{16,12},{20,16},{24,20},{28,24},{5,1},{9,5},{13... | collective-permute-start | bytes 147464 | tf_op jit(solution)/shard_map/ppermute | solution.py:26
  122.3 33.5 %collective-permute-start.13 = (bf16[6,18,1,256]{3,2,1,0:T(2,128)(2,1)S(1)}, bf16[6,18,1,256]{3,2,1,0:T(2,128)(2,1)S(1)}, u32[]{:S(2)}, u32[]{:S(2)}) collective-permute-start(bf16[6,18,1,256]{3,2,1,0:T(2,128)(2,1)S(1)} %get-tuple-element.49), channel_id=1, source_target_pairs={{0,1},{1,2},{2,3},{4,5},{5,6},{6,7},{8,9},{9,10},{10,11},{12,13},{... | collective-permute-start | bytes 165896 | tf_op jit(solution)/shard_map/ppermute | solution.py:24
  125.4 30.4 %collective-permute-start.14 = (bf16[6,18,1,256]{3,2,1,0:T(2,128)(2,1)S(1)}, bf16[6,18,1,256]{3,2,1,0:T(2,128)(2,1)S(1)}, u32[]{:S(2)}, u32[]{:S(2)}) collective-permute-start(bf16[6,18,1,256]{3,2,1,0:T(2,128)(2,1)S(1)} %get-tuple-element.48), channel_id=1, source_target_pairs={{1,0},{2,1},{3,2},{5,4},{6,5},{7,6},{9,8},{10,9},{11,10},{13,12},{... | collective-permute-start | bytes 165896 | tf_op jit(solution)/shard_map/ppermute | solution.py:26
  127.6 29.4 %copy-start.5 = (bf16[4,16,16,256]{3,2,1,0:T(8,128)(2,1)S(1)}, bf16[4,16,16,256]{3,2,1,0:T(8,128)(2,1)}, u32[]{:S(2)}) copy-start(bf16[4,16,16,256]{3,2,1,0:T(8,128)(2,1)} %param.12) | copy-start | bytes 1572868
  146.4 33.1 %collective-permute-start.5 = (bf16[2,16,16,256]{3,2,1,0:T(8,128)(2,1)S(1)}, bf16[2,16,16,256]{3,2,1,0:T(8,128)(2,1)S(1)}, u32[]{:S(2)}, u32[]{:S(2)}) collective-permute-start(bf16[2,16,16,256]{3,2,1,0:T(8,128)(2,1)S(1)} %slice.670), channel_id=1, source_target_pairs={{0,32},{32,64},{64,96},{1,33},{33,65},{65,97},{2,34},{34,66},{66,9... | collective-permute-start | bytes 786440 | tf_op jit(solution)/shard_map/ppermute | solution.py:13
  159.2 24.9 %slice-start = ((s8[14155776]{0:T(1024)(128)(4,1)}), s8[4194304]{0:T(1024)(128)(4,1)S(1)}, s32[]{:S(2)}) async-start(s8[14155776]{0:T(1024)(128)(4,1)} %bitcast.86), calls=%async_computation.1 | async-start | bytes 8388608
  165.4 18.8 %slice-start.1 = ((s8[14155776]{0:T(1024)(128)(4,1)}), s8[4194304]{0:T(1024)(128)(4,1)S(1)}, s32[]{:S(2)}) async-start(s8[14155776]{0:T(1024)(128)(4,1)} %bitcast.86), calls=%async_computation.2 | async-start | bytes 8388608
  165.4 18.8 %slice-start.2 = ((s8[14155776]{0:T(1024)(128)(4,1)}), s8[4194304]{0:T(1024)(128)(4,1)S(1)}, s32[]{:S(2)}) async-start(s8[14155776]{0:T(1024)(128)(4,1)} %bitcast.86), calls=%async_computation.3 | async-start | bytes 8388608
  165.4 18.8 %slice-start.3 = ((s8[14155776]{0:T(1024)(128)(4,1)}), s8[1572864]{0:T(1024)(128)(4,1)S(1)}, s32[]{:S(2)}) async-start(s8[14155776]{0:T(1024)(128)(4,1)} %bitcast.86), calls=%async_computation.4 | async-start | bytes 3145728
  177.5 61.9 %collective-permute-start.15 = (bf16[2,16,16,256]{3,2,1,0:T(8,128)(2,1)S(1)}, bf16[2,16,16,256]{3,2,1,0:T(8,128)(2,1)S(1)}, u32[]{:S(2)}, u32[]{:S(2)}) collective-permute-start(bf16[2,16,16,256]{3,2,1,0:T(8,128)(2,1)S(1)} %slice.727), channel_id=1, source_target_pairs={{32,0},{64,32},{96,64},{33,1},{65,33},{97,65},{34,2},{66,34},{98,6... | collective-permute-start | bytes 786440 | tf_op jit(solution)/shard_map/ppermute | solution.py:13
  179.4 10.8 %collective-permute-start.6 = (bf16[6,1,16,256]{3,2,1,0:T(8,128)(2,1)S(1)}, bf16[6,1,16,256]{3,2,1,0:T(8,128)(2,1)S(1)}, u32[]{:S(2)}, u32[]{:S(2)}) collective-permute-start(bf16[6,1,16,256]{3,2,1,0:T(8,128)(2,1)S(1)} %get-tuple-element.72), channel_id=1, source_target_pairs={{0,4},{4,8},{8,12},{12,16},{16,20},{20,24},{24,28},{1,5},{5,9},{9,... | collective-permute-start | bytes 147464 | tf_op jit(solution)/shard_map/ppermute | solution.py:24
  182.8 7.5 %collective-permute-start.7 = (bf16[6,1,16,256]{3,2,1,0:T(8,128)(2,1)S(1)}, bf16[6,1,16,256]{3,2,1,0:T(8,128)(2,1)S(1)}, u32[]{:S(2)}, u32[]{:S(2)}) collective-permute-start(bf16[6,1,16,256]{3,2,1,0:T(8,128)(2,1)S(1)} %get-tuple-element.73), channel_id=1, source_target_pairs={{4,0},{8,4},{12,8},{16,12},{20,16},{24,20},{28,24},{5,1},{9,5},{13... | collective-permute-start | bytes 147464 | tf_op jit(solution)/shard_map/ppermute | solution.py:26
  190.5 6.0 %collective-permute-start.8 = (bf16[6,18,1,256]{3,2,1,0:T(2,128)(2,1)S(1)}, bf16[6,18,1,256]{3,2,1,0:T(2,128)(2,1)S(1)}, u32[]{:S(2)}, u32[]{:S(2)}) collective-permute-start(bf16[6,18,1,256]{3,2,1,0:T(2,128)(2,1)S(1)} %get-tuple-element.53), channel_id=1, source_target_pairs={{0,1},{1,2},{2,3},{4,5},{5,6},{6,7},{8,9},{9,10},{10,11},{12,13},{... | collective-permute-start | bytes 165896 | tf_op jit(solution)/shard_map/ppermute | solution.py:24
  194.7 5.5 %collective-permute-start.9 = (bf16[6,18,1,256]{3,2,1,0:T(2,128)(2,1)S(1)}, bf16[6,18,1,256]{3,2,1,0:T(2,128)(2,1)S(1)}, u32[]{:S(2)}, u32[]{:S(2)}) collective-permute-start(bf16[6,18,1,256]{3,2,1,0:T(2,128)(2,1)S(1)} %get-tuple-element.52), channel_id=1, source_target_pairs={{1,0},{2,1},{3,2},{5,4},{6,5},{7,6},{9,8},{10,9},{11,10},{13,12},{... | collective-permute-start | bytes 165896 | tf_op jit(solution)/shard_map/ppermute | solution.py:26
  227.5 17.5 %copy-start.7 = (bf16[4,16,16,256]{3,2,1,0:T(8,128)(2,1)S(1)}, bf16[4,16,16,256]{3,2,1,0:T(8,128)(2,1)}, u32[]{:S(2)}) copy-start(bf16[4,16,16,256]{3,2,1,0:T(8,128)(2,1)} %slice.497) | copy-start | bytes 1572868
  227.5 17.5 %copy-start.15 = (f32[256]{0:T(256)S(1)}, f32[256]{0:T(256)}, u32[]{:S(2)}) copy-start(f32[256]{0:T(256)} %param.11) | copy-start | bytes 3076
  239.4 16.2 %collective-permute-start.16 = (bf16[6,1,16,256]{3,2,1,0:T(8,128)(2,1)S(1)}, bf16[6,1,16,256]{3,2,1,0:T(8,128)(2,1)S(1)}, u32[]{:S(2)}, u32[]{:S(2)}) collective-permute-start(bf16[6,1,16,256]{3,2,1,0:T(8,128)(2,1)S(1)} %get-tuple-element.66), channel_id=1, source_target_pairs={{0,4},{4,8},{8,12},{12,16},{16,20},{20,24},{24,28},{1,5},{5,9},{9,... | collective-permute-start | bytes 147464 | tf_op jit(solution)/shard_map/ppermute | solution.py:24
  243.7 12.0 %collective-permute-start.17 = (bf16[6,1,16,256]{3,2,1,0:T(8,128)(2,1)S(1)}, bf16[6,1,16,256]{3,2,1,0:T(8,128)(2,1)S(1)}, u32[]{:S(2)}, u32[]{:S(2)}) collective-permute-start(bf16[6,1,16,256]{3,2,1,0:T(8,128)(2,1)S(1)} %get-tuple-element.67), channel_id=1, source_target_pairs={{4,0},{8,4},{12,8},{16,12},{20,16},{24,20},{28,24},{5,1},{9,5},{13... | collective-permute-start | bytes 147464 | tf_op jit(solution)/shard_map/ppermute | solution.py:26
  255.9 4.7 %collective-permute-start.18 = (bf16[6,18,1,256]{3,2,1,0:T(2,128)(2,1)S(1)}, bf16[6,18,1,256]{3,2,1,0:T(2,128)(2,1)S(1)}, u32[]{:S(2)}, u32[]{:S(2)}) collective-permute-start(bf16[6,18,1,256]{3,2,1,0:T(2,128)(2,1)S(1)} %get-tuple-element.45), channel_id=1, source_target_pairs={{0,1},{1,2},{2,3},{4,5},{5,6},{6,7},{8,9},{9,10},{10,11},{12,13},{... | collective-permute-start | bytes 165896 | tf_op jit(solution)/shard_map/ppermute | solution.py:24
  258.7 6.2 %collective-permute-start.19 = (bf16[6,18,1,256]{3,2,1,0:T(2,128)(2,1)S(1)}, bf16[6,18,1,256]{3,2,1,0:T(2,128)(2,1)S(1)}, u32[]{:S(2)}, u32[]{:S(2)}) collective-permute-start(bf16[6,18,1,256]{3,2,1,0:T(2,128)(2,1)S(1)} %get-tuple-element.44), channel_id=1, source_target_pairs={{1,0},{2,1},{3,2},{5,4},{6,5},{7,6},{9,8},{10,9},{11,10},{13,12},{... | collective-permute-start | bytes 165896 | tf_op jit(solution)/shard_map/ppermute | solution.py:26
  (12 other events, 65.0 us)
Sparse Core Ops, SparseCore 0:
  239.5 176.2 all-reduce.2
where the time goes:
time: 439 us; the launch traced here: 433 us
  waiting for transfers between devices  158 us (36%)
  local copies, waits for them, and re-layouts  139 us (32%)
  starting transfers between devices  58.5 us (13%)
  matrix products  51.2 us (12%)
  between operations  15.7 us (4%)
  other arithmetic  10.3 us (2%)
    psum x1, waiting for transfers between devices, local(): lax.psum((grad_first, grad_second), ('tm', 'row', 'col'))  141 us
    unnamed x155, local copies, waits for them, and re-layouts  66.7 us
    dot_general x2, local copies, waits for them, and re-layouts, weight_gradient(): lax.dot_general(patches, grad.reshape(-1, channels), (((0,), (0,)), ((),...  37.3 us
    dot_general x4, matrix products, convolve(): jnp.dot(patches, matrix, preferred_element_type=jnp.float32).reshape(shape)  33.2 us
    ppermute x8, starting transfers between devices, extended_2(): lax.ppermute(tail, axis, [(i, (i + 1) % count) for i in range(ends)])  27.9 us
    ppermute x4, starting transfers between devices, shifted(): return lax.ppermute(block, axis, route)  19.4 us
    dot_general x2, matrix products, weight_gradient(): lax.dot_general(patches, grad.reshape(-1, channels), (((0,), (0,)), ((),...  18 us
    ppermute x8, waiting for transfers between devices, extended_2(): lax.ppermute(head, axis, [((i + 1) % count, i) for i in range(ends)])  16.8 us
  transfers between devices with their start and end apart: 21, of which 8 were waited for; matrix products, arithmetic and copies ran while one was open for 41% of the time, Pallas kernels for 0%

commit v1 on v0

--- a/solution.py
+++ b/solution.py
@@ -5,6 +5,7 @@
 
 KEEP_LEVEL = 6554
 KEEP_SCALE = 65536.0 / 58982.0
+ALL = ("tm", "row", "col")
 
 
 def shifted(block, axis, distance):
@@ -50,37 +51,47 @@
     return jnp.repeat(jnp.repeat(field, 2, axis=1), 2, axis=2)
 
 
-def unfold(extended):
-    frames_out = extended.shape[0] - 2
-    height = extended.shape[1] - 2
-    width = extended.shape[2] - 2
-    pieces = [
-        extended[a : a + frames_out, b : b + height, c : c + width]
-        for a in range(3)
-        for b in range(3)
-        for c in range(3)
-    ]
-    return jnp.concatenate(pieces, axis=-1).reshape(frames_out * height * width, -1)
-
-
-def convolve(patches, weight, shape):
-    matrix = weight.reshape(-1, weight.shape[-1])
-    return jnp.dot(patches, matrix, preferred_element_type=jnp.float32).reshape(shape)
+def convolve(extended, weight):
+    return lax.conv_general_dilated(
+        extended[None],
+        weight,
+        (1, 1, 1),
+        "VALID",
+        dimension_numbers=("NDHWC", "DHWIO", "NDHWC"),
+        preferred_element_type=jnp.float32,
+    )[0]
 
 
 def flipped(weight):
     return jnp.swapaxes(weight[::-1, ::-1, ::-1], 3, 4)
 
 
-def weight_gradient(patches, grad):
-    channels = grad.shape[-1]
-    summed = lax.dot_general(
-        patches,
-        grad.reshape(-1, channels),
-        (((0,), (0,)), ((), ())),
+def weight_gradient(extended, grad):
+    summed = lax.conv_general_dilated(
+        extended[None],
+        grad[None],
+        (1, 1, 1),
+        "VALID",
+        dimension_numbers=("CDHWN", "IDHWO", "NDHWC"),
         preferred_element_type=jnp.float32,
     )
-    return summed.reshape(3, 3, 3, channels, channels)
+    return jnp.transpose(summed, (1, 2, 3, 0, 4))
+
+
+def reduced(grad):
+    count = 8
+    for axis in ALL:
+        count *= lax.axis_size(axis)
+    flat = grad.reshape(-1, grad.shape[-1])
+    rows = flat.shape[0]
+    padded = -(-rows // count) * count
+    flat = jnp.pad(flat, ((0, padded - rows), (0, 0)))
+    for axis in ALL:
+        flat = lax.psum_scatter(flat, axis, scatter_dimension=0, tiled=True)
+    flat = flat.astype(jnp.bfloat16)
+    for axis in ALL[::-1]:
+        flat = lax.all_gather(flat, axis, axis=0, tiled=True)
+    return flat[:rows].astype(jnp.float32).reshape(grad.shape)
 
 
 def with_earlier(field):
@@ -111,33 +122,30 @@
     latent_ext = with_earlier(latent)
     cells_ext = face_cells(upsample(latent_ext))
     cells_here = cells_ext[2:, 1:-1, 1:-1]
-    cells_patches = unfold(cells_ext)
-    pre_first = convolve(cells_patches, w_first, cell_shape) + b_first
+    pre_first = convolve(cells_ext, w_first) + b_first
     scaling = keep_mask(
         dropout_key, frame_start, row_start, col_start, cell_shape, height_all, width_all
     )
     dropped = (jax.nn.silu(pre_first) * scaling).astype(jnp.bfloat16)
-    dropped_patches = unfold(face_cells(with_earlier(dropped)))
-    mixed = (
-        cells_here.astype(jnp.float32) + convolve(dropped_patches, w_second, cell_shape) + b_second
-    ).astype(jnp.bfloat16)
-    upstream_patches = unfold(face_cells(with_later(upstream)))
-    grad_dropped = convolve(upstream_patches, flipped(w_second), cell_shape)
-    grad_second = weight_gradient(dropped_patches, upstream)
+    dropped_ext = face_cells(with_earlier(dropped))
+    grad_second = reduced(weight_gradient(dropped_ext, upstream))
+    mixed = (cells_here.astype(jnp.float32) + convolve(dropped_ext, w_second) + b_second).astype(
+        jnp.bfloat16
+    )
+    grad_dropped = convolve(face_cells(with_later(upstream)), flipped(w_second))
     sigma = jax.nn.sigmoid(pre_first)
     grad_pre = (grad_dropped * scaling * sigma * (1.0 + pre_first * (1.0 - sigma))).astype(
         jnp.bfloat16
     )
-    grad_first = weight_gradient(cells_patches, grad_pre)
+    grad_first = reduced(weight_gradient(cells_ext, grad_pre))
     grad_cells = upstream.astype(jnp.float32) + convolve(
-        unfold(face_cells(with_later(grad_pre))), flipped(w_first), cell_shape
+        face_cells(with_later(grad_pre)), flipped(w_first)
     )
     grad_latent = (
         grad_cells.reshape(frames_here, low_rows, 2, low_cols, 2, channels)
         .sum(axis=(2, 4))
         .astype(jnp.bfloat16)
     )
-    grad_first, grad_second = lax.psum((grad_first, grad_second), ("tm", "row", "col"))
     return (mixed, grad_latent, grad_first, grad_second)
 
 

time: 439 us -> 589 us (1.34)
  waiting for transfers between devices: 158 us -> 256 us
  blocking collectives: 0 us -> 75 us
  local copies, waits for them, and re-layouts: 139 us -> 64.4 us
  other arithmetic: 10.3 us -> 33.3 us
  starting transfers between devices: 58.5 us -> 76.9 us
  matrix products: 51.2 us -> 60.9 us
    reduce_scatter x0 -> x6, waiting for transfers between devices: none -> 237 us  [reduced(): flat = lax.psum_scatter(flat, axis, scatter_dimension=0, tiled=True)]
    psum x1 -> x0, waiting for transfers between devices: 141 us -> none  [local(): lax.psum((grad_first, grad_second), ('tm', 'row', 'col'))]
    all_gather x0 -> x4, blocking collectives: none -> 75 us  [reduced(): flat = lax.all_gather(flat, axis, axis=0, tiled=True)]
    unnamed x155 -> x53, local copies, waits for them, and re-layouts: 66.7 us -> 9.71 us
    dot_general x6 -> x0, matrix products: 51.2 us -> none  [the longest x4 33.2 us: convolve(): jnp.dot(patches, matrix, preferred_element_type=jnp.float32).reshape(shape)]
    dot_general x2 -> x0, local copies, waits for them, and re-layouts: 37.3 us -> none  [weight_gradient(): lax.dot_general(patches, grad.reshape(-1, channels), (((0,), (0,)), ((),...]
    transpose x0 -> x2, matrix products: none -> 34.7 us  [weight_gradient(): return jnp.transpose(summed, (1, 2, 3, 0, 4))]
    conv_general_dilated x0 -> x4, matrix products: none -> 26.1 us  [convolve(): lax.conv_general_dilated(extended[None], weight, (1, 1, 1), 'VALID', dime...]
  transfers between devices with their start and end apart: 21 -> 28, of which waited for: 8 -> 12; matrix products, arithmetic and copies ran while one was open for 41% -> 21% of each run, Pallas kernels for 0% -> 0%
where the time goes in v1:
time: 589 us; the launch traced here: 582 us
  waiting for transfers between devices  256 us (43%)
  starting transfers between devices  76.9 us (13%)
  blocking collectives  75 us (13%)
  local copies, waits for them, and re-layouts  64.4 us (11%)
  matrix products  60.9 us (10%)
  other arithmetic  33.3 us (6%)
  between operations  15 us (3%)
    reduce_scatter x6, waiting for transfers between devices, reduced(): flat = lax.psum_scatter(flat, axis, scatter_dimension=0, tiled=True)  237 us
    all_gather x4, blocking collectives, reduced(): flat = lax.all_gather(flat, axis, axis=0, tiled=True)  75 us
    ppermute x4, starting transfers between devices, shifted(): return lax.ppermute(block, axis, route)  36.8 us
    transpose x2, matrix products, weight_gradient(): return jnp.transpose(summed, (1, 2, 3, 0, 4))  34.7 us
    ppermute x8, starting transfers between devices, extended_2(): lax.ppermute(tail, axis, [(i, (i + 1) % count) for i in range(ends)])  29.1 us
    conv_general_dilated x4, matrix products, convolve(): lax.conv_general_dilated(extended[None], weight, (1, 1, 1), 'VALID', dime...  26.1 us
    conv_general_dilated x14, local copies, waits for them, and re-layouts, convolve(): lax.conv_general_dilated(extended[None], weight, (1, 1, 1), 'VALID', dime...  18.1 us
  transfers between devices with their start and end apart: 28, of which 12 were waited for; matrix products, arithmetic and copies ran while one was open for 21% of the time, Pallas kernels for 0%

profile of v1, /device:TPU:1, one launch (start us, length us, event | category | flops | bytes accessed | tf_op | source)
XLA Modules:
  0.0 581.6 jit_solution(13027827747310807492)
XLA Ops:
  8.9 6.2 %collective-permute-start = (bf16[2,8,8,256]{3,2,1,0:T(8,128)(2,1)}, bf16[2,8,8,256]{3,2,1,0:T(8,128)(2,1)}, u32[]{:S(2)}, u32[]{:S(2)}) collective-permute-start(bf16[2,8,8,256]{3,2,1,0:T(8,128)(2,1)} %slice.77), channel_id=1, source_target_pairs={{0,32},{32,64},{64,96},{1,33},{33,65},{65,97},{2,34},{34,66},{66,9... | collective-permute-start | bytes 196616 | tf_op jit(solution)/shard_map/ppermute | solution.py:14
  28.1 3.5 collective-permute-start.1
  44.4 4.0 collective-permute-start.11
  52.9 4.6 reshape.113
  60.6 4.0 collective-permute-start.13
  66.3 7.8 %add_divide_fusion = (f32[4,16,8,3,256]{4,2,3,1,0:T(8,128)}, f32[4,16,8,3,256]{4,2,3,1,0:T(8,128)}, f32[4,16,8,3,256]{4,2,3,1,0:T(8,128)S(1)}) fusion(f32[256]{0:T(256)S(1)} %copy-done.17, bf16[3,3,3,256,256]{4,3,2,1,0:T(8,128)(2,1)S(1)} %copy-done, bf16[6,18,1,7,2,256]{5,3,4,1,0,2:T(8,128)(2,1)S(1)} %slice.115, ...), kind=kOutput, calls=%fused_computation.34 | convolution fusion | flops 5445599232 | bytes 10359832 | tf_op jit(solution)/shard_map/conv_general_dilated | solution.py:55
  78.7 5.1 reshape.127
  86.4 5.9 %fusion.42 = f32[4,16,8,3,256]{4,2,3,1,0:T(8,128)S(1)} fusion(bf16[3,3,3,256,256]{4,3,2,1,0:T(8,128)(2,1)S(1)} %copy-done.19, bf16[6,18,1,7,2,256]{5,3,4,1,0,2:T(8,128)(2,1)S(1)} %slice.122, bf16[6,18,1,8,3,256]{5,3,4,1,0,2:T(8,128)(2,1)S(1)} %copy.47, pred[8,3]{0,1:T(4,128)(4,1)S(1)} %copy-done.22), kind=kOutput, calls=%fused_computation.43 | convolution fusion | flops 5442846720 | bytes 7213080 | tf_op jit(solution)/shard_map/conv_general_dilated | solution.py:55
  96.8 7.8 %collective-permute-start.5 = (bf16[2,16,16,256]{3,1,2,0:T(8,128)(2,1)S(1)}, bf16[2,16,16,256]{3,1,2,0:T(8,128)(2,1)S(1)}, u32[]{:S(2)}, u32[]{:S(2)}) collective-permute-start(bf16[2,16,16,256]{3,1,2,0:T(8,128)(2,1)S(1)} %slice.117), channel_id=1, source_target_pairs={{0,32},{32,64},{64,96},{1,33},{33,65},{65,97},{2,34},{34,66},{66,9... | collective-permute-start | bytes 786440 | tf_op jit(solution)/shard_map/ppermute | solution.py:14
  108.1 4.3 collective-permute-start.6
  118.5 5.2 collective-permute-start.8
  125.2 17.6 %fusion.34 = f32[3,3,3,256,256]{4,3,2,1,0:T(8,128)S(1)} fusion(bf16[1,6,18,18,256]{4,3,2,1,0:T(8,128)(2,1)S(1)} %copy-done.11, bf16[1,4,16,16,256]{4,2,3,1,0:T(8,128)(2,1)S(1)} %fusion.67), kind=kOutput, calls=%fused_computation.31 | convolution fusion | flops 3623878656 | bytes 8597504 | tf_op jit(solution)/shard_map/transpose | solution.py:78
  142.8 3.4 pad.7
  146.3 3.2 fusion.91
  149.4 17.1 %fusion.32 = f32[3,3,3,256,256]{4,3,2,1,0:T(8,128)S(1)} fusion(bf16[1,6,18,18,256]{4,2,3,1,0:T(8,128)(2,1)S(1)} %get-tuple-element.16, bf16[1,4,16,16,256]{4,3,2,1,0:T(8,128)(2,1)S(1)} %bitcast.123), kind=kOutput, calls=%fused_computation.29 | convolution fusion | flops 3623878656 | bytes 8597504 | tf_op jit(solution)/shard_map/transpose | solution.py:78
  166.6 3.6 pad.8
  170.3 55.9 %reduce-scatter.7.cloned.1.call-done = f32[1792,256]{1,0:T(8,128)} async-done(((f32[7168,256]{1,0:T(8,128)}), f32[1792,256]{1,0:T(8,128)}) %reduce-scatter.7.cloned.1.call-update) | async-done | bytes 1835024 | tf_op jit(solution)/shard_map/reduce_scatter | solution.py:90
  226.2 74.9 %reduce-scatter.13.cloned.1.call-done = f32[1792,256]{1,0:T(8,128)} async-done(((f32[7168,256]{1,0:T(8,128)}), f32[1792,256]{1,0:T(8,128)}) %reduce-scatter.13.cloned.1.call-update) | async-done | bytes 1835024 | tf_op jit(solution)/shard_map/reduce_scatter | solution.py:90
  301.1 38.9 %reduce-scatter.9.cloned.1.call-done = f32[224,256]{1,0:T(8,128)} async-done(((f32[1792,256]{1,0:T(8,128)}), f32[224,256]{1,0:T(8,128)}) %reduce-scatter.9.cloned.1.call-update) | async-done | bytes 229392 | tf_op jit(solution)/shard_map/reduce_scatter | solution.py:90
  340.1 43.2 %reduce-scatter.15.cloned.1.call-done = f32[224,256]{1,0:T(8,128)} async-done(((f32[1792,256]{1,0:T(8,128)}), f32[224,256]{1,0:T(8,128)}) %reduce-scatter.15.cloned.1.call-update) | async-done | bytes 229392 | tf_op jit(solution)/shard_map/reduce_scatter | solution.py:90
  383.3 24.6 %reduce-scatter.11.cloned.1.call-done = f32[56,256]{1,0:T(8,128)} async-done(((f32[224,256]{1,0:T(8,128)}), f32[56,256]{1,0:T(8,128)}) %reduce-scatter.11.cloned.1.call-update) | async-done | bytes 57360 | tf_op jit(solution)/shard_map/reduce_scatter | solution.py:90
  408.8 9.1 %all_gather.18 = bf16[224,256]{1,0:T(8,128)(2,1)S(1)} all-gather(bf16[56,256]{1,0:T(8,128)(2,1)S(1)} %convert_element_type.49), channel_id=1, replica_groups=mesh['tm'=4,'row'=8,'col'=4] {'col'}, dimensions={0}, use_global_device_ids=true | all-gather | bytes 143360 | tf_op jit(solution)/shard_map/all_gather | solution.py:93
  417.8 27.3 %all_gather.19 = bf16[1792,256]{1,0:T(8,128)(2,1)} all-gather(bf16[224,256]{1,0:T(8,128)(2,1)S(1)} %all_gather.18), channel_id=1, replica_groups=mesh['tm'=4,'row'=8,'col'=4] {'row'}, dimensions={0}, use_global_device_ids=true | all-gather | bytes 1032192 | tf_op jit(solution)/shard_map/all_gather | solution.py:93
  446.0 9.5 %all_gather.21 = bf16[224,256]{1,0:T(8,128)(2,1)S(1)} all-gather(bf16[56,256]{1,0:T(8,128)(2,1)S(1)} %convert_element_type.50), channel_id=1, replica_groups=mesh['tm'=4,'row'=8,'col'=4] {'col'}, dimensions={0}, use_global_device_ids=true | all-gather | bytes 143360 | tf_op jit(solution)/shard_map/all_gather | solution.py:93
  455.5 29.2 %all_gather.22 = bf16[1792,256]{1,0:T(8,128)(2,1)} all-gather(bf16[224,256]{1,0:T(8,128)(2,1)S(1)} %all_gather.21), channel_id=1, replica_groups=mesh['tm'=4,'row'=8,'col'=4] {'row'}, dimensions={0}, use_global_device_ids=true | all-gather | bytes 1032192 | tf_op jit(solution)/shard_map/all_gather | solution.py:93
  485.8 20.8 %collective-permute-start.15 = (bf16[2,16,16,256]{3,1,2,0:T(8,128)(2,1)S(1)}, bf16[2,16,16,256]{3,1,2,0:T(8,128)(2,1)S(1)}, u32[]{:S(2)}, u32[]{:S(2)}) collective-permute-start(bf16[2,16,16,256]{3,1,2,0:T(8,128)(2,1)S(1)} %slice.124), channel_id=1, source_target_pairs={{32,0},{64,32},{96,64},{33,1},{65,33},{97,65},{34,2},{66,34},{98,6... | collective-permute-start | bytes 786440 | tf_op jit(solution)/shard_map/ppermute | solution.py:14
  506.6 6.3 %collective-permute-done.15 = bf16[2,16,16,256]{3,1,2,0:T(8,128)(2,1)S(1)} collective-permute-done((bf16[2,16,16,256]{3,1,2,0:T(8,128)(2,1)S(1)}, bf16[2,16,16,256]{3,1,2,0:T(8,128)(2,1)S(1)}, u32[]{:S(2)}, u32[]{:S(2)}) %collective-permute-start.15) | collective-permute-done | bytes 262176 | tf_op jit(solution)/shard_map/ppermute | solution.py:14
  518.7 4.1 collective-permute-done.17
  535.1 5.9 %fusion.36 = f32[4,16,8,3,256]{4,2,3,1,0:T(8,128)S(1)} fusion(bf16[3,3,3,256,256]{4,3,2,1,0:T(8,128)(2,1)S(1)} %copy-done, bf16[6,18,1,7,2,256]{5,3,4,1,0,2:T(8,128)(2,1)S(1)} %slice.125, bf16[6,18,1,8,3,256]{5,3,4,1,0,2:T(8,128)(2,1)S(1)} %copy.51, pred[8,3]{0,1:T(4,128)(4,1)S(1)} %copy-done.23), kind=kOutput, calls=%fused_computation.41 | convolution fusion | flops 5442846720 | bytes 7213080 | tf_op jit(solution)/shard_map/conv_general_dilated | solution.py:55
  553.9 6.5 %fusion.39 = f32[4,16,8,3,256]{4,2,3,1,0:T(8,128)S(1)} fusion(bf16[3,3,3,256,256]{4,3,2,1,0:T(8,128)(2,1)S(1)} %copy-done.20, bf16[6,18,1,7,2,256]{5,3,4,1,0,2:T(8,128)(2,1)S(1)} %slice.118, bf16[6,18,1,8,3,256]{5,3,4,1,0,2:T(8,128)(2,1)S(1)} %copy.43, pred[8,3]{0,1:T(4,128)(4,1)S(1)} %copy-done.23), kind=kOutput, calls=%fused_computation.42 | convolution fusion | flops 5442846720 | bytes 7213080 | tf_op jit(solution)/shard_map/conv_general_dilated | solution.py:55
  564.9 3.8 convert.2
  570.7 3.8 convert.3
  (160 shorter events, 99.4 us)
Async XLA Ops:
  7.2 59.1 %copy-start = (bf16[3,3,3,256,256]{4,3,2,1,0:T(8,128)(2,1)S(1)}, bf16[3,3,3,256,256]{4,3,2,1,0:T(8,128)(2,1)}, u32[]{:S(2)}) copy-start(bf16[3,3,3,256,256]{4,3,2,1,0:T(8,128)(2,1)} %param.8) | copy-start | bytes 10616836
  7.2 219.0 %reduce-scatter.7.cloned.1.call-start = ((), (), s32[]{:S(2)}) async-start(), calls=%async_computation.6 | async-start | bytes 9175040 | tf_op jit(solution)/shard_map/reduce_scatter | solution.py:90
  8.9 13.0 %collective-permute-start = (bf16[2,8,8,256]{3,2,1,0:T(8,128)(2,1)}, bf16[2,8,8,256]{3,2,1,0:T(8,128)(2,1)}, u32[]{:S(2)}, u32[]{:S(2)}) collective-permute-start(bf16[2,8,8,256]{3,2,1,0:T(8,128)(2,1)} %slice.77), channel_id=1, source_target_pairs={{0,32},{32,64},{64,96},{1,33},{33,65},{65,97},{2,34},{34,66},{66,9... | collective-permute-start | bytes 196616 | tf_op jit(solution)/shard_map/ppermute | solution.py:14
  16.7 24.6 %collective-permute-start.10 = (bf16[2,16,16,256]{3,2,1,0:T(8,128)(2,1)}, bf16[2,16,16,256]{3,2,1,0:T(8,128)(2,1)}, u32[]{:S(2)}, u32[]{:S(2)}) collective-permute-start(bf16[2,16,16,256]{3,2,1,0:T(8,128)(2,1)} %slice.89), channel_id=1, source_target_pairs={{32,0},{64,32},{96,64},{33,1},{65,33},{97,65},{34,2},{66,34},{98,6... | collective-permute-start | bytes 786440 | tf_op jit(solution)/shard_map/ppermute | solution.py:14
  28.1 4.9 collective-permute-start.1
  31.6 5.0 collective-permute-start.2
  36.8 12.8 %collective-permute-start.3 = (bf16[6,18,1,256]{3,2,1,0:T(2,128)(2,1)S(1)}, bf16[6,18,1,256]{3,2,1,0:T(2,128)(2,1)S(1)}, u32[]{:S(2)}, u32[]{:S(2)}) collective-permute-start(bf16[6,18,1,256]{3,2,1,0:T(2,128)(2,1)S(1)} %get-tuple-element.26), channel_id=1, source_target_pairs={{0,1},{1,2},{2,3},{4,5},{5,6},{6,7},{8,9},{9,10},{10,11},{12,13},{... | collective-permute-start | bytes 165896 | tf_op jit(solution)/shard_map/ppermute | solution.py:25
  40.0 9.7 %collective-permute-start.4 = (bf16[6,18,1,256]{3,2,1,0:T(2,128)(2,1)S(1)}, bf16[6,18,1,256]{3,2,1,0:T(2,128)(2,1)S(1)}, u32[]{:S(2)}, u32[]{:S(2)}) collective-permute-start(bf16[6,18,1,256]{3,2,1,0:T(2,128)(2,1)S(1)} %get-tuple-element.27), channel_id=1, source_target_pairs={{1,0},{2,1},{3,2},{5,4},{6,5},{7,6},{9,8},{10,9},{11,10},{13,12},{... | collective-permute-start | bytes 165896 | tf_op jit(solution)/shard_map/ppermute | solution.py:27
  44.4 15.2 %collective-permute-start.11 = (bf16[6,1,16,256]{3,2,1,0:T(8,128)(2,1)}, bf16[6,1,16,256]{3,2,1,0:T(8,128)(2,1)}, u32[]{:S(2)}, u32[]{:S(2)}) collective-permute-start(bf16[6,1,16,256]{3,2,1,0:T(8,128)(2,1)} %get-tuple-element.30), channel_id=1, source_target_pairs={{0,4},{4,8},{8,12},{12,16},{16,20},{20,24},{24,28},{1,5},{5,9},{9,... | collective-permute-start | bytes 147464 | tf_op jit(solution)/shard_map/ppermute | solution.py:25
  48.4 11.2 %collective-permute-start.12 = (bf16[6,1,16,256]{3,2,1,0:T(8,128)(2,1)}, bf16[6,1,16,256]{3,2,1,0:T(8,128)(2,1)}, u32[]{:S(2)}, u32[]{:S(2)}) collective-permute-start(bf16[6,1,16,256]{3,2,1,0:T(8,128)(2,1)} %get-tuple-element.31), channel_id=1, source_target_pairs={{4,0},{8,4},{12,8},{16,12},{20,16},{24,20},{28,24},{5,1},{9,5},{13... | collective-permute-start | bytes 147464 | tf_op jit(solution)/shard_map/ppermute | solution.py:27
  60.6 15.1 %collective-permute-start.13 = (bf16[6,18,1,256]{3,2,1,0:T(2,128)(2,1)S(1)}, bf16[6,18,1,256]{3,2,1,0:T(2,128)(2,1)S(1)}, u32[]{:S(2)}, u32[]{:S(2)}) collective-permute-start(bf16[6,18,1,256]{3,2,1,0:T(2,128)(2,1)S(1)} %get-tuple-element.24), channel_id=1, source_target_pairs={{0,1},{1,2},{2,3},{4,5},{5,6},{6,7},{8,9},{9,10},{10,11},{12,13},{... | collective-permute-start | bytes 165896 | tf_op jit(solution)/shard_map/ppermute | solution.py:25
  64.6 11.1 %collective-permute-start.14 = (bf16[6,18,1,256]{3,2,1,0:T(2,128)(2,1)S(1)}, bf16[6,18,1,256]{3,2,1,0:T(2,128)(2,1)S(1)}, u32[]{:S(2)}, u32[]{:S(2)}) collective-permute-start(bf16[6,18,1,256]{3,2,1,0:T(2,128)(2,1)S(1)} %get-tuple-element.25), channel_id=1, source_target_pairs={{1,0},{2,1},{3,2},{5,4},{6,5},{7,6},{9,8},{10,9},{11,10},{13,12},{... | collective-permute-start | bytes 165896 | tf_op jit(solution)/shard_map/ppermute | solution.py:27
  96.8 11.1 %collective-permute-start.5 = (bf16[2,16,16,256]{3,1,2,0:T(8,128)(2,1)S(1)}, bf16[2,16,16,256]{3,1,2,0:T(8,128)(2,1)S(1)}, u32[]{:S(2)}, u32[]{:S(2)}) collective-permute-start(bf16[2,16,16,256]{3,1,2,0:T(8,128)(2,1)S(1)} %slice.117), channel_id=1, source_target_pairs={{0,32},{32,64},{64,96},{1,33},{33,65},{65,97},{2,34},{34,66},{66,9... | collective-permute-start | bytes 786440 | tf_op jit(solution)/shard_map/ppermute | solution.py:14
  108.1 7.7 %collective-permute-start.6 = (bf16[6,1,16,256]{3,1,2,0:T(2,128)(2,1)S(1)}, bf16[6,1,16,256]{3,1,2,0:T(2,128)(2,1)S(1)}, u32[]{:S(2)}, u32[]{:S(2)}) collective-permute-start(bf16[6,1,16,256]{3,1,2,0:T(2,128)(2,1)S(1)} %get-tuple-element.32), channel_id=1, source_target_pairs={{0,4},{4,8},{8,12},{12,16},{16,20},{20,24},{24,28},{1,5},{5,9},{9,... | collective-permute-start | bytes 147464 | tf_op jit(solution)/shard_map/ppermute | solution.py:25
  112.4 5.4 collective-permute-start.7
  115.9 26.9 %copy-start.15 = (bf16[6,1,16,256]{3,1,2,0:T(2,128)(2,1)}, bf16[6,1,16,256]{3,1,2,0:T(2,128)(2,1)S(1)}, u32[]{:S(2)}) copy-start(bf16[6,1,16,256]{3,1,2,0:T(2,128)(2,1)S(1)} %collective-permute-done.6) | copy-start | bytes 147460
  117.8 25.0 %copy-start.16 = (bf16[6,1,16,256]{3,1,2,0:T(2,128)(2,1)}, bf16[6,1,16,256]{3,1,2,0:T(2,128)(2,1)S(1)}, u32[]{:S(2)}) copy-start(bf16[6,1,16,256]{3,1,2,0:T(2,128)(2,1)S(1)} %collective-permute-done.7) | copy-start | bytes 147460
  118.5 27.8 %collective-permute-start.8 = (bf16[6,18,1,256]{3,1,2,0:T(8,128)(2,1)}, bf16[6,18,1,256]{3,1,2,0:T(8,128)(2,1)}, u32[]{:S(2)}, u32[]{:S(2)}) collective-permute-start(bf16[6,18,1,256]{3,1,2,0:T(8,128)(2,1)} %get-tuple-element.22), channel_id=1, source_target_pairs={{0,1},{1,2},{2,3},{4,5},{5,6},{6,7},{8,9},{9,10},{10,11},{12,13},{... | collective-permute-start | bytes 165896 | tf_op jit(solution)/shard_map/ppermute | solution.py:25
  123.7 22.6 %collective-permute-start.9 = (bf16[6,18,1,256]{3,1,2,0:T(8,128)(2,1)}, bf16[6,18,1,256]{3,1,2,0:T(8,128)(2,1)}, u32[]{:S(2)}, u32[]{:S(2)}) collective-permute-start(bf16[6,18,1,256]{3,1,2,0:T(8,128)(2,1)} %get-tuple-element.23), channel_id=1, source_target_pairs={{1,0},{2,1},{3,2},{5,4},{6,5},{7,6},{9,8},{10,9},{11,10},{13,12},{... | collective-permute-start | bytes 165896 | tf_op jit(solution)/shard_map/ppermute | solution.py:27
  146.2 154.9 %reduce-scatter.13.cloned.1.call-start = ((), (), s32[]{:S(2)}) async-start(), calls=%async_computation.10 | async-start | bytes 9175040 | tf_op jit(solution)/shard_map/reduce_scatter | solution.py:90
  170.2 169.8 %reduce-scatter.9.cloned.1.call-start = ((), (), s32[]{:S(2)}) async-start(), calls=%async_computation.7 | async-start | bytes 2064384 | tf_op jit(solution)/shard_map/reduce_scatter | solution.py:90
  226.2 157.1 %reduce-scatter.15.cloned.1.call-start = ((), (), s32[]{:S(2)}) async-start(), calls=%async_computation.11 | async-start | bytes 2064384 | tf_op jit(solution)/shard_map/reduce_scatter | solution.py:90
  301.1 106.9 %reduce-scatter.11.cloned.1.call-start = ((), (), s32[]{:S(2)}) async-start(), calls=%async_computation.8 | async-start | bytes 286720 | tf_op jit(solution)/shard_map/reduce_scatter | solution.py:90
  340.0 105.2 %reduce-scatter.17.cloned.1.call-start = ((), (), s32[]{:S(2)}) async-start(), calls=%async_computation.12 | async-start | bytes 286720 | tf_op jit(solution)/shard_map/reduce_scatter | solution.py:90
  383.3 179.6 %all-gather.3.cloned.1.call-start = ((), (), s32[]{:S(2)}) async-start(), calls=%async_computation.9 | async-start | bytes 4587520 | tf_op jit(solution)/shard_map/all_gather | solution.py:93
  445.1 123.6 %all-gather.5.cloned.1.call-start = ((), (), s32[]{:S(2)}) async-start(), calls=%async_computation.13 | async-start | bytes 4587520 | tf_op jit(solution)/shard_map/all_gather | solution.py:93
  484.8 43.1 %copy-start.12 = (bf16[4,8,8,256]{3,2,1,0:T(8,128)(2,1)S(1)}, bf16[4,8,8,256]{3,2,1,0:T(8,128)(2,1)}, u32[]{:S(2)}) copy-start(bf16[4,8,8,256]{3,2,1,0:T(8,128)(2,1)} %param.7) | copy-start | bytes 393220
  485.8 27.2 %collective-permute-start.15 = (bf16[2,16,16,256]{3,1,2,0:T(8,128)(2,1)S(1)}, bf16[2,16,16,256]{3,1,2,0:T(8,128)(2,1)S(1)}, u32[]{:S(2)}, u32[]{:S(2)}) collective-permute-start(bf16[2,16,16,256]{3,1,2,0:T(8,128)(2,1)S(1)} %slice.124), channel_id=1, source_target_pairs={{32,0},{64,32},{96,64},{33,1},{65,33},{97,65},{34,2},{66,34},{98,6... | collective-permute-start | bytes 786440 | tf_op jit(solution)/shard_map/ppermute | solution.py:14
  514.3 4.4 collective-permute-start.16
  517.1 5.8 collective-permute-start.17
  524.4 6.8 %collective-permute-start.18 = (bf16[6,18,1,256]{3,1,2,0:T(8,128)(2,1)}, bf16[6,18,1,256]{3,1,2,0:T(8,128)(2,1)}, u32[]{:S(2)}, u32[]{:S(2)}) collective-permute-start(bf16[6,18,1,256]{3,1,2,0:T(8,128)(2,1)} %get-tuple-element.20), channel_id=1, source_target_pairs={{0,1},{1,2},{2,3},{4,5},{5,6},{6,7},{8,9},{9,10},{10,11},{12,13},{... | collective-permute-start | bytes 165896 | tf_op jit(solution)/shard_map/ppermute | solution.py:25
  526.6 5.7 collective-permute-start.19
  (22 other events, 120.8 us)
Sparse Core Ops, SparseCore 0:
  146.3 79.7 reduce-scatter.6
  228.8 72.2 reduce-scatter.12
  303.5 36.4 reduce-scatter.8
  342.3 40.9 reduce-scatter.14
  385.5 22.4 reduce-scatter.10
  410.2 20.7 reduce-scatter.16
  445.3 50.9 all-gather.2
  498.0 40.3 all-gather.4

commit v2 on v1

--- a/solution.py
+++ b/solution.py
@@ -78,20 +78,8 @@
     return jnp.transpose(summed, (1, 2, 3, 0, 4))
 
 
-def reduced(grad):
-    count = 8
-    for axis in ALL:
-        count *= lax.axis_size(axis)
-    flat = grad.reshape(-1, grad.shape[-1])
-    rows = flat.shape[0]
-    padded = -(-rows // count) * count
-    flat = jnp.pad(flat, ((0, padded - rows), (0, 0)))
-    for axis in ALL:
-        flat = lax.psum_scatter(flat, axis, scatter_dimension=0, tiled=True)
-    flat = flat.astype(jnp.bfloat16)
-    for axis in ALL[::-1]:
-        flat = lax.all_gather(flat, axis, axis=0, tiled=True)
-    return flat[:rows].astype(jnp.float32).reshape(grad.shape)
+def reduced(grad, axes=ALL):
+    return lax.psum(grad, axes)
 
 
 def with_earlier(field):
@@ -137,7 +125,7 @@
     grad_pre = (grad_dropped * scaling * sigma * (1.0 + pre_first * (1.0 - sigma))).astype(
         jnp.bfloat16
     )
-    grad_first = reduced(weight_gradient(cells_ext, grad_pre))
+    grad_first = reduced(weight_gradient(cells_ext, grad_pre), ALL[::-1])
     grad_cells = upstream.astype(jnp.float32) + convolve(
         face_cells(with_later(grad_pre)), flipped(w_first)
     )

time: 589 us -> 497 us (0.84)
  blocking collectives: 75 us -> 0 us
  starting transfers between devices: 76.9 us -> 60.6 us
  other arithmetic: 33.3 us -> 23.5 us
  waiting for transfers between devices: 256 us -> 264 us
    psum x0 -> x2, waiting for transfers between devices: none -> 254 us  [reduced(): return lax.psum(grad, axes)]
    reduce_scatter x6 -> x0, waiting for transfers between devices: 237 us -> none  [reduced(): flat = lax.psum_scatter(flat, axis, scatter_dimension=0, tiled=True)]
    all_gather x4 -> x0, blocking collectives: 75 us -> none  [reduced(): flat = lax.all_gather(flat, axis, axis=0, tiled=True)]
    ppermute x4, starting transfers between devices: 36.8 us -> 18 us  [shifted(): return lax.ppermute(block, axis, route)]
    unnamed x53 -> x57, local copies, waits for them, and re-layouts: 9.71 us -> 19.6 us
    ppermute x4, waiting for transfers between devices: 8.64 us -> 0.01 us  [shifted(): return lax.ppermute(block, axis, route)]
    reshape x2 -> x0, other arithmetic: 7.68 us -> none  [reduced(): return flat[:rows].astype(jnp.float32).reshape(grad.shape)]
    pad x2 -> x0, local copies, waits for them, and re-layouts: 6.99 us -> none  [reduced(): flat = jnp.pad(flat, ((0, padded - rows), (0, 0)))]
  transfers between devices with their start and end apart: 28 -> 22, of which waited for: 12 -> 7; matrix products, arithmetic and copies ran while one was open for 21% -> 24% of each run, Pallas kernels for 0% -> 0%
where the time goes in v2:
time: 497 us; the launch traced here: 491 us
  waiting for transfers between devices  264 us (53%)
  matrix products  65 us (13%)
  local copies, waits for them, and re-layouts  62.6 us (13%)
  starting transfers between devices  60.6 us (12%)
  other arithmetic  23.5 us (5%)
  between operations  14.9 us (3%)
    psum x2, waiting for transfers between devices, reduced(): return lax.psum(grad, axes)  254 us
    transpose x2, matrix products, weight_gradient(): return jnp.transpose(summed, (1, 2, 3, 0, 4))  38.8 us
    ppermute x8, starting transfers between devices, extended_2(): lax.ppermute(tail, axis, [(i, (i + 1) % count) for i in range(ends)])  31.6 us
    conv_general_dilated x4, matrix products, convolve(): lax.conv_general_dilated(extended[None], weight, (1, 1, 1), 'VALID', dime...  26.1 us
    unnamed x57, local copies, waits for them, and re-layouts  19.6 us
    ppermute x4, starting transfers between devices, shifted(): return lax.ppermute(block, axis, route)  18 us
    conv_general_dilated x14, local copies, waits for them, and re-layouts, convolve(): lax.conv_general_dilated(extended[None], weight, (1, 1, 1), 'VALID', dime...  17.8 us
    ppermute x8, starting transfers between devices, extended_2(): lax.ppermute(head, axis, [((i + 1) % count, i) for i in range(ends)])  11 us
  transfers between devices with their start and end apart: 22, of which 7 were waited for; matrix products, arithmetic and copies ran while one was open for 24% of the time, Pallas kernels for 0%

profile of v2, /device:TPU:1, one launch (start us, length us, event | category | flops | bytes accessed | tf_op | source)
XLA Modules:
  0.0 491.1 jit_solution(6102498772503347900)
XLA Ops:
  8.9 6.2 %collective-permute-start = (bf16[2,8,8,256]{3,2,1,0:T(8,128)(2,1)}, bf16[2,8,8,256]{3,2,1,0:T(8,128)(2,1)}, u32[]{:S(2)}, u32[]{:S(2)}) collective-permute-start(bf16[2,8,8,256]{3,2,1,0:T(8,128)(2,1)} %slice.71), channel_id=1, source_target_pairs={{0,32},{32,64},{64,96},{1,33},{33,65},{65,97},{2,34},{34,66},{66,9... | collective-permute-start | bytes 196616 | tf_op jit(solution)/shard_map/ppermute | solution.py:14
  24.3 3.0 reshape.85
  28.1 3.5 collective-permute-start.1
  34.2 2.5 collective-permute-done.2
  36.9 3.1 collective-permute-start.3
  44.4 4.0 collective-permute-start.11
  52.8 4.6 reshape.89
  60.6 4.0 collective-permute-start.13
  66.5 7.8 %add_divide_fusion = (f32[4,16,8,3,256]{4,2,3,1,0:T(8,128)}, f32[4,16,8,3,256]{4,2,3,1,0:T(8,128)}, f32[4,16,8,3,256]{4,2,3,1,0:T(8,128)S(1)}) fusion(f32[256]{0:T(256)S(1)} %copy-done.18, bf16[3,3,3,256,256]{4,3,2,1,0:T(8,128)(2,1)S(1)} %copy-done, bf16[6,18,1,7,2,256]{5,3,4,1,0,2:T(8,128)(2,1)S(1)} %slice.107, ...), kind=kOutput, calls=%fused_computation.34 | convolution fusion | flops 5445599232 | bytes 10359832 | tf_op jit(solution)/shard_map/conv_general_dilated | solution.py:55
  78.9 4.8 reshape.103
  86.2 5.9 %fusion.42 = f32[4,16,8,3,256]{4,2,3,1,0:T(8,128)S(1)} fusion(bf16[3,3,3,256,256]{4,3,2,1,0:T(8,128)(2,1)S(1)} %copy-done.20, bf16[6,18,1,7,2,256]{5,3,4,1,0,2:T(8,128)(2,1)S(1)} %slice.114, bf16[6,18,1,8,3,256]{5,3,4,1,0,2:T(8,128)(2,1)S(1)} %copy.47, pred[8,3]{0,1:T(4,128)(4,1)S(1)} %copy-done.23), kind=kOutput, calls=%fused_computation.43 | convolution fusion | flops 5442846720 | bytes 7213080 | tf_op jit(solution)/shard_map/conv_general_dilated | solution.py:55
  93.5 2.4 fusion.55
  96.0 8.0 %collective-permute-start.5 = (bf16[2,16,16,256]{3,1,2,0:T(8,128)(2,1)S(1)}, bf16[2,16,16,256]{3,1,2,0:T(8,128)(2,1)S(1)}, u32[]{:S(2)}, u32[]{:S(2)}) collective-permute-start(bf16[2,16,16,256]{3,1,2,0:T(8,128)(2,1)S(1)} %slice.109), channel_id=1, source_target_pairs={{0,32},{32,64},{64,96},{1,33},{33,65},{65,97},{2,34},{34,66},{66,9... | collective-permute-start | bytes 786440 | tf_op jit(solution)/shard_map/ppermute | solution.py:14
  107.9 4.3 collective-permute-start.6
  113.5 2.2 fusion.67
  118.3 4.9 collective-permute-start.8
  124.5 19.6 %fusion.34 = f32[3,3,3,256,256]{4,3,2,1,0:T(8,128)} fusion(bf16[1,6,18,18,256]{4,3,2,1,0:T(8,128)(2,1)S(1)} %copy-done.12, bf16[1,4,16,16,256]{4,2,3,1,0:T(8,128)(2,1)S(1)} %fusion.67), kind=kOutput, calls=%fused_computation.31 | convolution fusion | flops 3623878656 | bytes 8597504 | tf_op jit(solution)/shard_map/transpose | solution.py:78
  144.1 3.2 fusion.91
  147.3 19.2 %fusion.32 = f32[3,3,3,256,256]{4,3,2,1,0:T(8,128)} fusion(bf16[1,6,18,18,256]{4,2,3,1,0:T(8,128)(2,1)S(1)} %get-tuple-element.16, bf16[1,4,16,16,256]{4,3,2,1,0:T(8,128)(2,1)S(1)} %bitcast.113), kind=kOutput, calls=%fused_computation.29 | convolution fusion | flops 3623878656 | bytes 8597504 | tf_op jit(solution)/shard_map/transpose | solution.py:78
  168.0 3.3 collective-permute-start.16
  173.7 3.8 collective-permute-done.17
  179.1 4.5 collective-permute-start.18
  186.3 2.2 convert_element_type.30
  189.5 2.1 maximum_bitcast_fusion.1
  192.4 5.9 %fusion.36 = f32[4,16,8,3,256]{4,2,3,1,0:T(8,128)S(1)} fusion(bf16[3,3,3,256,256]{4,3,2,1,0:T(8,128)(2,1)S(1)} %copy-done, bf16[6,18,1,7,2,256]{5,3,4,1,0,2:T(8,128)(2,1)S(1)} %slice.117, bf16[6,18,1,8,3,256]{5,3,4,1,0,2:T(8,128)(2,1)S(1)} %copy.51, pred[8,3]{0,1:T(4,128)(4,1)S(1)} %copy-done.24), kind=kOutput, calls=%fused_computation.41 | convolution fusion | flops 5442846720 | bytes 7213080 | tf_op jit(solution)/shard_map/conv_general_dilated | solution.py:55
  200.5 2.8 reshape.86
  203.4 2.7 reduce_sum.9
  211.2 6.5 %fusion.39 = f32[4,16,8,3,256]{4,2,3,1,0:T(8,128)S(1)} fusion(bf16[3,3,3,256,256]{4,3,2,1,0:T(8,128)(2,1)S(1)} %copy-done.21, bf16[6,18,1,7,2,256]{5,3,4,1,0,2:T(8,128)(2,1)S(1)} %slice.110, bf16[6,18,1,8,3,256]{5,3,4,1,0,2:T(8,128)(2,1)S(1)} %copy.43, pred[8,3]{0,1:T(4,128)(4,1)S(1)} %copy-done.24), kind=kOutput, calls=%fused_computation.42 | convolution fusion | flops 5442846720 | bytes 7213080 | tf_op jit(solution)/shard_map/conv_general_dilated | solution.py:55
  220.1 91.0 %all-reduce.3.cloned.1.call-done = f32[3,3,3,256,256]{4,3,2,1,0:T(8,128)} async-done(((f32[3,3,3,256,256]{4,3,2,1,0:T(8,128)}), f32[3,3,3,256,256]{4,3,2,1,0:T(8,128)}) %all-reduce.3.cloned.1.call-update) | async-done | bytes 7077904 | tf_op jit(solution)/shard_map/psum | solution.py:82
  311.1 163.1 %all-reduce.5.cloned.1.call-done = f32[3,3,3,256,256]{4,3,2,1,0:T(8,128)} async-done(((f32[3,3,3,256,256]{4,3,2,1,0:T(8,128)}), f32[3,3,3,256,256]{4,3,2,1,0:T(8,128)}) %all-reduce.5.cloned.1.call-update) | async-done | bytes 7077904 | tf_op jit(solution)/shard_map/psum | solution.py:82
  474.2 6.9 %copy.82 = f32[3,3,3,256,256]{4,3,2,1,0:T(8,128)} copy(f32[3,3,3,256,256]{4,3,2,1,0:T(8,128)} %all-reduce.3.cloned.1.call-done) | data formatting | bytes 14155776
  481.1 3.0 copy.83
  (132 shorter events, 65.2 us)
Async XLA Ops:
  7.2 59.3 %copy-start = (bf16[3,3,3,256,256]{4,3,2,1,0:T(8,128)(2,1)S(1)}, bf16[3,3,3,256,256]{4,3,2,1,0:T(8,128)(2,1)}, u32[]{:S(2)}) copy-start(bf16[3,3,3,256,256]{4,3,2,1,0:T(8,128)(2,1)} %param.8) | copy-start | bytes 10616836
  7.2 303.9 %all-reduce.3.cloned.1.call-start = ((), (), s32[]{:S(2)}) async-start(), calls=%async_computation | async-start | bytes 14155776 | tf_op jit(solution)/shard_map/psum | solution.py:82
  8.9 13.0 %collective-permute-start = (bf16[2,8,8,256]{3,2,1,0:T(8,128)(2,1)}, bf16[2,8,8,256]{3,2,1,0:T(8,128)(2,1)}, u32[]{:S(2)}, u32[]{:S(2)}) collective-permute-start(bf16[2,8,8,256]{3,2,1,0:T(8,128)(2,1)} %slice.71), channel_id=1, source_target_pairs={{0,32},{32,64},{64,96},{1,33},{33,65},{65,97},{2,34},{34,66},{66,9... | collective-permute-start | bytes 196616 | tf_op jit(solution)/shard_map/ppermute | solution.py:14
  16.7 24.6 %collective-permute-start.10 = (bf16[2,16,16,256]{3,2,1,0:T(8,128)(2,1)}, bf16[2,16,16,256]{3,2,1,0:T(8,128)(2,1)}, u32[]{:S(2)}, u32[]{:S(2)}) collective-permute-start(bf16[2,16,16,256]{3,2,1,0:T(8,128)(2,1)} %slice.83), channel_id=1, source_target_pairs={{32,0},{64,32},{96,64},{33,1},{65,33},{97,65},{34,2},{66,34},{98,6... | collective-permute-start | bytes 786440 | tf_op jit(solution)/shard_map/ppermute | solution.py:14
  28.1 4.9 collective-permute-start.1
  31.7 5.0 %collective-permute-start.2 = (bf16[6,1,16,256]{3,2,1,0:T(8,128)(2,1)S(1)}, bf16[6,1,16,256]{3,2,1,0:T(8,128)(2,1)S(1)}, u32[]{:S(2)}, u32[]{:S(2)}) collective-permute-start(bf16[6,1,16,256]{3,2,1,0:T(8,128)(2,1)S(1)} %get-tuple-element.34), channel_id=1, source_target_pairs={{4,0},{8,4},{12,8},{16,12},{20,16},{24,20},{28,24},{5,1},{9,5},{13... | collective-permute-start | bytes 147464 | tf_op jit(solution)/shard_map/ppermute | solution.py:27
  36.9 12.8 %collective-permute-start.3 = (bf16[6,18,1,256]{3,2,1,0:T(2,128)(2,1)S(1)}, bf16[6,18,1,256]{3,2,1,0:T(2,128)(2,1)S(1)}, u32[]{:S(2)}, u32[]{:S(2)}) collective-permute-start(bf16[6,18,1,256]{3,2,1,0:T(2,128)(2,1)S(1)} %get-tuple-element.26), channel_id=1, source_target_pairs={{0,1},{1,2},{2,3},{4,5},{5,6},{6,7},{8,9},{9,10},{10,11},{12,13},{... | collective-permute-start | bytes 165896 | tf_op jit(solution)/shard_map/ppermute | solution.py:25
  40.0 9.7 %collective-permute-start.4 = (bf16[6,18,1,256]{3,2,1,0:T(2,128)(2,1)S(1)}, bf16[6,18,1,256]{3,2,1,0:T(2,128)(2,1)S(1)}, u32[]{:S(2)}, u32[]{:S(2)}) collective-permute-start(bf16[6,18,1,256]{3,2,1,0:T(2,128)(2,1)S(1)} %get-tuple-element.27), channel_id=1, source_target_pairs={{1,0},{2,1},{3,2},{5,4},{6,5},{7,6},{9,8},{10,9},{11,10},{13,12},{... | collective-permute-start | bytes 165896 | tf_op jit(solution)/shard_map/ppermute | solution.py:27
  44.4 15.2 %collective-permute-start.11 = (bf16[6,1,16,256]{3,2,1,0:T(8,128)(2,1)}, bf16[6,1,16,256]{3,2,1,0:T(8,128)(2,1)}, u32[]{:S(2)}, u32[]{:S(2)}) collective-permute-start(bf16[6,1,16,256]{3,2,1,0:T(8,128)(2,1)} %get-tuple-element.30), channel_id=1, source_target_pairs={{0,4},{4,8},{8,12},{12,16},{16,20},{20,24},{24,28},{1,5},{5,9},{9,... | collective-permute-start | bytes 147464 | tf_op jit(solution)/shard_map/ppermute | solution.py:25
  48.4 11.2 %collective-permute-start.12 = (bf16[6,1,16,256]{3,2,1,0:T(8,128)(2,1)}, bf16[6,1,16,256]{3,2,1,0:T(8,128)(2,1)}, u32[]{:S(2)}, u32[]{:S(2)}) collective-permute-start(bf16[6,1,16,256]{3,2,1,0:T(8,128)(2,1)} %get-tuple-element.31), channel_id=1, source_target_pairs={{4,0},{8,4},{12,8},{16,12},{20,16},{24,20},{28,24},{5,1},{9,5},{13... | collective-permute-start | bytes 147464 | tf_op jit(solution)/shard_map/ppermute | solution.py:27
  60.6 15.3 %collective-permute-start.13 = (bf16[6,18,1,256]{3,2,1,0:T(2,128)(2,1)S(1)}, bf16[6,18,1,256]{3,2,1,0:T(2,128)(2,1)S(1)}, u32[]{:S(2)}, u32[]{:S(2)}) collective-permute-start(bf16[6,18,1,256]{3,2,1,0:T(2,128)(2,1)S(1)} %get-tuple-element.24), channel_id=1, source_target_pairs={{0,1},{1,2},{2,3},{4,5},{5,6},{6,7},{8,9},{9,10},{10,11},{12,13},{... | collective-permute-start | bytes 165896 | tf_op jit(solution)/shard_map/ppermute | solution.py:25
  64.6 11.3 %collective-permute-start.14 = (bf16[6,18,1,256]{3,2,1,0:T(2,128)(2,1)S(1)}, bf16[6,18,1,256]{3,2,1,0:T(2,128)(2,1)S(1)}, u32[]{:S(2)}, u32[]{:S(2)}) collective-permute-start(bf16[6,18,1,256]{3,2,1,0:T(2,128)(2,1)S(1)} %get-tuple-element.25), channel_id=1, source_target_pairs={{1,0},{2,1},{3,2},{5,4},{6,5},{7,6},{9,8},{10,9},{11,10},{13,12},{... | collective-permute-start | bytes 165896 | tf_op jit(solution)/shard_map/ppermute | solution.py:27
  92.6 11.4 %copy-start.11 = (f32[4,16,8,3,256]{4,2,3,1,0:T(8,128)S(1)}, f32[4,16,8,3,256]{4,2,3,1,0:T(8,128)}, u32[]{:S(2)}) copy-start(f32[4,16,8,3,256]{4,2,3,1,0:T(8,128)} %get-tuple-element.14) | copy-start | bytes 4718596
  96.0 9.0 %copy-start.1 = (bf16[4,16,16,256]{3,1,2,0:T(8,128)(2,1)}, bf16[4,16,16,256]{3,1,2,0:T(8,128)(2,1)S(1)}, u32[]{:S(2)}) copy-start(bf16[4,16,16,256]{3,1,2,0:T(8,128)(2,1)S(1)} %get-tuple-element.12) | copy-start | bytes 1572868
  96.0 21.5 %copy-start.2 = (bf16[4,16,16,256]{3,1,2,0:T(8,128)(2,1)}, bf16[4,16,16,256]{3,1,2,0:T(8,128)(2,1)S(1)}, u32[]{:S(2)}) copy-start(bf16[4,16,16,256]{3,1,2,0:T(8,128)(2,1)S(1)} %get-tuple-element.13) | copy-start | bytes 1572868
  96.0 8.5 %copy-start.10 = (f32[4,16,8,3,256]{4,2,3,1,0:T(8,128)S(1)}, f32[4,16,8,3,256]{4,2,3,1,0:T(8,128)}, u32[]{:S(2)}) copy-start(f32[4,16,8,3,256]{4,2,3,1,0:T(8,128)} %get-tuple-element.15) | copy-start | bytes 4718596
  96.0 11.6 %collective-permute-start.5 = (bf16[2,16,16,256]{3,1,2,0:T(8,128)(2,1)S(1)}, bf16[2,16,16,256]{3,1,2,0:T(8,128)(2,1)S(1)}, u32[]{:S(2)}, u32[]{:S(2)}) collective-permute-start(bf16[2,16,16,256]{3,1,2,0:T(8,128)(2,1)S(1)} %slice.109), channel_id=1, source_target_pairs={{0,32},{32,64},{64,96},{1,33},{33,65},{65,97},{2,34},{34,66},{66,9... | collective-permute-start | bytes 786440 | tf_op jit(solution)/shard_map/ppermute | solution.py:14
  105.7 60.9 %collective-permute-start.15 = (bf16[2,16,16,256]{3,1,2,0:T(8,128)(2,1)}, bf16[2,16,16,256]{3,1,2,0:T(8,128)(2,1)}, u32[]{:S(2)}, u32[]{:S(2)}) collective-permute-start(bf16[2,16,16,256]{3,1,2,0:T(8,128)(2,1)} %slice.116), channel_id=1, source_target_pairs={{32,0},{64,32},{96,64},{33,1},{65,33},{97,65},{34,2},{66,34},{98,6... | collective-permute-start | bytes 786440 | tf_op jit(solution)/shard_map/ppermute | solution.py:14
  107.7 9.8 %copy-start.8 = (bf16[2,16,16,256]{3,1,2,0:T(8,128)(2,1)}, bf16[2,16,16,256]{3,1,2,0:T(8,128)(2,1)S(1)}, u32[]{:S(2)}) copy-start(bf16[2,16,16,256]{3,1,2,0:T(8,128)(2,1)S(1)} %collective-permute-done.5) | copy-start | bytes 786436
  107.9 7.8 %collective-permute-start.6 = (bf16[6,1,16,256]{3,1,2,0:T(2,128)(2,1)S(1)}, bf16[6,1,16,256]{3,1,2,0:T(2,128)(2,1)S(1)}, u32[]{:S(2)}, u32[]{:S(2)}) collective-permute-start(bf16[6,1,16,256]{3,1,2,0:T(2,128)(2,1)S(1)} %get-tuple-element.32), channel_id=1, source_target_pairs={{0,4},{4,8},{8,12},{12,16},{16,20},{20,24},{24,28},{1,5},{5,9},{9,... | collective-permute-start | bytes 147464 | tf_op jit(solution)/shard_map/ppermute | solution.py:25
  112.1 5.4 %collective-permute-start.7 = (bf16[6,1,16,256]{3,1,2,0:T(2,128)(2,1)S(1)}, bf16[6,1,16,256]{3,1,2,0:T(2,128)(2,1)S(1)}, u32[]{:S(2)}, u32[]{:S(2)}) collective-permute-start(bf16[6,1,16,256]{3,1,2,0:T(2,128)(2,1)S(1)} %get-tuple-element.33), channel_id=1, source_target_pairs={{4,0},{8,4},{12,8},{16,12},{20,16},{24,20},{28,24},{5,1},{9,5},{13... | collective-permute-start | bytes 147464 | tf_op jit(solution)/shard_map/ppermute | solution.py:27
  113.4 11.0 %copy-start.12 = (bf16[1,6,18,18,256]{4,3,2,1,0:T(8,128)(2,1)S(1)}, bf16[1,6,18,18,256]{4,3,2,1,0:T(8,128)(2,1)}, u32[]{:S(2)}) copy-start(bf16[1,6,18,18,256]{4,3,2,1,0:T(8,128)(2,1)} %get-tuple-element.18) | copy-start | bytes 2985988
  118.3 25.9 %collective-permute-start.8 = (bf16[6,18,1,256]{3,1,2,0:T(8,128)(2,1)}, bf16[6,18,1,256]{3,1,2,0:T(8,128)(2,1)}, u32[]{:S(2)}, u32[]{:S(2)}) collective-permute-start(bf16[6,18,1,256]{3,1,2,0:T(8,128)(2,1)} %get-tuple-element.22), channel_id=1, source_target_pairs={{0,1},{1,2},{2,3},{4,5},{5,6},{6,7},{8,9},{9,10},{10,11},{12,13},{... | collective-permute-start | bytes 165896 | tf_op jit(solution)/shard_map/ppermute | solution.py:25
  123.2 21.0 %collective-permute-start.9 = (bf16[6,18,1,256]{3,1,2,0:T(8,128)(2,1)}, bf16[6,18,1,256]{3,1,2,0:T(8,128)(2,1)}, u32[]{:S(2)}, u32[]{:S(2)}) collective-permute-start(bf16[6,18,1,256]{3,1,2,0:T(8,128)(2,1)} %get-tuple-element.23), channel_id=1, source_target_pairs={{1,0},{2,1},{3,2},{5,4},{6,5},{7,6},{9,8},{10,9},{11,10},{13,12},{... | collective-permute-start | bytes 165896 | tf_op jit(solution)/shard_map/ppermute | solution.py:27
  144.1 330.1 %all-reduce.5.cloned.1.call-start = ((), (), s32[]{:S(2)}) async-start(), calls=%async_computation.1 | async-start | bytes 14155776 | tf_op jit(solution)/shard_map/psum | solution.py:82
  166.6 18.6 %copy-start.13 = (bf16[4,8,8,256]{3,2,1,0:T(8,128)(2,1)S(1)}, bf16[4,8,8,256]{3,2,1,0:T(8,128)(2,1)}, u32[]{:S(2)}) copy-start(bf16[4,8,8,256]{3,2,1,0:T(8,128)(2,1)} %param.7) | copy-start | bytes 393220
  168.0 5.8 %collective-permute-start.16 = (bf16[6,1,16,256]{3,1,2,0:T(2,128)(2,1)S(1)}, bf16[6,1,16,256]{3,1,2,0:T(2,128)(2,1)S(1)}, u32[]{:S(2)}, u32[]{:S(2)}) collective-permute-start(bf16[6,1,16,256]{3,1,2,0:T(2,128)(2,1)S(1)} %get-tuple-element.28), channel_id=1, source_target_pairs={{0,4},{4,8},{8,12},{12,16},{16,20},{20,24},{24,28},{1,5},{5,9},{9,... | collective-permute-start | bytes 147464 | tf_op jit(solution)/shard_map/ppermute | solution.py:25
  171.3 6.3 %collective-permute-start.17 = (bf16[6,1,16,256]{3,1,2,0:T(2,128)(2,1)S(1)}, bf16[6,1,16,256]{3,1,2,0:T(2,128)(2,1)S(1)}, u32[]{:S(2)}, u32[]{:S(2)}) collective-permute-start(bf16[6,1,16,256]{3,1,2,0:T(2,128)(2,1)S(1)} %get-tuple-element.29), channel_id=1, source_target_pairs={{4,0},{8,4},{12,8},{16,12},{20,16},{24,20},{28,24},{5,1},{9,5},{13... | collective-permute-start | bytes 147464 | tf_op jit(solution)/shard_map/ppermute | solution.py:27
  173.7 9.9 %copy-start.14 = (bf16[6,1,16,256]{3,1,2,0:T(2,128)(2,1)}, bf16[6,1,16,256]{3,1,2,0:T(2,128)(2,1)S(1)}, u32[]{:S(2)}) copy-start(bf16[6,1,16,256]{3,1,2,0:T(2,128)(2,1)S(1)} %collective-permute-done.16) | copy-start | bytes 147460
  177.6 7.6 %copy-start.15 = (bf16[6,1,16,256]{3,1,2,0:T(2,128)(2,1)}, bf16[6,1,16,256]{3,1,2,0:T(2,128)(2,1)S(1)}, u32[]{:S(2)}) copy-start(bf16[6,1,16,256]{3,1,2,0:T(2,128)(2,1)S(1)} %collective-permute-done.17) | copy-start | bytes 147460
  179.1 9.3 %collective-permute-start.18 = (bf16[6,18,1,256]{3,1,2,0:T(8,128)(2,1)}, bf16[6,18,1,256]{3,1,2,0:T(8,128)(2,1)}, u32[]{:S(2)}, u32[]{:S(2)}) collective-permute-start(bf16[6,18,1,256]{3,1,2,0:T(8,128)(2,1)} %get-tuple-element.20), channel_id=1, source_target_pairs={{0,1},{1,2},{2,3},{4,5},{5,6},{6,7},{8,9},{9,10},{10,11},{12,13},{... | collective-permute-start | bytes 165896 | tf_op jit(solution)/shard_map/ppermute | solution.py:25
  183.7 5.8 %collective-permute-start.19 = (bf16[6,18,1,256]{3,1,2,0:T(8,128)(2,1)}, bf16[6,18,1,256]{3,1,2,0:T(8,128)(2,1)}, u32[]{:S(2)}, u32[]{:S(2)}) collective-permute-start(bf16[6,18,1,256]{3,1,2,0:T(8,128)(2,1)} %get-tuple-element.21), channel_id=1, source_target_pairs={{1,0},{2,1},{3,2},{5,4},{6,5},{7,6},{9,8},{10,9},{11,10},{13,12},{... | collective-permute-start | bytes 165896 | tf_op jit(solution)/shard_map/ppermute | solution.py:27
  (15 other events, 42.2 us)
Sparse Core Ops, SparseCore 0:
  144.2 166.8 all-reduce.2
  316.7 157.4 all-reduce.4

commit v3 on v2

--- a/solution.py
+++ b/solution.py
@@ -78,10 +78,6 @@
     return jnp.transpose(summed, (1, 2, 3, 0, 4))
 
 
-def reduced(grad, axes=ALL):
-    return lax.psum(grad, axes)
-
-
 def with_earlier(field):
     frames_here = field.shape[0]
     tail = shifted(field[frames_here - 2 :], "tm", 1)
@@ -116,7 +112,7 @@
     )
     dropped = (jax.nn.silu(pre_first) * scaling).astype(jnp.bfloat16)
     dropped_ext = face_cells(with_earlier(dropped))
-    grad_second = reduced(weight_gradient(dropped_ext, upstream))
+    grad_second = weight_gradient(dropped_ext, upstream)
     mixed = (cells_here.astype(jnp.float32) + convolve(dropped_ext, w_second) + b_second).astype(
         jnp.bfloat16
     )
@@ -125,7 +121,7 @@
     grad_pre = (grad_dropped * scaling * sigma * (1.0 + pre_first * (1.0 - sigma))).astype(
         jnp.bfloat16
     )
-    grad_first = reduced(weight_gradient(cells_ext, grad_pre), ALL[::-1])
+    grad_first = weight_gradient(cells_ext, grad_pre)
     grad_cells = upstream.astype(jnp.float32) + convolve(
         face_cells(with_later(grad_pre)), flipped(w_first)
     )
@@ -134,6 +130,7 @@
         .sum(axis=(2, 4))
         .astype(jnp.bfloat16)
     )
+    grad_first, grad_second = lax.psum((grad_first, grad_second), ALL)
     return (mixed, grad_latent, grad_first, grad_second)
 
 

time: 497 us -> 370 us (0.74)
  waiting for transfers between devices: 264 us -> 134 us
    psum x2 -> x1, waiting for transfers between devices: 254 us -> 113 us  [local(): grad_first, grad_second = lax.psum((grad_first, grad_second), ALL)]
    ppermute x4, waiting for transfers between devices: 0.01 us -> 11.7 us  [shifted(): return lax.ppermute(block, axis, route)]
    unnamed x57 -> x65, local copies, waits for them, and re-layouts: 19.6 us -> 19.6 us
  transfers between devices with their start and end apart: 22 -> 21, of which waited for: 7 -> 8; matrix products, arithmetic and copies ran while one was open for 24% -> 25% of each run, Pallas kernels for 0% -> 0%
where the time goes in v3:
time: 370 us; the launch traced here: 364 us
  waiting for transfers between devices  134 us (36%)
  matrix products  65 us (18%)
  local copies, waits for them, and re-layouts  63 us (17%)
  starting transfers between devices  62.9 us (17%)
  other arithmetic  23.8 us (6%)
  between operations  14.9 us (4%)
    psum x1, waiting for transfers between devices, local(): grad_first, grad_second = lax.psum((grad_first, grad_second), ALL)  113 us
    transpose x2, matrix products, weight_gradient(): return jnp.transpose(summed, (1, 2, 3, 0, 4))  38.8 us
    ppermute x8, starting transfers between devices, extended_2(): lax.ppermute(tail, axis, [(i, (i + 1) % count) for i in range(ends)])  34 us
    conv_general_dilated x4, matrix products, convolve(): lax.conv_general_dilated(extended[None], weight, (1, 1, 1), 'VALID', dime...  26.2 us
    unnamed x65, local copies, waits for them, and re-layouts  19.6 us
    ppermute x4, starting transfers between devices, shifted(): return lax.ppermute(block, axis, route)  17.8 us
    conv_general_dilated x14, local copies, waits for them, and re-layouts, convolve(): lax.conv_general_dilated(extended[None], weight, (1, 1, 1), 'VALID', dime...  17.8 us
    ppermute x4, waiting for transfers between devices, shifted(): return lax.ppermute(block, axis, route)  11.7 us
  transfers between devices with their start and end apart: 21, of which 8 were waited for; matrix products, arithmetic and copies ran while one was open for 25% of the time, Pallas kernels for 0%

profile of v3, /device:TPU:1, one launch (start us, length us, event | category | flops | bytes accessed | tf_op | source)
XLA Modules:
  0.0 364.2 jit_solution(243747136648806772)
XLA Ops:
  8.9 6.2 %collective-permute-start = (bf16[2,8,8,256]{3,2,1,0:T(8,128)(2,1)}, bf16[2,8,8,256]{3,2,1,0:T(8,128)(2,1)}, u32[]{:S(2)}, u32[]{:S(2)}) collective-permute-start(bf16[2,8,8,256]{3,2,1,0:T(8,128)(2,1)} %slice.71), channel_id=1, source_target_pairs={{0,32},{32,64},{64,96},{1,33},{33,65},{65,97},{2,34},{34,66},{66,9... | collective-permute-start | bytes 196616 | tf_op jit(solution)/shard_map/ppermute | solution.py:14
  24.4 3.0 reshape.85
  28.1 3.5 collective-permute-start.1
  34.2 2.5 collective-permute-done.2
  36.9 3.1 collective-permute-start.3
  44.5 4.0 %collective-permute-start.11 = (bf16[6,1,16,256]{3,2,1,0:T(8,128)(2,1)}, bf16[6,1,16,256]{3,2,1,0:T(8,128)(2,1)}, u32[]{:S(2)}, u32[]{:S(2)}) collective-permute-start(bf16[6,1,16,256]{3,2,1,0:T(8,128)(2,1)} %get-tuple-element.32), channel_id=1, source_target_pairs={{0,4},{4,8},{8,12},{12,16},{16,20},{20,24},{24,28},{1,5},{5,9},{9,... | collective-permute-start | bytes 147464 | tf_op jit(solution)/shard_map/ppermute | solution.py:25
  52.9 4.6 %reshape.89 = bf16[6,18,1,8,3,256]{5,4,3,1,0,2:T(4,128)(2,1)} reshape(bf16[6,18,1,24,256]{4,3,1,0,2:T(8,128)(2,1)} %pad) | data formatting | bytes 2654208 | tf_op jit(solution)/shard_map/conv_general_dilated | solution.py:55
  60.7 4.0 %collective-permute-start.13 = (bf16[6,18,1,256]{3,2,1,0:T(2,128)(2,1)S(1)}, bf16[6,18,1,256]{3,2,1,0:T(2,128)(2,1)S(1)}, u32[]{:S(2)}, u32[]{:S(2)}) collective-permute-start(bf16[6,18,1,256]{3,2,1,0:T(2,128)(2,1)S(1)} %get-tuple-element.26), channel_id=1, source_target_pairs={{0,1},{1,2},{2,3},{4,5},{5,6},{6,7},{8,9},{9,10},{10,11},{12,13},{... | collective-permute-start | bytes 165896 | tf_op jit(solution)/shard_map/ppermute | solution.py:25
  66.6 7.8 %add_divide_fusion = (f32[4,16,8,3,256]{4,2,3,1,0:T(8,128)}, f32[4,16,8,3,256]{4,2,3,1,0:T(8,128)}, f32[4,16,8,3,256]{4,2,3,1,0:T(8,128)S(1)}) fusion(f32[256]{0:T(256)S(1)} %copy-done.22, bf16[3,3,3,256,256]{4,3,2,1,0:T(8,128)(2,1)S(1)} %copy-done, bf16[6,18,1,7,2,256]{5,3,4,1,0,2:T(8,128)(2,1)S(1)} %slice.107, ...), kind=kOutput, calls=%fused_computation.34 | convolution fusion | flops 5445599232 | bytes 10359832 | tf_op jit(solution)/shard_map/conv_general_dilated | solution.py:55
  79.0 4.8 %reshape.103 = bf16[6,18,1,8,3,256]{5,4,3,1,0,2:T(4,128)(2,1)} reshape(bf16[6,18,1,24,256]{4,3,1,0,2:T(8,128)(2,1)} %pad.4) | data formatting | bytes 2654208 | tf_op jit(solution)/shard_map/conv_general_dilated | solution.py:55
  86.3 5.9 %fusion.42 = f32[4,16,8,3,256]{4,2,3,1,0:T(8,128)S(1)} fusion(bf16[3,3,3,256,256]{4,3,2,1,0:T(8,128)(2,1)S(1)} %copy-done.24, bf16[6,18,1,7,2,256]{5,3,4,1,0,2:T(8,128)(2,1)S(1)} %slice.114, bf16[6,18,1,8,3,256]{5,3,4,1,0,2:T(8,128)(2,1)S(1)} %copy.47, pred[8,3]{0,1:T(4,128)(4,1)S(1)} %copy-done.27), kind=kOutput, calls=%fused_computation.43 | convolution fusion | flops 5442846720 | bytes 7213080 | tf_op jit(solution)/shard_map/conv_general_dilated | solution.py:55
  93.6 3.1 fusion.55
  96.8 7.8 %collective-permute-start.5 = (bf16[2,16,16,256]{3,1,2,0:T(8,128)(2,1)S(1)}, bf16[2,16,16,256]{3,1,2,0:T(8,128)(2,1)S(1)}, u32[]{:S(2)}, u32[]{:S(2)}) collective-permute-start(bf16[2,16,16,256]{3,1,2,0:T(8,128)(2,1)S(1)} %slice.109), channel_id=1, source_target_pairs={{0,32},{32,64},{64,96},{1,33},{33,65},{65,97},{2,34},{34,66},{66,9... | collective-permute-start | bytes 786440 | tf_op jit(solution)/shard_map/ppermute | solution.py:14
  105.6 2.3 collective-permute-done.5
  108.1 4.3 %collective-permute-start.6 = (bf16[6,1,16,256]{3,1,2,0:T(2,128)(2,1)S(1)}, bf16[6,1,16,256]{3,1,2,0:T(2,128)(2,1)S(1)}, u32[]{:S(2)}, u32[]{:S(2)}) collective-permute-start(bf16[6,1,16,256]{3,1,2,0:T(2,128)(2,1)S(1)} %get-tuple-element.34), channel_id=1, source_target_pairs={{0,4},{4,8},{8,12},{12,16},{16,20},{20,24},{24,28},{1,5},{5,9},{9,... | collective-permute-start | bytes 147464 | tf_op jit(solution)/shard_map/ppermute | solution.py:25
  113.7 2.1 fusion.67
  118.4 5.2 %collective-permute-start.8 = (bf16[6,18,1,256]{3,1,2,0:T(8,128)(2,1)}, bf16[6,18,1,256]{3,1,2,0:T(8,128)(2,1)}, u32[]{:S(2)}, u32[]{:S(2)}) collective-permute-start(bf16[6,18,1,256]{3,1,2,0:T(8,128)(2,1)} %get-tuple-element.24), channel_id=1, source_target_pairs={{0,1},{1,2},{2,3},{4,5},{5,6},{6,7},{8,9},{9,10},{10,11},{12,13},{... | collective-permute-start | bytes 165896 | tf_op jit(solution)/shard_map/ppermute | solution.py:25
  125.0 19.6 %fusion.34 = f32[3,3,3,256,256]{4,3,2,1,0:T(8,128)} fusion(bf16[1,6,18,18,256]{4,3,2,1,0:T(8,128)(2,1)S(1)} %copy-done.14, bf16[1,4,16,16,256]{4,2,3,1,0:T(8,128)(2,1)S(1)} %fusion.67), kind=kOutput, calls=%fused_computation.31 | convolution fusion | flops 3623878656 | bytes 8597504 | tf_op jit(solution)/shard_map/transpose | solution.py:78
  144.6 2.9 fusion.91
  147.5 19.2 %fusion.32 = f32[3,3,3,256,256]{4,3,2,1,0:T(8,128)} fusion(bf16[1,6,18,18,256]{4,2,3,1,0:T(8,128)(2,1)S(1)} %get-tuple-element.18, bf16[1,4,16,16,256]{4,3,2,1,0:T(8,128)(2,1)S(1)} %bitcast.113), kind=kOutput, calls=%fused_computation.29 | convolution fusion | flops 3623878656 | bytes 8597504 | tf_op jit(solution)/shard_map/transpose | solution.py:78
  169.8 9.4 %collective-permute-done.15 = bf16[2,16,16,256]{3,1,2,0:T(8,128)(2,1)S(1)} collective-permute-done((bf16[2,16,16,256]{3,1,2,0:T(8,128)(2,1)S(1)}, bf16[2,16,16,256]{3,1,2,0:T(8,128)(2,1)S(1)}, u32[]{:S(2)}, u32[]{:S(2)}) %collective-permute-start.15) | collective-permute-done | bytes 262176 | tf_op jit(solution)/shard_map/ppermute | solution.py:14
  180.5 3.8 %collective-permute-start.16 = (bf16[6,1,16,256]{3,1,2,0:T(2,128)(2,1)S(1)}, bf16[6,1,16,256]{3,1,2,0:T(2,128)(2,1)S(1)}, u32[]{:S(2)}, u32[]{:S(2)}) collective-permute-start(bf16[6,1,16,256]{3,1,2,0:T(2,128)(2,1)S(1)} %get-tuple-element.30), channel_id=1, source_target_pairs={{0,4},{4,8},{8,12},{12,16},{16,20},{20,24},{24,28},{1,5},{5,9},{9,... | collective-permute-start | bytes 147464 | tf_op jit(solution)/shard_map/ppermute | solution.py:25
  186.3 3.7 %collective-permute-done.17 = bf16[6,1,16,256]{3,1,2,0:T(2,128)(2,1)S(1)} collective-permute-done((bf16[6,1,16,256]{3,1,2,0:T(2,128)(2,1)S(1)}, bf16[6,1,16,256]{3,1,2,0:T(2,128)(2,1)S(1)}, u32[]{:S(2)}, u32[]{:S(2)}) %collective-permute-start.17) | collective-permute-done | bytes 49184 | tf_op jit(solution)/shard_map/ppermute | solution.py:27
  191.6 6.1 %collective-permute-start.18 = (bf16[6,18,1,256]{3,1,2,0:T(8,128)(2,1)}, bf16[6,18,1,256]{3,1,2,0:T(8,128)(2,1)}, u32[]{:S(2)}, u32[]{:S(2)}) collective-permute-start(bf16[6,18,1,256]{3,1,2,0:T(8,128)(2,1)} %get-tuple-element.22), channel_id=1, source_target_pairs={{0,1},{1,2},{2,3},{4,5},{5,6},{6,7},{8,9},{9,10},{10,11},{12,13},{... | collective-permute-start | bytes 165896 | tf_op jit(solution)/shard_map/ppermute | solution.py:25
  200.3 2.2 convert_element_type.30
  206.8 5.9 %fusion.36 = f32[4,16,8,3,256]{4,2,3,1,0:T(8,128)S(1)} fusion(bf16[3,3,3,256,256]{4,3,2,1,0:T(8,128)(2,1)S(1)} %copy-done, bf16[6,18,1,7,2,256]{5,3,4,1,0,2:T(8,128)(2,1)S(1)} %slice.117, bf16[6,18,1,8,3,256]{5,3,4,1,0,2:T(8,128)(2,1)S(1)} %copy.51, pred[8,3]{0,1:T(4,128)(4,1)S(1)} %copy-done.28), kind=kOutput, calls=%fused_computation.41 | convolution fusion | flops 5442846720 | bytes 7213080 | tf_op jit(solution)/shard_map/conv_general_dilated | solution.py:55
  215.0 2.9 reshape.86
  217.9 2.8 reduce_sum.9
  225.7 6.5 %fusion.39 = f32[4,16,8,3,256]{4,2,3,1,0:T(8,128)S(1)} fusion(bf16[3,3,3,256,256]{4,3,2,1,0:T(8,128)(2,1)S(1)} %copy-done.25, bf16[6,18,1,7,2,256]{5,3,4,1,0,2:T(8,128)(2,1)S(1)} %slice.110, bf16[6,18,1,8,3,256]{5,3,4,1,0,2:T(8,128)(2,1)S(1)} %copy.43, pred[8,3]{0,1:T(4,128)(4,1)S(1)} %copy-done.28), kind=kOutput, calls=%fused_computation.42 | convolution fusion | flops 5442846720 | bytes 7213080 | tf_op jit(solution)/shard_map/conv_general_dilated | solution.py:55
  234.7 112.6 %all-reduce.3.cloned.1.call-done = (f32[3,3,3,256,256]{4,3,2,1,0:T(8,128)}, f32[3,3,3,256,256]{4,3,2,1,0:T(8,128)}) async-done(((f32[3,3,3,256,256]{4,3,2,1,0:T(8,128)}, f32[3,3,3,256,256]{4,3,2,1,0:T(8,128)}), (f32[3,3,3,256,256]{4,3,2,1,0:T(8,128)}, f32[3,3,3,256,256]{4,3,2,1,0:T(8,128)})) %all-reduce.3.cloned.1.call-update) | async-done | bytes 14155792 | tf_op jit(solution)/shard_map/psum | solution.py:133
  347.3 6.9 %copy.82 = f32[3,3,3,256,256]{4,3,2,1,0:T(8,128)} copy(f32[3,3,3,256,256]{4,3,2,1,0:T(8,128)} %get-tuple-element.45) | data formatting | bytes 14155776
  354.2 3.0 copy.83
  (137 shorter events, 67.5 us)
Async XLA Ops:
  7.2 59.4 %copy-start = (bf16[3,3,3,256,256]{4,3,2,1,0:T(8,128)(2,1)S(1)}, bf16[3,3,3,256,256]{4,3,2,1,0:T(8,128)(2,1)}, u32[]{:S(2)}) copy-start(bf16[3,3,3,256,256]{4,3,2,1,0:T(8,128)(2,1)} %param.8) | copy-start | bytes 10616836
  7.2 340.1 %all-reduce.3.cloned.1.call-start = ((), (), s32[]{:S(2)}) async-start(), calls=%async_computation | async-start | bytes 28311552 | tf_op jit(solution)/shard_map/psum | solution.py:133
  8.9 13.1 %collective-permute-start = (bf16[2,8,8,256]{3,2,1,0:T(8,128)(2,1)}, bf16[2,8,8,256]{3,2,1,0:T(8,128)(2,1)}, u32[]{:S(2)}, u32[]{:S(2)}) collective-permute-start(bf16[2,8,8,256]{3,2,1,0:T(8,128)(2,1)} %slice.71), channel_id=1, source_target_pairs={{0,32},{32,64},{64,96},{1,33},{33,65},{65,97},{2,34},{34,66},{66,9... | collective-permute-start | bytes 196616 | tf_op jit(solution)/shard_map/ppermute | solution.py:14
  16.7 24.6 %collective-permute-start.10 = (bf16[2,16,16,256]{3,2,1,0:T(8,128)(2,1)}, bf16[2,16,16,256]{3,2,1,0:T(8,128)(2,1)}, u32[]{:S(2)}, u32[]{:S(2)}) collective-permute-start(bf16[2,16,16,256]{3,2,1,0:T(8,128)(2,1)} %slice.83), channel_id=1, source_target_pairs={{32,0},{64,32},{96,64},{33,1},{65,33},{97,65},{34,2},{66,34},{98,6... | collective-permute-start | bytes 786440 | tf_op jit(solution)/shard_map/ppermute | solution.py:14
  28.1 4.9 %collective-permute-start.1 = (bf16[6,1,16,256]{3,2,1,0:T(8,128)(2,1)S(1)}, bf16[6,1,16,256]{3,2,1,0:T(8,128)(2,1)S(1)}, u32[]{:S(2)}, u32[]{:S(2)}) collective-permute-start(bf16[6,1,16,256]{3,2,1,0:T(8,128)(2,1)S(1)} %get-tuple-element.37), channel_id=1, source_target_pairs={{0,4},{4,8},{8,12},{12,16},{16,20},{20,24},{24,28},{1,5},{5,9},{9,... | collective-permute-start | bytes 147464 | tf_op jit(solution)/shard_map/ppermute | solution.py:25
  31.7 5.0 %collective-permute-start.2 = (bf16[6,1,16,256]{3,2,1,0:T(8,128)(2,1)S(1)}, bf16[6,1,16,256]{3,2,1,0:T(8,128)(2,1)S(1)}, u32[]{:S(2)}, u32[]{:S(2)}) collective-permute-start(bf16[6,1,16,256]{3,2,1,0:T(8,128)(2,1)S(1)} %get-tuple-element.36), channel_id=1, source_target_pairs={{4,0},{8,4},{12,8},{16,12},{20,16},{24,20},{28,24},{5,1},{9,5},{13... | collective-permute-start | bytes 147464 | tf_op jit(solution)/shard_map/ppermute | solution.py:27
  36.9 12.9 %collective-permute-start.3 = (bf16[6,18,1,256]{3,2,1,0:T(2,128)(2,1)S(1)}, bf16[6,18,1,256]{3,2,1,0:T(2,128)(2,1)S(1)}, u32[]{:S(2)}, u32[]{:S(2)}) collective-permute-start(bf16[6,18,1,256]{3,2,1,0:T(2,128)(2,1)S(1)} %get-tuple-element.28), channel_id=1, source_target_pairs={{0,1},{1,2},{2,3},{4,5},{5,6},{6,7},{8,9},{9,10},{10,11},{12,13},{... | collective-permute-start | bytes 165896 | tf_op jit(solution)/shard_map/ppermute | solution.py:25
  40.0 9.7 %collective-permute-start.4 = (bf16[6,18,1,256]{3,2,1,0:T(2,128)(2,1)S(1)}, bf16[6,18,1,256]{3,2,1,0:T(2,128)(2,1)S(1)}, u32[]{:S(2)}, u32[]{:S(2)}) collective-permute-start(bf16[6,18,1,256]{3,2,1,0:T(2,128)(2,1)S(1)} %get-tuple-element.29), channel_id=1, source_target_pairs={{1,0},{2,1},{3,2},{5,4},{6,5},{7,6},{9,8},{10,9},{11,10},{13,12},{... | collective-permute-start | bytes 165896 | tf_op jit(solution)/shard_map/ppermute | solution.py:27
  44.5 15.2 %collective-permute-start.11 = (bf16[6,1,16,256]{3,2,1,0:T(8,128)(2,1)}, bf16[6,1,16,256]{3,2,1,0:T(8,128)(2,1)}, u32[]{:S(2)}, u32[]{:S(2)}) collective-permute-start(bf16[6,1,16,256]{3,2,1,0:T(8,128)(2,1)} %get-tuple-element.32), channel_id=1, source_target_pairs={{0,4},{4,8},{8,12},{12,16},{16,20},{20,24},{24,28},{1,5},{5,9},{9,... | collective-permute-start | bytes 147464 | tf_op jit(solution)/shard_map/ppermute | solution.py:25
  48.5 11.2 %collective-permute-start.12 = (bf16[6,1,16,256]{3,2,1,0:T(8,128)(2,1)}, bf16[6,1,16,256]{3,2,1,0:T(8,128)(2,1)}, u32[]{:S(2)}, u32[]{:S(2)}) collective-permute-start(bf16[6,1,16,256]{3,2,1,0:T(8,128)(2,1)} %get-tuple-element.33), channel_id=1, source_target_pairs={{4,0},{8,4},{12,8},{16,12},{20,16},{24,20},{28,24},{5,1},{9,5},{13... | collective-permute-start | bytes 147464 | tf_op jit(solution)/shard_map/ppermute | solution.py:27
  60.7 15.3 %collective-permute-start.13 = (bf16[6,18,1,256]{3,2,1,0:T(2,128)(2,1)S(1)}, bf16[6,18,1,256]{3,2,1,0:T(2,128)(2,1)S(1)}, u32[]{:S(2)}, u32[]{:S(2)}) collective-permute-start(bf16[6,18,1,256]{3,2,1,0:T(2,128)(2,1)S(1)} %get-tuple-element.26), channel_id=1, source_target_pairs={{0,1},{1,2},{2,3},{4,5},{5,6},{6,7},{8,9},{9,10},{10,11},{12,13},{... | collective-permute-start | bytes 165896 | tf_op jit(solution)/shard_map/ppermute | solution.py:25
  64.7 11.3 %collective-permute-start.14 = (bf16[6,18,1,256]{3,2,1,0:T(2,128)(2,1)S(1)}, bf16[6,18,1,256]{3,2,1,0:T(2,128)(2,1)S(1)}, u32[]{:S(2)}, u32[]{:S(2)}) collective-permute-start(bf16[6,18,1,256]{3,2,1,0:T(2,128)(2,1)S(1)} %get-tuple-element.27), channel_id=1, source_target_pairs={{1,0},{2,1},{3,2},{5,4},{6,5},{7,6},{9,8},{10,9},{11,10},{13,12},{... | collective-permute-start | bytes 165896 | tf_op jit(solution)/shard_map/ppermute | solution.py:27
  92.7 11.9 %copy-start.13 = (f32[4,16,8,3,256]{4,2,3,1,0:T(8,128)S(1)}, f32[4,16,8,3,256]{4,2,3,1,0:T(8,128)}, u32[]{:S(2)}) copy-start(f32[4,16,8,3,256]{4,2,3,1,0:T(8,128)} %get-tuple-element.16) | copy-start | bytes 4718596
  96.7 21.0 %copy-start.1 = (bf16[4,16,16,256]{3,1,2,0:T(8,128)(2,1)}, bf16[4,16,16,256]{3,1,2,0:T(8,128)(2,1)S(1)}, u32[]{:S(2)}) copy-start(bf16[4,16,16,256]{3,1,2,0:T(8,128)(2,1)S(1)} %get-tuple-element.15) | copy-start | bytes 1572868
  96.8 11.1 %collective-permute-start.5 = (bf16[2,16,16,256]{3,1,2,0:T(8,128)(2,1)S(1)}, bf16[2,16,16,256]{3,1,2,0:T(8,128)(2,1)S(1)}, u32[]{:S(2)}, u32[]{:S(2)}) collective-permute-start(bf16[2,16,16,256]{3,1,2,0:T(8,128)(2,1)S(1)} %slice.109), channel_id=1, source_target_pairs={{0,32},{32,64},{64,96},{1,33},{33,65},{65,97},{2,34},{34,66},{66,9... | collective-permute-start | bytes 786440 | tf_op jit(solution)/shard_map/ppermute | solution.py:14
  108.1 7.7 %collective-permute-start.6 = (bf16[6,1,16,256]{3,1,2,0:T(2,128)(2,1)S(1)}, bf16[6,1,16,256]{3,1,2,0:T(2,128)(2,1)S(1)}, u32[]{:S(2)}, u32[]{:S(2)}) collective-permute-start(bf16[6,1,16,256]{3,1,2,0:T(2,128)(2,1)S(1)} %get-tuple-element.34), channel_id=1, source_target_pairs={{0,4},{4,8},{8,12},{12,16},{16,20},{20,24},{24,28},{1,5},{5,9},{9,... | collective-permute-start | bytes 147464 | tf_op jit(solution)/shard_map/ppermute | solution.py:25
  112.4 5.4 %collective-permute-start.7 = (bf16[6,1,16,256]{3,1,2,0:T(2,128)(2,1)S(1)}, bf16[6,1,16,256]{3,1,2,0:T(2,128)(2,1)S(1)}, u32[]{:S(2)}, u32[]{:S(2)}) collective-permute-start(bf16[6,1,16,256]{3,1,2,0:T(2,128)(2,1)S(1)} %get-tuple-element.35), channel_id=1, source_target_pairs={{4,0},{8,4},{12,8},{16,12},{20,16},{24,20},{28,24},{5,1},{9,5},{13... | collective-permute-start | bytes 147464 | tf_op jit(solution)/shard_map/ppermute | solution.py:27
  113.7 11.3 %copy-start.14 = (bf16[1,6,18,18,256]{4,3,2,1,0:T(8,128)(2,1)S(1)}, bf16[1,6,18,18,256]{4,3,2,1,0:T(8,128)(2,1)}, u32[]{:S(2)}) copy-start(bf16[1,6,18,18,256]{4,3,2,1,0:T(8,128)(2,1)} %get-tuple-element.20) | copy-start | bytes 2985988
  118.4 26.2 %collective-permute-start.8 = (bf16[6,18,1,256]{3,1,2,0:T(8,128)(2,1)}, bf16[6,18,1,256]{3,1,2,0:T(8,128)(2,1)}, u32[]{:S(2)}, u32[]{:S(2)}) collective-permute-start(bf16[6,18,1,256]{3,1,2,0:T(8,128)(2,1)} %get-tuple-element.24), channel_id=1, source_target_pairs={{0,1},{1,2},{2,3},{4,5},{5,6},{6,7},{8,9},{9,10},{10,11},{12,13},{... | collective-permute-start | bytes 165896 | tf_op jit(solution)/shard_map/ppermute | solution.py:25
  123.7 20.9 %collective-permute-start.9 = (bf16[6,18,1,256]{3,1,2,0:T(8,128)(2,1)}, bf16[6,18,1,256]{3,1,2,0:T(8,128)(2,1)}, u32[]{:S(2)}, u32[]{:S(2)}) collective-permute-start(bf16[6,18,1,256]{3,1,2,0:T(8,128)(2,1)} %get-tuple-element.25), channel_id=1, source_target_pairs={{1,0},{2,1},{3,2},{5,4},{6,5},{7,6},{9,8},{10,9},{11,10},{13,12},{... | collective-permute-start | bytes 165896 | tf_op jit(solution)/shard_map/ppermute | solution.py:27
  125.0 19.6 %copy-start.2 = (bf16[4,16,16,256]{3,1,2,0:T(8,128)(2,1)S(1)}, bf16[4,16,16,256]{3,1,2,0:T(8,128)(2,1)}, u32[]{:S(2)}) copy-start(bf16[4,16,16,256]{3,1,2,0:T(8,128)(2,1)} %copy-done.1) | copy-start | bytes 1572868
  125.0 19.6 %copy-start.10 = (bf16[2,16,16,256]{3,1,2,0:T(8,128)(2,1)S(1)}, bf16[2,16,16,256]{3,1,2,0:T(8,128)(2,1)}, u32[]{:S(2)}) copy-start(bf16[2,16,16,256]{3,1,2,0:T(8,128)(2,1)} %copy-done.9) | copy-start | bytes 786436
  125.0 19.6 %copy-start.19 = (bf16[6,1,16,256]{3,1,2,0:T(2,128)(2,1)S(1)}, bf16[6,1,16,256]{3,1,2,0:T(2,128)(2,1)}, u32[]{:S(2)}) copy-start(bf16[6,1,16,256]{3,1,2,0:T(2,128)(2,1)} %copy-done.18) | copy-start | bytes 147460
  125.0 19.6 %copy-start.21 = (bf16[6,1,16,256]{3,1,2,0:T(2,128)(2,1)S(1)}, bf16[6,1,16,256]{3,1,2,0:T(2,128)(2,1)}, u32[]{:S(2)}) copy-start(bf16[6,1,16,256]{3,1,2,0:T(2,128)(2,1)} %copy-done.20) | copy-start | bytes 147460
  166.8 32.3 %copy-start.15 = (bf16[4,8,8,256]{3,2,1,0:T(8,128)(2,1)S(1)}, bf16[4,8,8,256]{3,2,1,0:T(8,128)(2,1)}, u32[]{:S(2)}) copy-start(bf16[4,8,8,256]{3,2,1,0:T(8,128)(2,1)} %param.7) | copy-start | bytes 393220
  167.8 11.3 %collective-permute-start.15 = (bf16[2,16,16,256]{3,1,2,0:T(8,128)(2,1)S(1)}, bf16[2,16,16,256]{3,1,2,0:T(8,128)(2,1)S(1)}, u32[]{:S(2)}, u32[]{:S(2)}) collective-permute-start(bf16[2,16,16,256]{3,1,2,0:T(8,128)(2,1)S(1)} %slice.116), channel_id=1, source_target_pairs={{32,0},{64,32},{96,64},{33,1},{65,33},{97,65},{34,2},{66,34},{98,6... | collective-permute-start | bytes 786440 | tf_op jit(solution)/shard_map/ppermute | solution.py:14
  179.2 10.9 %copy-start.8 = (bf16[2,16,16,256]{3,1,2,0:T(8,128)(2,1)}, bf16[2,16,16,256]{3,1,2,0:T(8,128)(2,1)S(1)}, u32[]{:S(2)}) copy-start(bf16[2,16,16,256]{3,1,2,0:T(8,128)(2,1)S(1)} %collective-permute-done.15) | copy-start | bytes 786436
  180.5 5.9 %collective-permute-start.16 = (bf16[6,1,16,256]{3,1,2,0:T(2,128)(2,1)S(1)}, bf16[6,1,16,256]{3,1,2,0:T(2,128)(2,1)S(1)}, u32[]{:S(2)}, u32[]{:S(2)}) collective-permute-start(bf16[6,1,16,256]{3,1,2,0:T(2,128)(2,1)S(1)} %get-tuple-element.30), channel_id=1, source_target_pairs={{0,4},{4,8},{8,12},{12,16},{16,20},{20,24},{24,28},{1,5},{5,9},{9,... | collective-permute-start | bytes 147464 | tf_op jit(solution)/shard_map/ppermute | solution.py:25
  184.3 5.8 %collective-permute-start.17 = (bf16[6,1,16,256]{3,1,2,0:T(2,128)(2,1)S(1)}, bf16[6,1,16,256]{3,1,2,0:T(2,128)(2,1)S(1)}, u32[]{:S(2)}, u32[]{:S(2)}) collective-permute-start(bf16[6,1,16,256]{3,1,2,0:T(2,128)(2,1)S(1)} %get-tuple-element.31), channel_id=1, source_target_pairs={{4,0},{8,4},{12,8},{16,12},{20,16},{24,20},{28,24},{5,1},{9,5},{13... | collective-permute-start | bytes 147464 | tf_op jit(solution)/shard_map/ppermute | solution.py:27
  186.3 11.4 %copy-start.16 = (bf16[6,1,16,256]{3,1,2,0:T(2,128)(2,1)}, bf16[6,1,16,256]{3,1,2,0:T(2,128)(2,1)S(1)}, u32[]{:S(2)}) copy-start(bf16[6,1,16,256]{3,1,2,0:T(2,128)(2,1)S(1)} %collective-permute-done.16) | copy-start | bytes 147460
  191.6 10.9 %collective-permute-start.18 = (bf16[6,18,1,256]{3,1,2,0:T(8,128)(2,1)}, bf16[6,18,1,256]{3,1,2,0:T(8,128)(2,1)}, u32[]{:S(2)}, u32[]{:S(2)}) collective-permute-start(bf16[6,18,1,256]{3,1,2,0:T(8,128)(2,1)} %get-tuple-element.22), channel_id=1, source_target_pairs={{0,1},{1,2},{2,3},{4,5},{5,6},{6,7},{8,9},{9,10},{10,11},{12,13},{... | collective-permute-start | bytes 165896 | tf_op jit(solution)/shard_map/ppermute | solution.py:25
  197.7 6.2 %collective-permute-start.19 = (bf16[6,18,1,256]{3,1,2,0:T(8,128)(2,1)}, bf16[6,18,1,256]{3,1,2,0:T(8,128)(2,1)}, u32[]{:S(2)}, u32[]{:S(2)}) collective-permute-start(bf16[6,18,1,256]{3,1,2,0:T(8,128)(2,1)} %get-tuple-element.23), channel_id=1, source_target_pairs={{1,0},{2,1},{3,2},{5,4},{6,5},{7,6},{9,8},{10,9},{11,10},{13,12},{... | collective-permute-start | bytes 165896 | tf_op jit(solution)/shard_map/ppermute | solution.py:27
  (18 other events, 82.3 us)
Sparse Core Ops, SparseCore 0:
  166.9 180.3 all-reduce.2

commit v4 on v3

--- a/solution.py
+++ b/solution.py
@@ -67,15 +67,20 @@
 
 
 def weight_gradient(extended, grad):
-    summed = lax.conv_general_dilated(
-        extended[None],
-        grad[None],
-        (1, 1, 1),
-        "VALID",
-        dimension_numbers=("CDHWN", "IDHWO", "NDHWC"),
-        preferred_element_type=jnp.float32,
+    frames, height, width, channels = grad.shape
+    spread = jnp.concatenate(
+        [extended[:, b : b + height, c : c + width] for b in range(3) for c in range(3)], axis=-1
     )
-    return jnp.transpose(summed, (1, 2, 3, 0, 4))
+    taps = [
+        lax.dot_general(
+            spread[a : a + frames],
+            grad,
+            (((0, 1, 2), (0, 1, 2)), ((), ())),
+            preferred_element_type=jnp.float32,
+        )
+        for a in range(3)
+    ]
+    return jnp.stack(taps).reshape(3, 3, 3, channels, channels)
 
 
 def with_earlier(field):

time: 370 us -> 394 us (1.065)
  local copies, waits for them, and re-layouts: 63 us -> 121 us
  matrix products: 65 us -> 35.1 us
  waiting for transfers between devices: 134 us -> 116 us
  other arithmetic: 23.8 us -> 36.8 us
    transpose x2 -> x0, matrix products: 38.8 us -> none  [weight_gradient(): return jnp.transpose(summed, (1, 2, 3, 0, 4))]
    another operation x0 -> x3, local copies, waits for them, and re-layouts: none -> 33.7 us
    conv_general_dilated x14 -> x18, local copies, waits for them, and re-layouts: 17.8 us -> 30.6 us  [convolve(): lax.conv_general_dilated(extended[None], weight, (1, 1, 1), 'VALID', dime...]
    dot_general x0 -> x6, matrix products: none -> 9.15 us  [weight_gradient(): lax.dot_general(spread[a:a + frames], grad, (((0, 1, 2), (0, 1, 2)), ((),...]
    psum x1, waiting for transfers between devices: 113 us -> 104 us  [local(): grad_first, grad_second = lax.psum((grad_first, grad_second), ALL)]
    another operation x0 -> x2, other arithmetic: none -> 6.85 us  [weight_gradient(): return jnp.stack(taps).reshape(3, 3, 3, channels, channels)]
    ppermute x8, waiting for transfers between devices: 9.45 us -> 3.04 us  [extended_2(): lax.ppermute(head, axis, [((i + 1) % count, i) for i in range(ends)])]
    dot_general x0 -> x1, local copies, waits for them, and re-layouts: none -> 5.24 us  [weight_gradient(): lax.dot_general(spread[a:a + frames], grad, (((0, 1, 2), (0, 1, 2)), ((),...]
  transfers between devices with their start and end apart: 21 -> 21, of which waited for: 8 -> 6; matrix products, arithmetic and copies ran while one was open for 25% -> 37% of each run, Pallas kernels for 0% -> 0%
where the time goes in v4:
time: 394 us; the launch traced here: 389 us
  local copies, waits for them, and re-layouts  121 us (31%)
  waiting for transfers between devices  116 us (29%)
  starting transfers between devices  64.3 us (16%)
  other arithmetic  36.8 us (9%)
  matrix products  35.1 us (9%)
  between operations  15.3 us (4%)
    psum x1, waiting for transfers between devices, local(): grad_first, grad_second = lax.psum((grad_first, grad_second), ALL)  104 us
    ppermute x8, starting transfers between devices, extended_2(): lax.ppermute(tail, axis, [(i, (i + 1) % count) for i in range(ends)])  36.1 us
    another operation x3, local copies, waits for them, and re-layouts  33.7 us
    conv_general_dilated x18, local copies, waits for them, and re-layouts, convolve(): lax.conv_general_dilated(extended[None], weight, (1, 1, 1), 'VALID', dime...  30.6 us
    conv_general_dilated x4, matrix products, convolve(): lax.conv_general_dilated(extended[None], weight, (1, 1, 1), 'VALID', dime...  26 us
    unnamed x101, local copies, waits for them, and re-layouts  22 us
    ppermute x4, starting transfers between devices, shifted(): return lax.ppermute(block, axis, route)  17.9 us
    ppermute x8, starting transfers between devices, extended_2(): lax.ppermute(head, axis, [((i + 1) % count, i) for i in range(ends)])  10.3 us
  transfers between devices with their start and end apart: 21, of which 6 were waited for; matrix products, arithmetic and copies ran while one was open for 37% of the time, Pallas kernels for 0%

profile of v4, /device:TPU:1, one launch (start us, length us, event | category | flops | bytes accessed | tf_op | source)
XLA Modules:
  0.0 388.6 jit_solution(7771167317168885191)
XLA Ops:
  9.0 3.3 collective-permute-start.10
  13.8 4.8 %collective-permute-start = (bf16[2,8,8,256]{3,2,1,0:T(8,128)(2,1)}, bf16[2,8,8,256]{3,2,1,0:T(8,128)(2,1)}, u32[]{:S(2)}, u32[]{:S(2)}) collective-permute-start(bf16[2,8,8,256]{3,2,1,0:T(8,128)(2,1)} %slice.153), channel_id=1, source_target_pairs={{0,32},{32,64},{64,96},{1,33},{33,65},{65,97},{2,34},{34,66},{66,9... | collective-permute-start | bytes 196616 | tf_op jit(solution)/shard_map/ppermute | solution.py:14
  24.3 2.9 reshape.102
  28.7 4.1 %collective-permute-start.1 = (bf16[6,1,16,256]{3,2,1,0:T(8,128)(2,1)}, bf16[6,1,16,256]{3,2,1,0:T(8,128)(2,1)}, u32[]{:S(2)}, u32[]{:S(2)}) collective-permute-start(bf16[6,1,16,256]{3,2,1,0:T(8,128)(2,1)} %get-tuple-element.38), channel_id=1, source_target_pairs={{0,4},{4,8},{8,12},{12,16},{16,20},{20,24},{24,28},{1,5},{5,9},{9,... | collective-permute-start | bytes 147464 | tf_op jit(solution)/shard_map/ppermute | solution.py:25
  39.4 4.2 %collective-permute-start.3 = (bf16[6,18,1,256]{3,2,1,0:T(2,128)(2,1)S(1)}, bf16[6,18,1,256]{3,2,1,0:T(2,128)(2,1)S(1)}, u32[]{:S(2)}, u32[]{:S(2)}) collective-permute-start(bf16[6,18,1,256]{3,2,1,0:T(2,128)(2,1)S(1)} %get-tuple-element.29), channel_id=1, source_target_pairs={{0,1},{1,2},{2,3},{4,5},{5,6},{6,7},{8,9},{9,10},{10,11},{12,13},{... | collective-permute-start | bytes 165896 | tf_op jit(solution)/shard_map/ppermute | solution.py:25
  47.9 4.6 %reshape.109 = bf16[6,18,1,8,3,256]{5,4,3,1,0,2:T(4,128)(2,1)} reshape(bf16[6,18,1,24,256]{4,3,1,0,2:T(8,128)(2,1)} %pad) | data formatting | bytes 2654208 | tf_op jit(solution)/shard_map/conv_general_dilated | solution.py:55
  57.4 7.9 %add_divide_fusion = (f32[4,16,8,3,256]{4,2,3,1,0:T(8,128)}, f32[4,16,8,3,256]{4,2,3,1,0:T(8,128)}, f32[4,16,8,3,256]{4,2,3,1,0:T(8,128)S(1)}) fusion(f32[256]{0:T(256)S(1)} %copy-done.31, bf16[3,3,3,256,256]{4,3,2,1,0:T(8,128)(2,1)S(1)} %copy-done, bf16[6,18,1,7,2,256]{5,3,4,1,0,2:T(8,128)(2,1)S(1)} %slice.211, ...), kind=kOutput, calls=%fused_computation.48 | convolution fusion | flops 5445599232 | bytes 10359832 | tf_op jit(solution)/shard_map/conv_general_dilated | solution.py:55
  68.8 4.0 %collective-permute-start.11 = (bf16[6,1,16,256]{3,2,1,0:T(8,128)(2,1)S(1)}, bf16[6,1,16,256]{3,2,1,0:T(8,128)(2,1)S(1)}, u32[]{:S(2)}, u32[]{:S(2)}) collective-permute-start(bf16[6,1,16,256]{3,2,1,0:T(8,128)(2,1)S(1)} %get-tuple-element.33), channel_id=1, source_target_pairs={{0,4},{4,8},{8,12},{12,16},{16,20},{20,24},{24,28},{1,5},{5,9},{9,... | collective-permute-start | bytes 147464 | tf_op jit(solution)/shard_map/ppermute | solution.py:25
  76.1 5.6 %collective-permute-start.13 = (bf16[6,18,1,256]{3,2,1,0:T(2,128)(2,1)}, bf16[6,18,1,256]{3,2,1,0:T(2,128)(2,1)}, u32[]{:S(2)}, u32[]{:S(2)}) collective-permute-start(bf16[6,18,1,256]{3,2,1,0:T(2,128)(2,1)} %get-tuple-element.25), channel_id=1, source_target_pairs={{0,1},{1,2},{2,3},{4,5},{5,6},{6,7},{8,9},{9,10},{10,11},{12,13},{... | collective-permute-start | bytes 165896 | tf_op jit(solution)/shard_map/ppermute | solution.py:25
  81.7 5.2 %slice_bitcast_fusion.2 = (bf16[2304,4,16,16]{0,3,2,1:T(8,128)(2,1)}, bf16[2304,4,16,16]{0,3,2,1:T(8,128)(2,1)}, bf16[2304,4,16,16]{0,3,2,1:T(8,128)(2,1)}) fusion(bf16[6,16,16,2304]{3,2,1,0:T(8,128)(2,1)S(1)} %fusion.96), kind=kLoop, calls=%fused_computation.4 | loop fusion | bytes 28311552 | tf_op jit(solution)/shard_map/dot_general | solution.py:75
  88.4 11.2 %reshape.106 = bf16[3,3,256,4,16,16]{2,1,0,5,4,3:T(4,128)(2,1)} reshape(bf16[2304,4,16,16]{0,3,2,1:T(8,128)(2,1)} %get-tuple-element.15) | data formatting | bytes 9437184 | tf_op jit(solution)/shard_map/reshape.38
  104.3 11.2 %reshape.105 = bf16[3,3,256,4,16,16]{2,1,0,5,4,3:T(4,128)(2,1)} reshape(bf16[2304,4,16,16]{0,3,2,1:T(8,128)(2,1)} %get-tuple-element.16) | data formatting | bytes 9437184 | tf_op jit(solution)/shard_map/reshape.36
  115.6 11.2 %reshape.104 = bf16[3,3,256,4,16,16]{2,1,0,5,4,3:T(4,128)(2,1)} reshape(bf16[2304,4,16,16]{0,3,2,1:T(8,128)(2,1)} %get-tuple-element.14) | data formatting | bytes 9437184 | tf_op jit(solution)/shard_map/reshape.34
  130.2 4.7 %reshape.123 = bf16[6,18,1,8,3,256]{5,4,3,1,0,2:T(4,128)(2,1)} reshape(bf16[6,18,1,24,256]{4,3,1,0,2:T(8,128)(2,1)} %pad.4) | data formatting | bytes 2654208 | tf_op jit(solution)/shard_map/conv_general_dilated | solution.py:55
  137.4 5.9 %fusion.53 = f32[4,16,8,3,256]{4,2,3,1,0:T(8,128)S(1)} fusion(bf16[3,3,3,256,256]{4,3,2,1,0:T(8,128)(2,1)S(1)} %copy-done.33, bf16[6,18,1,7,2,256]{5,3,4,1,0,2:T(8,128)(2,1)S(1)} %slice.222, bf16[6,18,1,8,3,256]{5,3,4,1,0,2:T(8,128)(2,1)S(1)} %copy.45, pred[8,3]{0,1:T(4,128)(4,1)S(1)} %copy-done.36), kind=kOutput, calls=%fused_computation.57 | convolution fusion | flops 5442846720 | bytes 7213080 | tf_op jit(solution)/shard_map/conv_general_dilated | solution.py:55
  144.5 4.0 %fusion.66 = (bf16[4,16,16,256]{3,2,1,0:T(8,128)(2,1)}, bf16[4,16,16,256]{3,2,1,0:T(8,128)(2,1)S(1)}) fusion(f32[4,16,1,16,256]{4,1,3,0,2:T(8,128)S(1)} %slice.223, f32[4,16,1,16,256]{4,1,3,0,2:T(8,128)S(1)} %copy-done.12, s32[]{:T(128)} %bitcast.7, s32[]{:T(128)} %bitcast.6, s32[16]{0:T(128)S(1)} %get-tuple-element.42, s32[16]{0:T(128)S(1)} %get-tuple-element.43, ...), kind=kLoop, calls=%fused_computation.81 | loop fusion | flops 8650752 | bytes 3146904 | tf_op jit(solution)/shard_map/convert_element_type | solution.py:126
  148.5 7.8 %collective-permute-start.5 = (bf16[2,16,16,256]{3,2,1,0:T(8,128)(2,1)S(1)}, bf16[2,16,16,256]{3,2,1,0:T(8,128)(2,1)S(1)}, u32[]{:S(2)}, u32[]{:S(2)}) collective-permute-start(bf16[2,16,16,256]{3,2,1,0:T(8,128)(2,1)S(1)} %slice.213), channel_id=1, source_target_pairs={{0,32},{32,64},{64,96},{1,33},{33,65},{65,97},{2,34},{34,66},{66,9... | collective-permute-start | bytes 786440 | tf_op jit(solution)/shard_map/ppermute | solution.py:14
  156.4 4.5 %fusion.82 = bf16[1,4,16,16,256]{4,3,2,1,0:T(8,128)(2,1)S(1)} fusion(f32[4,16,1,16,256]{4,1,3,0,2:T(8,128)S(1)} %copy-done.10, f32[4,16,1,16,256]{4,1,3,0,2:T(8,128)S(1)} %copy-done.11, f32[4,16,1,16,256]{4,1,3,0,2:T(8,128)S(1)} %slice.223, s32[]{:T(128)} %bitcast.7, s32[]{:T(128)} %bitcast.6, s32[16]{0:T(128)S(1)} %get-tuple-element.42, ...), kind=kLoop, calls=%fused_computation.100 | loop fusion | flops 6029312 | bytes 3670168 | tf_op jit(solution)/shard_map/convert_element_type | solution.py:126
  165.4 4.6 %collective-permute-start.6 = (bf16[6,1,16,256]{3,2,1,0:T(8,128)(2,1)S(1)}, bf16[6,1,16,256]{3,2,1,0:T(8,128)(2,1)S(1)}, u32[]{:S(2)}, u32[]{:S(2)}) collective-permute-start(bf16[6,1,16,256]{3,2,1,0:T(8,128)(2,1)S(1)} %get-tuple-element.35), channel_id=1, source_target_pairs={{0,4},{4,8},{8,12},{12,16},{16,20},{20,24},{24,28},{1,5},{5,9},{9,... | collective-permute-start | bytes 147464 | tf_op jit(solution)/shard_map/ppermute | solution.py:25
  173.1 4.2 %collective-permute-start.8 = (bf16[6,18,1,256]{3,2,1,0:T(2,128)(2,1)S(1)}, bf16[6,18,1,256]{3,2,1,0:T(2,128)(2,1)S(1)}, u32[]{:S(2)}, u32[]{:S(2)}) collective-permute-start(bf16[6,18,1,256]{3,2,1,0:T(2,128)(2,1)S(1)} %get-tuple-element.27), channel_id=1, source_target_pairs={{0,1},{1,2},{2,3},{4,5},{5,6},{6,7},{8,9},{9,10},{10,11},{12,13},{... | collective-permute-start | bytes 165896 | tf_op jit(solution)/shard_map/ppermute | solution.py:25
  177.3 3.4 pad_maximum_fusion
  188.3 3.4 pad_maximum_fusion.1
  194.6 7.3 %collective-permute-done.15 = bf16[2,16,16,256]{3,2,1,0:T(8,128)(2,1)S(1)} collective-permute-done((bf16[2,16,16,256]{3,2,1,0:T(8,128)(2,1)S(1)}, bf16[2,16,16,256]{3,2,1,0:T(8,128)(2,1)S(1)}, u32[]{:S(2)}, u32[]{:S(2)}) %collective-permute-start.15) | collective-permute-done | bytes 262176 | tf_op jit(solution)/shard_map/ppermute | solution.py:14
  205.3 4.6 %collective-permute-start.16 = (bf16[6,1,16,256]{3,2,1,0:T(8,128)(2,1)}, bf16[6,1,16,256]{3,2,1,0:T(8,128)(2,1)}, u32[]{:S(2)}, u32[]{:S(2)}) collective-permute-start(bf16[6,1,16,256]{3,2,1,0:T(8,128)(2,1)} %get-tuple-element.31), channel_id=1, source_target_pairs={{0,4},{4,8},{8,12},{12,16},{16,20},{20,24},{24,28},{1,5},{5,9},{9,... | collective-permute-start | bytes 147464 | tf_op jit(solution)/shard_map/ppermute | solution.py:25
  217.6 4.9 %collective-permute-start.18 = (bf16[6,18,1,256]{3,2,1,0:T(2,128)(2,1)}, bf16[6,18,1,256]{3,2,1,0:T(2,128)(2,1)}, u32[]{:S(2)}, u32[]{:S(2)}) collective-permute-start(bf16[6,18,1,256]{3,2,1,0:T(2,128)(2,1)} %get-tuple-element.23), channel_id=1, source_target_pairs={{0,1},{1,2},{2,3},{4,5},{5,6},{6,7},{8,9},{9,10},{10,11},{12,13},{... | collective-permute-start | bytes 165896 | tf_op jit(solution)/shard_map/ppermute | solution.py:25
  225.9 4.7 %reshape.116 = bf16[6,18,1,8,3,256]{5,4,3,1,0,2:T(4,128)(2,1)} reshape(bf16[6,18,1,24,256]{4,3,1,0,2:T(8,128)(2,1)} %pad.2) | data formatting | bytes 2654208 | tf_op jit(solution)/shard_map/conv_general_dilated | solution.py:55
  233.3 6.3 %fusion.50 = f32[4,16,8,3,256]{4,2,3,1,0:T(8,128)S(1)} fusion(bf16[3,3,3,256,256]{4,3,2,1,0:T(8,128)(2,1)S(1)} %copy-done.34, bf16[6,18,1,7,2,256]{5,3,4,1,0,2:T(8,128)(2,1)S(1)} %slice.218, bf16[6,18,1,8,3,256]{5,3,4,1,0,2:T(8,128)(2,1)S(1)} %copy.41, pred[8,3]{0,1:T(4,128)(4,1)S(1)} %copy-done.37), kind=kOutput, calls=%fused_computation.56 | convolution fusion | flops 5442846720 | bytes 7213080 | tf_op jit(solution)/shard_map/conv_general_dilated | solution.py:55
  245.2 4.9 %reshape.130 = bf16[6,18,1,8,3,256]{5,4,3,1,0,2:T(4,128)(2,1)} reshape(bf16[6,18,1,24,256]{4,3,1,0,2:T(8,128)(2,1)} %pad.6) | data formatting | bytes 2654208 | tf_op jit(solution)/shard_map/conv_general_dilated | solution.py:55
  252.4 5.9 %fusion.47 = f32[4,16,8,3,256]{4,2,3,1,0:T(8,128)S(1)} fusion(bf16[3,3,3,256,256]{4,3,2,1,0:T(8,128)(2,1)S(1)} %copy-done, bf16[6,18,1,7,2,256]{5,3,4,1,0,2:T(8,128)(2,1)S(1)} %slice.225, bf16[6,18,1,8,3,256]{5,3,4,1,0,2:T(8,128)(2,1)S(1)} %copy.49, pred[8,3]{0,1:T(4,128)(4,1)S(1)} %copy-done.37), kind=kOutput, calls=%fused_computation.55 | convolution fusion | flops 5442846720 | bytes 7213080 | tf_op jit(solution)/shard_map/conv_general_dilated | solution.py:55
  267.7 104.0 %all-reduce.3.cloned.1.call-done = (f32[3,3,3,256,256]{4,3,2,1,0:T(8,128)}, f32[3,3,3,256,256]{4,3,2,1,0:T(8,128)}) async-done(((f32[3,3,3,256,256]{4,3,2,1,0:T(8,128)}, f32[3,3,3,256,256]{4,3,2,1,0:T(8,128)}), (f32[3,3,3,256,256]{4,3,2,1,0:T(8,128)}, f32[3,3,3,256,256]{4,3,2,1,0:T(8,128)})) %all-reduce.3.cloned.1.call-update) | async-done | bytes 14155792 | tf_op jit(solution)/shard_map/psum | solution.py:138
  371.7 6.9 %copy.124 = f32[3,3,3,256,256]{4,3,2,1,0:T(8,128)} copy(f32[3,3,3,256,256]{4,3,2,1,0:T(8,128)} %get-tuple-element.46) | data formatting | bytes 14155776
  378.6 3.0 copy.125
  (205 shorter events, 98.2 us)
Async XLA Ops:
  7.2 50.2 %copy-start = (bf16[3,3,3,256,256]{4,3,2,1,0:T(8,128)(2,1)S(1)}, bf16[3,3,3,256,256]{4,3,2,1,0:T(8,128)(2,1)}, u32[]{:S(2)}) copy-start(bf16[3,3,3,256,256]{4,3,2,1,0:T(8,128)(2,1)} %param.8) | copy-start | bytes 10616836
  7.2 364.5 %all-reduce.3.cloned.1.call-start = ((), (), s32[]{:S(2)}) async-start(), calls=%async_computation | async-start | bytes 28311552 | tf_op jit(solution)/shard_map/psum | solution.py:138
  9.0 57.2 %collective-permute-start.10 = (bf16[2,16,16,256]{3,2,1,0:T(8,128)(2,1)}, bf16[2,16,16,256]{3,2,1,0:T(8,128)(2,1)}, u32[]{:S(2)}, u32[]{:S(2)}) collective-permute-start(bf16[2,16,16,256]{3,2,1,0:T(8,128)(2,1)} %slice.165), channel_id=1, source_target_pairs={{32,0},{64,32},{96,64},{33,1},{65,33},{97,65},{34,2},{66,34},{98,6... | collective-permute-start | bytes 786440 | tf_op jit(solution)/shard_map/ppermute | solution.py:14
  13.8 8.1 %collective-permute-start = (bf16[2,8,8,256]{3,2,1,0:T(8,128)(2,1)}, bf16[2,8,8,256]{3,2,1,0:T(8,128)(2,1)}, u32[]{:S(2)}, u32[]{:S(2)}) collective-permute-start(bf16[2,8,8,256]{3,2,1,0:T(8,128)(2,1)} %slice.153), channel_id=1, source_target_pairs={{0,32},{32,64},{64,96},{1,33},{33,65},{65,97},{2,34},{34,66},{66,9... | collective-permute-start | bytes 196616 | tf_op jit(solution)/shard_map/ppermute | solution.py:14
  28.7 5.4 %collective-permute-start.1 = (bf16[6,1,16,256]{3,2,1,0:T(8,128)(2,1)}, bf16[6,1,16,256]{3,2,1,0:T(8,128)(2,1)}, u32[]{:S(2)}, u32[]{:S(2)}) collective-permute-start(bf16[6,1,16,256]{3,2,1,0:T(8,128)(2,1)} %get-tuple-element.38), channel_id=1, source_target_pairs={{0,4},{4,8},{8,12},{12,16},{16,20},{20,24},{24,28},{1,5},{5,9},{9,... | collective-permute-start | bytes 147464 | tf_op jit(solution)/shard_map/ppermute | solution.py:25
  32.9 5.0 %collective-permute-start.2 = (bf16[6,1,16,256]{3,2,1,0:T(8,128)(2,1)}, bf16[6,1,16,256]{3,2,1,0:T(8,128)(2,1)S(1)}, u32[]{:S(2)}, u32[]{:S(2)}) collective-permute-start(bf16[6,1,16,256]{3,2,1,0:T(8,128)(2,1)} %get-tuple-element.37), channel_id=1, source_target_pairs={{4,0},{8,4},{12,8},{16,12},{20,16},{24,20},{28,24},{5,1},{9,5},{13... | collective-permute-start | bytes 147464 | tf_op jit(solution)/shard_map/ppermute | solution.py:27
  37.9 7.9 %copy-start.1 = (bf16[6,18,16,256]{3,2,1,0:T(8,128)(2,1)}, bf16[6,18,16,256]{3,2,1,0:T(8,128)(2,1)S(1)}, u32[]{:S(2)}) copy-start(bf16[6,18,16,256]{3,2,1,0:T(8,128)(2,1)S(1)} %constant_dynamic-update-slice_fusion) | copy-start | bytes 2654212
  38.1 6.8 %collective-permute-start.4 = (bf16[6,18,1,256]{3,2,1,0:T(2,128)(2,1)S(1)}, bf16[6,18,1,256]{3,2,1,0:T(2,128)(2,1)S(1)}, u32[]{:S(2)}, u32[]{:S(2)}) collective-permute-start(bf16[6,18,1,256]{3,2,1,0:T(2,128)(2,1)S(1)} %get-tuple-element.30), channel_id=1, source_target_pairs={{1,0},{2,1},{3,2},{5,4},{6,5},{7,6},{9,8},{10,9},{11,10},{13,12},{... | collective-permute-start | bytes 165896 | tf_op jit(solution)/shard_map/ppermute | solution.py:27
  39.4 6.4 %collective-permute-start.3 = (bf16[6,18,1,256]{3,2,1,0:T(2,128)(2,1)S(1)}, bf16[6,18,1,256]{3,2,1,0:T(2,128)(2,1)S(1)}, u32[]{:S(2)}, u32[]{:S(2)}) collective-permute-start(bf16[6,18,1,256]{3,2,1,0:T(2,128)(2,1)S(1)} %get-tuple-element.29), channel_id=1, source_target_pairs={{0,1},{1,2},{2,3},{4,5},{5,6},{6,7},{8,9},{9,10},{10,11},{12,13},{... | collective-permute-start | bytes 165896 | tf_op jit(solution)/shard_map/ppermute | solution.py:25
  67.5 5.8 %collective-permute-start.12 = (bf16[6,1,16,256]{3,2,1,0:T(8,128)(2,1)S(1)}, bf16[6,1,16,256]{3,2,1,0:T(8,128)(2,1)S(1)}, u32[]{:S(2)}, u32[]{:S(2)}) collective-permute-start(bf16[6,1,16,256]{3,2,1,0:T(8,128)(2,1)S(1)} %get-tuple-element.34), channel_id=1, source_target_pairs={{4,0},{8,4},{12,8},{16,12},{20,16},{24,20},{28,24},{5,1},{9,5},{13... | collective-permute-start | bytes 147464 | tf_op jit(solution)/shard_map/ppermute | solution.py:27
  68.8 5.2 %collective-permute-start.11 = (bf16[6,1,16,256]{3,2,1,0:T(8,128)(2,1)S(1)}, bf16[6,1,16,256]{3,2,1,0:T(8,128)(2,1)S(1)}, u32[]{:S(2)}, u32[]{:S(2)}) collective-permute-start(bf16[6,1,16,256]{3,2,1,0:T(8,128)(2,1)S(1)} %get-tuple-element.33), channel_id=1, source_target_pairs={{0,4},{4,8},{8,12},{12,16},{16,20},{20,24},{24,28},{1,5},{5,9},{9,... | collective-permute-start | bytes 147464 | tf_op jit(solution)/shard_map/ppermute | solution.py:25
  74.8 52.0 %collective-permute-start.14 = (bf16[6,18,1,256]{3,2,1,0:T(2,128)(2,1)}, bf16[6,18,1,256]{3,2,1,0:T(2,128)(2,1)}, u32[]{:S(2)}, u32[]{:S(2)}) collective-permute-start(bf16[6,18,1,256]{3,2,1,0:T(2,128)(2,1)} %get-tuple-element.26), channel_id=1, source_target_pairs={{1,0},{2,1},{3,2},{5,4},{6,5},{7,6},{9,8},{10,9},{11,10},{13,12},{... | collective-permute-start | bytes 165896 | tf_op jit(solution)/shard_map/ppermute | solution.py:27
  76.1 50.8 %collective-permute-start.13 = (bf16[6,18,1,256]{3,2,1,0:T(2,128)(2,1)}, bf16[6,18,1,256]{3,2,1,0:T(2,128)(2,1)}, u32[]{:S(2)}, u32[]{:S(2)}) collective-permute-start(bf16[6,18,1,256]{3,2,1,0:T(2,128)(2,1)} %get-tuple-element.25), channel_id=1, source_target_pairs={{0,1},{1,2},{2,3},{4,5},{5,6},{6,7},{8,9},{9,10},{10,11},{12,13},{... | collective-permute-start | bytes 165896 | tf_op jit(solution)/shard_map/ppermute | solution.py:25
  136.8 24.0 %slice-start.2 = ((s8[6291456]{0:T(1024)(128)(4,1)}), s8[4194304]{0:T(1024)(128)(4,1)S(1)}, s32[]{:S(2)}) async-start(s8[6291456]{0:T(1024)(128)(4,1)} %bitcast.174), calls=%async_computation.3 | async-start | bytes 8388608
  137.4 23.5 %slice-start.3 = ((s8[6291456]{0:T(1024)(128)(4,1)}), s8[2097152]{0:T(1024)(128)(4,1)S(1)}, s32[]{:S(2)}) async-start(s8[6291456]{0:T(1024)(128)(4,1)} %bitcast.174), calls=%async_computation.4 | async-start | bytes 4194304
  143.8 12.5 %copy-start.10 = (f32[4,16,1,16,256]{4,1,3,0,2:T(8,128)S(1)}, f32[4,16,1,16,256]{4,1,3,0,2:T(8,128)}, u32[]{:S(2)}) copy-start(f32[4,16,1,16,256]{4,1,3,0,2:T(8,128)} %slice.237) | copy-start | bytes 3145732
  143.8 12.5 %copy-start.11 = (f32[4,16,1,16,256]{4,1,3,0,2:T(8,128)S(1)}, f32[4,16,1,16,256]{4,1,3,0,2:T(8,128)}, u32[]{:S(2)}) copy-start(f32[4,16,1,16,256]{4,1,3,0,2:T(8,128)} %slice.236) | copy-start | bytes 3145732
  148.5 34.3 %copy-start.3 = (bf16[4,16,16,256]{3,2,1,0:T(8,128)(2,1)}, bf16[4,16,16,256]{3,2,1,0:T(8,128)(2,1)S(1)}, u32[]{:S(2)}) copy-start(bf16[4,16,16,256]{3,2,1,0:T(8,128)(2,1)S(1)} %get-tuple-element.20) | copy-start | bytes 1572868
  148.5 15.6 %collective-permute-start.5 = (bf16[2,16,16,256]{3,2,1,0:T(8,128)(2,1)S(1)}, bf16[2,16,16,256]{3,2,1,0:T(8,128)(2,1)S(1)}, u32[]{:S(2)}, u32[]{:S(2)}) collective-permute-start(bf16[2,16,16,256]{3,2,1,0:T(8,128)(2,1)S(1)} %slice.213), channel_id=1, source_target_pairs={{0,32},{32,64},{64,96},{1,33},{33,65},{65,97},{2,34},{34,66},{66,9... | collective-permute-start | bytes 786440 | tf_op jit(solution)/shard_map/ppermute | solution.py:14
  160.9 9.1 %slice-start = ((s8[6291456]{0:T(1024)(128)(4,1)}), s8[4194304]{0:T(1024)(128)(4,1)S(1)}, s32[]{:S(2)}) async-start(s8[6291456]{0:T(1024)(128)(4,1)} %bitcast.172), calls=%async_computation.1 | async-start | bytes 8388608
  164.1 18.7 %copy-start.5 = (bf16[2,16,16,256]{3,2,1,0:T(8,128)(2,1)}, bf16[2,16,16,256]{3,2,1,0:T(8,128)(2,1)S(1)}, u32[]{:S(2)}) copy-start(bf16[2,16,16,256]{3,2,1,0:T(8,128)(2,1)S(1)} %collective-permute-done.5) | copy-start | bytes 786436
  164.1 7.5 %collective-permute-start.7 = (bf16[6,1,16,256]{3,2,1,0:T(8,128)(2,1)S(1)}, bf16[6,1,16,256]{3,2,1,0:T(8,128)(2,1)S(1)}, u32[]{:S(2)}, u32[]{:S(2)}) collective-permute-start(bf16[6,1,16,256]{3,2,1,0:T(8,128)(2,1)S(1)} %get-tuple-element.36), channel_id=1, source_target_pairs={{4,0},{8,4},{12,8},{16,12},{20,16},{24,20},{28,24},{5,1},{9,5},{13... | collective-permute-start | bytes 147464 | tf_op jit(solution)/shard_map/ppermute | solution.py:27
  165.4 6.2 %collective-permute-start.6 = (bf16[6,1,16,256]{3,2,1,0:T(8,128)(2,1)S(1)}, bf16[6,1,16,256]{3,2,1,0:T(8,128)(2,1)S(1)}, u32[]{:S(2)}, u32[]{:S(2)}) collective-permute-start(bf16[6,1,16,256]{3,2,1,0:T(8,128)(2,1)S(1)} %get-tuple-element.35), channel_id=1, source_target_pairs={{0,4},{4,8},{8,12},{12,16},{16,20},{20,24},{24,28},{1,5},{5,9},{9,... | collective-permute-start | bytes 147464 | tf_op jit(solution)/shard_map/ppermute | solution.py:25
  171.6 11.2 %copy-start.23 = (bf16[6,1,16,256]{3,2,1,0:T(8,128)(2,1)}, bf16[6,1,16,256]{3,2,1,0:T(8,128)(2,1)S(1)}, u32[]{:S(2)}) copy-start(bf16[6,1,16,256]{3,2,1,0:T(8,128)(2,1)S(1)} %collective-permute-done.7) | copy-start | bytes 147460
  171.6 10.2 %copy-start.24 = (bf16[6,1,16,256]{3,2,1,0:T(8,128)(2,1)}, bf16[6,1,16,256]{3,2,1,0:T(8,128)(2,1)S(1)}, u32[]{:S(2)}) copy-start(bf16[6,1,16,256]{3,2,1,0:T(8,128)(2,1)S(1)} %collective-permute-done.6) | copy-start | bytes 147460
  171.8 8.9 %collective-permute-start.9 = (bf16[6,18,1,256]{3,2,1,0:T(2,128)(2,1)S(1)}, bf16[6,18,1,256]{3,2,1,0:T(2,128)(2,1)S(1)}, u32[]{:S(2)}, u32[]{:S(2)}) collective-permute-start(bf16[6,18,1,256]{3,2,1,0:T(2,128)(2,1)S(1)} %get-tuple-element.28), channel_id=1, source_target_pairs={{1,0},{2,1},{3,2},{5,4},{6,5},{7,6},{9,8},{10,9},{11,10},{13,12},{... | collective-permute-start | bytes 165896 | tf_op jit(solution)/shard_map/ppermute | solution.py:27
  173.1 7.6 %collective-permute-start.8 = (bf16[6,18,1,256]{3,2,1,0:T(2,128)(2,1)S(1)}, bf16[6,18,1,256]{3,2,1,0:T(2,128)(2,1)S(1)}, u32[]{:S(2)}, u32[]{:S(2)}) collective-permute-start(bf16[6,18,1,256]{3,2,1,0:T(2,128)(2,1)S(1)} %get-tuple-element.27), channel_id=1, source_target_pairs={{0,1},{1,2},{2,3},{4,5},{5,6},{6,7},{8,9},{9,10},{10,11},{12,13},{... | collective-permute-start | bytes 165896 | tf_op jit(solution)/shard_map/ppermute | solution.py:25
  192.7 9.2 %collective-permute-start.15 = (bf16[2,16,16,256]{3,2,1,0:T(8,128)(2,1)S(1)}, bf16[2,16,16,256]{3,2,1,0:T(8,128)(2,1)S(1)}, u32[]{:S(2)}, u32[]{:S(2)}) collective-permute-start(bf16[2,16,16,256]{3,2,1,0:T(8,128)(2,1)S(1)} %slice.224), channel_id=1, source_target_pairs={{32,0},{64,32},{96,64},{33,1},{65,33},{97,65},{34,2},{66,34},{98,6... | collective-permute-start | bytes 786440 | tf_op jit(solution)/shard_map/ppermute | solution.py:14
  204.1 10.2 %collective-permute-start.17 = (bf16[6,1,16,256]{3,2,1,0:T(8,128)(2,1)}, bf16[6,1,16,256]{3,2,1,0:T(8,128)(2,1)}, u32[]{:S(2)}, u32[]{:S(2)}) collective-permute-start(bf16[6,1,16,256]{3,2,1,0:T(8,128)(2,1)} %get-tuple-element.32), channel_id=1, source_target_pairs={{4,0},{8,4},{12,8},{16,12},{20,16},{24,20},{28,24},{5,1},{9,5},{13... | collective-permute-start | bytes 147464 | tf_op jit(solution)/shard_map/ppermute | solution.py:27
  205.3 8.9 %collective-permute-start.16 = (bf16[6,1,16,256]{3,2,1,0:T(8,128)(2,1)}, bf16[6,1,16,256]{3,2,1,0:T(8,128)(2,1)}, u32[]{:S(2)}, u32[]{:S(2)}) collective-permute-start(bf16[6,1,16,256]{3,2,1,0:T(8,128)(2,1)} %get-tuple-element.31), channel_id=1, source_target_pairs={{0,4},{4,8},{8,12},{12,16},{16,20},{20,24},{24,28},{1,5},{5,9},{9,... | collective-permute-start | bytes 147464 | tf_op jit(solution)/shard_map/ppermute | solution.py:25
  216.4 25.7 %collective-permute-start.19 = (bf16[6,18,1,256]{3,2,1,0:T(2,128)(2,1)}, bf16[6,18,1,256]{3,2,1,0:T(2,128)(2,1)}, u32[]{:S(2)}, u32[]{:S(2)}) collective-permute-start(bf16[6,18,1,256]{3,2,1,0:T(2,128)(2,1)} %get-tuple-element.24), channel_id=1, source_target_pairs={{1,0},{2,1},{3,2},{5,4},{6,5},{7,6},{9,8},{10,9},{11,10},{13,12},{... | collective-permute-start | bytes 165896 | tf_op jit(solution)/shard_map/ppermute | solution.py:27
  217.6 24.4 %collective-permute-start.18 = (bf16[6,18,1,256]{3,2,1,0:T(2,128)(2,1)}, bf16[6,18,1,256]{3,2,1,0:T(2,128)(2,1)}, u32[]{:S(2)}, u32[]{:S(2)}) collective-permute-start(bf16[6,18,1,256]{3,2,1,0:T(2,128)(2,1)} %get-tuple-element.23), channel_id=1, source_target_pairs={{0,1},{1,2},{2,3},{4,5},{5,6},{6,7},{8,9},{9,10},{10,11},{12,13},{... | collective-permute-start | bytes 165896 | tf_op jit(solution)/shard_map/ppermute | solution.py:25
  (33 other events, 76.8 us)
Sparse Core Ops, SparseCore 0:
  191.8 179.7 all-reduce.2

commit v5 on v3

--- a/solution.py
+++ b/solution.py
@@ -93,6 +93,28 @@
     return extended_2(field, (("row", 1), ("col", 2)), 1)
 
 
+def faces_together(fields):
+    for axis, dim, other in (("row", 1, 2), ("col", 2, 1)):
+        ends = lax.axis_size(axis) - 1
+        head = jnp.concatenate([lax.slice_in_dim(f, 0, 1, axis=dim) for f in fields], axis=other)
+        tail = jnp.concatenate(
+            [lax.slice_in_dim(f, f.shape[dim] - 1, f.shape[dim], axis=dim) for f in fields],
+            axis=other,
+        )
+        from_prev = lax.ppermute(tail, axis, [(i, i + 1) for i in range(ends)])
+        from_next = lax.ppermute(head, axis, [(i + 1, i) for i in range(ends)])
+        placed = []
+        start = 0
+        for f in fields:
+            size = f.shape[other]
+            before = lax.slice_in_dim(from_prev, start, start + size, axis=other)
+            after = lax.slice_in_dim(from_next, start, start + size, axis=other)
+            placed.append(jnp.concatenate([before, f, after], axis=dim))
+            start += size
+        fields = placed
+    return fields
+
+
 def local(latent, w_first, b_first, w_second, b_second, upstream, dropout_key):
     frames_here, low_rows, low_cols, channels = latent.shape
     high_rows = 2 * low_rows
@@ -103,8 +125,8 @@
     col_start = lax.axis_index("col") * high_cols
     height_all = high_rows * lax.axis_size("row")
     width_all = high_cols * lax.axis_size("col")
-    latent_ext = with_earlier(latent)
-    cells_ext = face_cells(upsample(latent_ext))
+    latent_ext, upstream_ext = faces_together([with_earlier(latent), with_later(upstream)])
+    cells_ext = upsample(latent_ext)[:, 1:-1, 1:-1]
     cells_here = cells_ext[2:, 1:-1, 1:-1]
     pre_first = convolve(cells_ext, w_first) + b_first
     scaling = keep_mask(
@@ -116,7 +138,7 @@
     mixed = (cells_here.astype(jnp.float32) + convolve(dropped_ext, w_second) + b_second).astype(
         jnp.bfloat16
     )
-    grad_dropped = convolve(face_cells(with_later(upstream)), flipped(w_second))
+    grad_dropped = convolve(upstream_ext, flipped(w_second))
     sigma = jax.nn.sigmoid(pre_first)
     grad_pre = (grad_dropped * scaling * sigma * (1.0 + pre_first * (1.0 - sigma))).astype(
         jnp.bfloat16

time: 370 us -> 353 us (0.954)
  starting transfers between devices: 62.9 us -> 48.8 us
  waiting for transfers between devices: 134 us -> 147 us
  local copies, waits for them, and re-layouts: 63 us -> 52.5 us
    ppermute x8 -> x4, starting transfers between devices: 34 us -> 17.7 us  [extended_2(): lax.ppermute(tail, axis, [(i, (i + 1) % count) for i in range(ends)])]
    ppermute x0 -> x4, starting transfers between devices: none -> 10.7 us  [the longest x2 8.17 us: faces_together(): from_prev = lax.ppermute(tail, axis, [(i, i + 1) for i in range(ends)])]
    conv_general_dilated x14 -> x13, local copies, waits for them, and re-layouts: 17.8 us -> 10.7 us  [convolve(): lax.conv_general_dilated(extended[None], weight, (1, 1, 1), 'VALID', dime...]
    ppermute x8 -> x4, starting transfers between devices: 11 us -> 5.56 us  [extended_2(): lax.ppermute(head, axis, [((i + 1) % count, i) for i in range(ends)])]
    psum x1, waiting for transfers between devices: 113 us -> 117 us  [local(): grad_first, grad_second = lax.psum((grad_first, grad_second), ALL)]
    ppermute x8 -> x4, waiting for transfers between devices: 9.45 us -> 13.1 us  [extended_2(): lax.ppermute(head, axis, [((i + 1) % count, i) for i in range(ends)])]
    broadcast_in_dim x4 -> x3, other arithmetic: 8.66 us -> 5.86 us  [convolve(): extended[None]]
    unnamed x65 -> x52, local copies, waits for them, and re-layouts: 19.6 us -> 19.3 us
  transfers between devices with their start and end apart: 21 -> 17, of which waited for: 8 -> 10; matrix products, arithmetic and copies ran while one was open for 25% -> 17% of each run, Pallas kernels for 0% -> 0%
where the time goes in v5:
time: 353 us; the launch traced here: 348 us
  waiting for transfers between devices  147 us (42%)
  matrix products  62.8 us (18%)
  local copies, waits for them, and re-layouts  52.5 us (15%)
  starting transfers between devices  48.8 us (14%)
  other arithmetic  21.5 us (6%)
  between operations  14.9 us (4%)
    psum x1, waiting for transfers between devices, local(): grad_first, grad_second = lax.psum((grad_first, grad_second), ALL)  117 us
    transpose x2, matrix products, weight_gradient(): return jnp.transpose(summed, (1, 2, 3, 0, 4))  38.2 us
    conv_general_dilated x4, matrix products, convolve(): lax.conv_general_dilated(extended[None], weight, (1, 1, 1), 'VALID', dime...  24.5 us
    unnamed x52, local copies, waits for them, and re-layouts  19.3 us
    ppermute x4, starting transfers between devices, extended_2(): lax.ppermute(tail, axis, [(i, (i + 1) % count) for i in range(ends)])  17.7 us
    ppermute x4, starting transfers between devices, shifted(): return lax.ppermute(block, axis, route)  14.7 us
    ppermute x4, waiting for transfers between devices, shifted(): return lax.ppermute(block, axis, route)  14.4 us
    ppermute x4, waiting for transfers between devices, extended_2(): lax.ppermute(head, axis, [((i + 1) % count, i) for i in range(ends)])  13.1 us
  transfers between devices with their start and end apart: 17, of which 10 were waited for; matrix products, arithmetic and copies ran while one was open for 17% of the time, Pallas kernels for 0%

profile of v5, /device:TPU:1, one launch (start us, length us, event | category | flops | bytes accessed | tf_op | source)
XLA Modules:
  0.0 347.7 jit_solution(13546716717145713861)
XLA Ops:
  8.9 6.2 %collective-permute-start = (bf16[2,8,8,256]{3,2,1,0:T(8,128)(2,1)}, bf16[2,8,8,256]{3,2,1,0:T(8,128)(2,1)}, u32[]{:S(2)}, u32[]{:S(2)}) collective-permute-start(bf16[2,8,8,256]{3,2,1,0:T(8,128)(2,1)} %slice.97), channel_id=1, source_target_pairs={{0,32},{32,64},{64,96},{1,33},{33,65},{65,97},{2,34},{34,66},{66,9... | collective-permute-start | bytes 196616 | tf_op jit(solution)/shard_map/ppermute | solution.py:14
  23.7 2.6 collective-permute-done.1
  30.0 4.2 %collective-permute-start.2 = (bf16[6,1,24,256]{3,2,1,0:T(8,128)(2,1)S(1)}, bf16[6,1,24,256]{3,2,1,0:T(8,128)(2,1)S(1)}, u32[]{:S(2)}, u32[]{:S(2)}) collective-permute-start(bf16[6,1,24,256]{3,2,1,0:T(8,128)(2,1)S(1)} %pad_maximum_fusion.19), channel_id=1, source_target_pairs={{0,4},{4,8},{8,12},{12,16},{16,20},{20,24},{24,28},{1,5},{5,9},{9,... | collective-permute-start | bytes 221192 | tf_op jit(solution)/shard_map/ppermute | solution.py:104
  38.5 4.0 %collective-permute-start.4 = (bf16[6,28,1,256]{3,1,2,0:T(8,128)(2,1)S(1)}, bf16[6,28,1,256]{3,1,2,0:T(8,128)(2,1)S(1)}, u32[]{:S(2)}, u32[]{:S(2)}) collective-permute-start(bf16[6,28,1,256]{3,1,2,0:T(8,128)(2,1)S(1)} %pad_maximum_fusion.9), channel_id=1, source_target_pairs={{0,1},{1,2},{2,3},{4,5},{5,6},{6,7},{8,9},{9,10},{10,11},{12,13},{... | collective-permute-start | bytes 258056 | tf_op jit(solution)/shard_map/ppermute | solution.py:104
  46.6 2.7 reshape.80
  49.3 2.1 maximum_bitcast_fusion
  52.6 5.1 %reshape.99 = bf16[6,18,1,8,3,256]{5,4,3,1,0,2:T(4,128)(2,1)} reshape(bf16[6,18,1,24,256]{4,3,1,0,2:T(8,128)(2,1)} %pad.4) | data formatting | bytes 2654208 | tf_op jit(solution)/shard_map/conv_general_dilated | solution.py:55
  57.8 2.0 copy.89
  60.3 5.9 %fusion.42 = f32[4,16,8,3,256]{4,2,3,1,0:T(8,128)S(1)} fusion(bf16[3,3,3,256,256]{4,3,2,1,0:T(8,128)(2,1)S(1)} %copy-done.19, bf16[6,18,1,7,2,256]{5,3,4,1,0,2:T(8,128)(2,1)S(1)} %slice.158, bf16[6,18,1,8,3,256]{5,3,4,1,0,2:T(8,128)(2,1)S(1)} %copy.89, pred[8,3]{0,1:T(4,128)(4,1)S(1)} %copy-done.21), kind=kOutput, calls=%fused_computation.43 | convolution fusion | flops 5442846720 | bytes 7213080 | tf_op jit(solution)/shard_map/conv_general_dilated | solution.py:55
  69.4 6.3 %add_divide_fusion = (f32[4,16,8,3,256]{4,2,3,1,0:T(8,128)S(1)}, f32[4,16,8,3,256]{4,2,3,1,0:T(8,128)S(1)}, f32[4,16,8,3,256]{4,2,3,1,0:T(8,128)S(1)}) fusion(f32[256]{0:T(256)S(1)} %copy-done.17, bf16[3,3,3,256,256]{4,3,2,1,0:T(8,128)(2,1)S(1)} %copy-done, bf16[6,18,1,7,2,256]{5,3,4,1,0,2:T(8,128)(2,1)S(1)} %slice.151, ...), kind=kOutput, calls=%fused_computation.34 | convolution fusion | flops 5445599232 | bytes 10359832 | tf_op jit(solution)/shard_map/conv_general_dilated | solution.py:55
  76.2 3.2 fusion.55
  79.4 4.7 %collective-permute-start.6 = (bf16[2,16,16,256]{3,1,2,0:T(8,128)(2,1)S(1)}, bf16[2,16,16,256]{3,1,2,0:T(8,128)(2,1)S(1)}, u32[]{:S(2)}, u32[]{:S(2)}) collective-permute-start(bf16[2,16,16,256]{3,1,2,0:T(8,128)(2,1)S(1)} %slice.153), channel_id=1, source_target_pairs={{0,32},{32,64},{64,96},{1,33},{33,65},{65,97},{2,34},{34,66},{66,9... | collective-permute-start | bytes 786440 | tf_op jit(solution)/shard_map/ppermute | solution.py:14
  85.1 2.3 collective-permute-done.6
  87.6 4.0 %collective-permute-start.7 = (bf16[6,1,16,256]{3,1,2,0:T(2,128)(2,1)S(1)}, bf16[6,1,16,256]{3,1,2,0:T(2,128)(2,1)S(1)}, u32[]{:S(2)}, u32[]{:S(2)}) collective-permute-start(bf16[6,1,16,256]{3,1,2,0:T(2,128)(2,1)S(1)} %get-tuple-element.34), channel_id=1, source_target_pairs={{0,4},{4,8},{8,12},{12,16},{16,20},{20,24},{24,28},{1,5},{5,9},{9,... | collective-permute-start | bytes 147464 | tf_op jit(solution)/shard_map/ppermute | solution.py:25
  92.9 2.1 fusion.67
  95.1 2.1 collective-permute-done.8
  97.9 4.6 %collective-permute-start.9 = (bf16[6,18,1,256]{3,1,2,0:T(8,128)(2,1)}, bf16[6,18,1,256]{3,1,2,0:T(8,128)(2,1)}, u32[]{:S(2)}, u32[]{:S(2)}) collective-permute-start(bf16[6,18,1,256]{3,1,2,0:T(8,128)(2,1)} %get-tuple-element.28), channel_id=1, source_target_pairs={{0,1},{1,2},{2,3},{4,5},{5,6},{6,7},{8,9},{9,10},{10,11},{12,13},{... | collective-permute-start | bytes 165896 | tf_op jit(solution)/shard_map/ppermute | solution.py:25
  103.9 19.2 %fusion.34 = f32[3,3,3,256,256]{4,3,2,1,0:T(8,128)} fusion(bf16[1,6,18,18,256]{4,2,3,1,0:T(8,128)(2,1)S(1)} %get-tuple-element.22, bf16[1,4,16,16,256]{4,2,3,1,0:T(8,128)(2,1)S(1)} %fusion.67), kind=kOutput, calls=%fused_computation.31 | convolution fusion | flops 3623878656 | bytes 8597504 | tf_op jit(solution)/shard_map/transpose | solution.py:78
  123.1 2.9 fusion.89
  126.0 19.0 %fusion.32 = f32[3,3,3,256,256]{4,3,2,1,0:T(8,128)} fusion(bf16[1,6,18,18,256]{4,2,3,1,0:T(8,128)(2,1)S(1)} %get-tuple-element.24, bf16[1,4,16,16,256]{4,3,2,1,0:T(8,128)(2,1)S(1)} %bitcast.111), kind=kOutput, calls=%fused_computation.29 | convolution fusion | flops 3623878656 | bytes 8597504 | tf_op jit(solution)/shard_map/transpose | solution.py:78
  148.0 9.5 %collective-permute-done.11 = bf16[2,16,16,256]{3,1,2,0:T(8,128)(2,1)S(1)} collective-permute-done((bf16[2,16,16,256]{3,1,2,0:T(8,128)(2,1)S(1)}, bf16[2,16,16,256]{3,1,2,0:T(8,128)(2,1)S(1)}, u32[]{:S(2)}, u32[]{:S(2)}) %collective-permute-start.11) | collective-permute-done | bytes 262176 | tf_op jit(solution)/shard_map/ppermute | solution.py:14
  158.8 4.8 %collective-permute-start.12 = (bf16[6,1,16,256]{3,1,2,0:T(2,128)(2,1)S(1)}, bf16[6,1,16,256]{3,1,2,0:T(2,128)(2,1)S(1)}, u32[]{:S(2)}, u32[]{:S(2)}) collective-permute-start(bf16[6,1,16,256]{3,1,2,0:T(2,128)(2,1)S(1)} %get-tuple-element.32), channel_id=1, source_target_pairs={{0,4},{4,8},{8,12},{12,16},{16,20},{20,24},{24,28},{1,5},{5,9},{9,... | collective-permute-start | bytes 147464 | tf_op jit(solution)/shard_map/ppermute | solution.py:25
  165.2 6.9 %collective-permute-done.13 = bf16[6,1,16,256]{3,1,2,0:T(2,128)(2,1)S(1)} collective-permute-done((bf16[6,1,16,256]{3,1,2,0:T(2,128)(2,1)S(1)}, bf16[6,1,16,256]{3,1,2,0:T(2,128)(2,1)S(1)}, u32[]{:S(2)}, u32[]{:S(2)}) %collective-permute-start.13) | collective-permute-done | bytes 49184 | tf_op jit(solution)/shard_map/ppermute | solution.py:27
  173.0 4.3 %collective-permute-start.14 = (bf16[6,18,1,256]{3,1,2,0:T(8,128)(2,1)S(1)}, bf16[6,18,1,256]{3,1,2,0:T(8,128)(2,1)S(1)}, u32[]{:S(2)}, u32[]{:S(2)}) collective-permute-start(bf16[6,18,1,256]{3,1,2,0:T(8,128)(2,1)S(1)} %get-tuple-element.26), channel_id=1, source_target_pairs={{0,1},{1,2},{2,3},{4,5},{5,6},{6,7},{8,9},{9,10},{10,11},{12,13},{... | collective-permute-start | bytes 165896 | tf_op jit(solution)/shard_map/ppermute | solution.py:25
  179.0 4.1 %collective-permute-done.15 = bf16[6,18,1,256]{3,1,2,0:T(8,128)(2,1)S(1)} collective-permute-done((bf16[6,18,1,256]{3,1,2,0:T(8,128)(2,1)S(1)}, bf16[6,18,1,256]{3,1,2,0:T(8,128)(2,1)S(1)}, u32[]{:S(2)}, u32[]{:S(2)}) %collective-permute-start.15) | collective-permute-done | bytes 55328 | tf_op jit(solution)/shard_map/ppermute | solution.py:27
  184.7 5.9 %fusion.36 = f32[4,16,8,3,256]{4,2,3,1,0:T(8,128)S(1)} fusion(bf16[3,3,3,256,256]{4,3,2,1,0:T(8,128)(2,1)S(1)} %copy-done, bf16[6,18,1,7,2,256]{5,3,4,1,0,2:T(8,128)(2,1)S(1)} %slice.161, bf16[6,18,1,8,3,256]{5,3,4,1,0,2:T(8,128)(2,1)S(1)} %copy.93, pred[8,3]{0,1:T(4,128)(4,1)S(1)} %copy-done.22), kind=kOutput, calls=%fused_computation.41 | convolution fusion | flops 5442846720 | bytes 7213080 | tf_op jit(solution)/shard_map/conv_general_dilated | solution.py:55
  192.9 2.9 reshape.82
  195.9 2.8 reduce_sum.9
  204.0 6.5 %fusion.39 = f32[4,16,8,3,256]{4,2,3,1,0:T(8,128)S(1)} fusion(bf16[3,3,3,256,256]{4,3,2,1,0:T(8,128)(2,1)S(1)} %copy-done.20, bf16[6,18,1,7,2,256]{5,3,4,1,0,2:T(8,128)(2,1)S(1)} %slice.154, bf16[6,18,1,8,3,256]{5,3,4,1,0,2:T(8,128)(2,1)S(1)} %copy.83, pred[8,3]{0,1:T(4,128)(4,1)S(1)} %copy-done.22), kind=kOutput, calls=%fused_computation.42 | convolution fusion | flops 5442846720 | bytes 7213080 | tf_op jit(solution)/shard_map/conv_general_dilated | solution.py:55
  213.6 117.3 %all-reduce.3.cloned.1.call-done = (f32[3,3,3,256,256]{4,3,2,1,0:T(8,128)}, f32[3,3,3,256,256]{4,3,2,1,0:T(8,128)}) async-done(((f32[3,3,3,256,256]{4,3,2,1,0:T(8,128)}, f32[3,3,3,256,256]{4,3,2,1,0:T(8,128)}), (f32[3,3,3,256,256]{4,3,2,1,0:T(8,128)}, f32[3,3,3,256,256]{4,3,2,1,0:T(8,128)})) %all-reduce.3.cloned.1.call-update) | async-done | bytes 14155792 | tf_op jit(solution)/shard_map/psum | solution.py:155
  330.8 6.9 %copy.128 = f32[3,3,3,256,256]{4,3,2,1,0:T(8,128)} copy(f32[3,3,3,256,256]{4,3,2,1,0:T(8,128)} %get-tuple-element.49) | data formatting | bytes 14155776
  337.7 3.0 copy.129
  (132 shorter events, 52.8 us)
Async XLA Ops:
  7.2 62.0 %copy-start = (bf16[3,3,3,256,256]{4,3,2,1,0:T(8,128)(2,1)S(1)}, bf16[3,3,3,256,256]{4,3,2,1,0:T(8,128)(2,1)}, u32[]{:S(2)}) copy-start(bf16[3,3,3,256,256]{4,3,2,1,0:T(8,128)(2,1)} %param.8) | copy-start | bytes 10616836
  7.2 323.6 %all-reduce.3.cloned.1.call-start = ((), (), s32[]{:S(2)}) async-start(), calls=%async_computation | async-start | bytes 28311552 | tf_op jit(solution)/shard_map/psum | solution.py:155
  8.9 13.0 %collective-permute-start = (bf16[2,8,8,256]{3,2,1,0:T(8,128)(2,1)}, bf16[2,8,8,256]{3,2,1,0:T(8,128)(2,1)}, u32[]{:S(2)}, u32[]{:S(2)}) collective-permute-start(bf16[2,8,8,256]{3,2,1,0:T(8,128)(2,1)} %slice.97), channel_id=1, source_target_pairs={{0,32},{32,64},{64,96},{1,33},{33,65},{65,97},{2,34},{34,66},{66,9... | collective-permute-start | bytes 196616 | tf_op jit(solution)/shard_map/ppermute | solution.py:14
  16.7 9.5 %collective-permute-start.1 = (bf16[2,16,16,256]{3,2,1,0:T(8,128)(2,1)}, bf16[2,16,16,256]{3,2,1,0:T(8,128)(2,1)}, u32[]{:S(2)}, u32[]{:S(2)}) collective-permute-start(bf16[2,16,16,256]{3,2,1,0:T(8,128)(2,1)} %slice.99), channel_id=1, source_target_pairs={{32,0},{64,32},{96,64},{33,1},{65,33},{97,65},{34,2},{66,34},{98,6... | collective-permute-start | bytes 786440 | tf_op jit(solution)/shard_map/ppermute | solution.py:14
  28.7 5.5 %collective-permute-start.3 = (bf16[6,1,24,256]{3,2,1,0:T(8,128)(2,1)S(1)}, bf16[6,1,24,256]{3,2,1,0:T(8,128)(2,1)S(1)}, u32[]{:S(2)}, u32[]{:S(2)}) collective-permute-start(bf16[6,1,24,256]{3,2,1,0:T(8,128)(2,1)S(1)} %pad_maximum_fusion.20), channel_id=1, source_target_pairs={{4,0},{8,4},{12,8},{16,12},{20,16},{24,20},{28,24},{5,1},{9,5},{13... | collective-permute-start | bytes 221192 | tf_op jit(solution)/shard_map/ppermute | solution.py:105
  30.0 5.6 %collective-permute-start.2 = (bf16[6,1,24,256]{3,2,1,0:T(8,128)(2,1)S(1)}, bf16[6,1,24,256]{3,2,1,0:T(8,128)(2,1)S(1)}, u32[]{:S(2)}, u32[]{:S(2)}) collective-permute-start(bf16[6,1,24,256]{3,2,1,0:T(8,128)(2,1)S(1)} %pad_maximum_fusion.19), channel_id=1, source_target_pairs={{0,4},{4,8},{8,12},{12,16},{16,20},{20,24},{24,28},{1,5},{5,9},{9,... | collective-permute-start | bytes 221192 | tf_op jit(solution)/shard_map/ppermute | solution.py:104
  35.8 9.5 %copy-start.11 = (bf16[6,1,16,256]{3,2,1,0:T(8,128)(2,1)}, bf16[6,1,16,256]{3,2,1,0:T(8,128)(2,1)S(1)}, u32[]{:S(2)}) copy-start(bf16[6,1,16,256]{3,2,1,0:T(8,128)(2,1)S(1)} %slice.146) | copy-start | bytes 147460
  35.8 9.5 %copy-start.12 = (bf16[6,1,16,256]{3,2,1,0:T(8,128)(2,1)}, bf16[6,1,16,256]{3,2,1,0:T(8,128)(2,1)S(1)}, u32[]{:S(2)}) copy-start(bf16[6,1,16,256]{3,2,1,0:T(8,128)(2,1)S(1)} %slice.145) | copy-start | bytes 147460
  37.2 5.4 %collective-permute-start.5 = (bf16[6,28,1,256]{3,1,2,0:T(8,128)(2,1)S(1)}, bf16[6,28,1,256]{3,1,2,0:T(8,128)(2,1)S(1)}, u32[]{:S(2)}, u32[]{:S(2)}) collective-permute-start(bf16[6,28,1,256]{3,1,2,0:T(8,128)(2,1)S(1)} %pad_maximum_fusion.10), channel_id=1, source_target_pairs={{1,0},{2,1},{3,2},{5,4},{6,5},{7,6},{9,8},{10,9},{11,10},{13,12},{... | collective-permute-start | bytes 258056 | tf_op jit(solution)/shard_map/ppermute | solution.py:105
  38.5 5.6 %collective-permute-start.4 = (bf16[6,28,1,256]{3,1,2,0:T(8,128)(2,1)S(1)}, bf16[6,28,1,256]{3,1,2,0:T(8,128)(2,1)S(1)}, u32[]{:S(2)}, u32[]{:S(2)}) collective-permute-start(bf16[6,28,1,256]{3,1,2,0:T(8,128)(2,1)S(1)} %pad_maximum_fusion.9), channel_id=1, source_target_pairs={{0,1},{1,2},{2,3},{4,5},{5,6},{6,7},{8,9},{9,10},{10,11},{12,13},{... | collective-permute-start | bytes 258056 | tf_op jit(solution)/shard_map/ppermute | solution.py:104
  57.8 2.5 copy-start.19
  79.4 17.8 %copy-start.2 = (bf16[4,16,16,256]{3,1,2,0:T(8,128)(2,1)}, bf16[4,16,16,256]{3,1,2,0:T(8,128)(2,1)S(1)}, u32[]{:S(2)}) copy-start(bf16[4,16,16,256]{3,1,2,0:T(8,128)(2,1)S(1)} %get-tuple-element.19) | copy-start | bytes 1572868
  79.4 8.0 %collective-permute-start.6 = (bf16[2,16,16,256]{3,1,2,0:T(8,128)(2,1)S(1)}, bf16[2,16,16,256]{3,1,2,0:T(8,128)(2,1)S(1)}, u32[]{:S(2)}, u32[]{:S(2)}) collective-permute-start(bf16[2,16,16,256]{3,1,2,0:T(8,128)(2,1)S(1)} %slice.153), channel_id=1, source_target_pairs={{0,32},{32,64},{64,96},{1,33},{33,65},{65,97},{2,34},{34,66},{66,9... | collective-permute-start | bytes 786440 | tf_op jit(solution)/shard_map/ppermute | solution.py:14
  87.4 9.7 %copy-start.9 = (bf16[2,16,16,256]{3,1,2,0:T(8,128)(2,1)}, bf16[2,16,16,256]{3,1,2,0:T(8,128)(2,1)S(1)}, u32[]{:S(2)}) copy-start(bf16[2,16,16,256]{3,1,2,0:T(8,128)(2,1)S(1)} %collective-permute-done.6) | copy-start | bytes 786436
  87.6 7.5 %collective-permute-start.7 = (bf16[6,1,16,256]{3,1,2,0:T(2,128)(2,1)S(1)}, bf16[6,1,16,256]{3,1,2,0:T(2,128)(2,1)S(1)}, u32[]{:S(2)}, u32[]{:S(2)}) collective-permute-start(bf16[6,1,16,256]{3,1,2,0:T(2,128)(2,1)S(1)} %get-tuple-element.34), channel_id=1, source_target_pairs={{0,4},{4,8},{8,12},{12,16},{16,20},{20,24},{24,28},{1,5},{5,9},{9,... | collective-permute-start | bytes 147464 | tf_op jit(solution)/shard_map/ppermute | solution.py:25
  91.6 5.5 %collective-permute-start.8 = (bf16[6,1,16,256]{3,1,2,0:T(2,128)(2,1)S(1)}, bf16[6,1,16,256]{3,1,2,0:T(2,128)(2,1)S(1)}, u32[]{:S(2)}, u32[]{:S(2)}) collective-permute-start(bf16[6,1,16,256]{3,1,2,0:T(2,128)(2,1)S(1)} %get-tuple-element.35), channel_id=1, source_target_pairs={{4,0},{8,4},{12,8},{16,12},{20,16},{24,20},{28,24},{5,1},{9,5},{13... | collective-permute-start | bytes 147464 | tf_op jit(solution)/shard_map/ppermute | solution.py:27
  95.1 8.8 %copy-start.13 = (bf16[6,1,16,256]{3,1,2,0:T(2,128)(2,1)}, bf16[6,1,16,256]{3,1,2,0:T(2,128)(2,1)S(1)}, u32[]{:S(2)}) copy-start(bf16[6,1,16,256]{3,1,2,0:T(2,128)(2,1)S(1)} %collective-permute-done.7) | copy-start | bytes 147460
  97.2 6.7 %copy-start.15 = (bf16[6,1,16,256]{3,1,2,0:T(2,128)(2,1)}, bf16[6,1,16,256]{3,1,2,0:T(2,128)(2,1)S(1)}, u32[]{:S(2)}) copy-start(bf16[6,1,16,256]{3,1,2,0:T(2,128)(2,1)S(1)} %collective-permute-done.8) | copy-start | bytes 147460
  97.9 25.2 %collective-permute-start.9 = (bf16[6,18,1,256]{3,1,2,0:T(8,128)(2,1)}, bf16[6,18,1,256]{3,1,2,0:T(8,128)(2,1)}, u32[]{:S(2)}, u32[]{:S(2)}) collective-permute-start(bf16[6,18,1,256]{3,1,2,0:T(8,128)(2,1)} %get-tuple-element.28), channel_id=1, source_target_pairs={{0,1},{1,2},{2,3},{4,5},{5,6},{6,7},{8,9},{9,10},{10,11},{12,13},{... | collective-permute-start | bytes 165896 | tf_op jit(solution)/shard_map/ppermute | solution.py:25
  102.5 20.5 %collective-permute-start.10 = (bf16[6,18,1,256]{3,1,2,0:T(8,128)(2,1)}, bf16[6,18,1,256]{3,1,2,0:T(8,128)(2,1)}, u32[]{:S(2)}, u32[]{:S(2)}) collective-permute-start(bf16[6,18,1,256]{3,1,2,0:T(8,128)(2,1)} %get-tuple-element.29), channel_id=1, source_target_pairs={{1,0},{2,1},{3,2},{5,4},{6,5},{7,6},{9,8},{10,9},{11,10},{13,12},{... | collective-permute-start | bytes 165896 | tf_op jit(solution)/shard_map/ppermute | solution.py:27
  103.8 19.2 %copy-start.3 = (bf16[4,16,16,256]{3,1,2,0:T(8,128)(2,1)S(1)}, bf16[4,16,16,256]{3,1,2,0:T(8,128)(2,1)}, u32[]{:S(2)}) copy-start(bf16[4,16,16,256]{3,1,2,0:T(8,128)(2,1)} %copy-done.2) | copy-start | bytes 1572868
  103.8 19.2 %copy-start.10 = (bf16[2,16,16,256]{3,1,2,0:T(8,128)(2,1)S(1)}, bf16[2,16,16,256]{3,1,2,0:T(8,128)(2,1)}, u32[]{:S(2)}) copy-start(bf16[2,16,16,256]{3,1,2,0:T(8,128)(2,1)} %copy-done.9) | copy-start | bytes 786436
  103.9 19.2 %copy-start.14 = (bf16[6,1,16,256]{3,1,2,0:T(2,128)(2,1)S(1)}, bf16[6,1,16,256]{3,1,2,0:T(2,128)(2,1)}, u32[]{:S(2)}) copy-start(bf16[6,1,16,256]{3,1,2,0:T(2,128)(2,1)} %copy-done.13) | copy-start | bytes 147460
  103.9 19.2 %copy-start.16 = (bf16[6,1,16,256]{3,1,2,0:T(2,128)(2,1)S(1)}, bf16[6,1,16,256]{3,1,2,0:T(2,128)(2,1)}, u32[]{:S(2)}) copy-start(bf16[6,1,16,256]{3,1,2,0:T(2,128)(2,1)} %copy-done.15) | copy-start | bytes 147460
  123.1 2.9 copy-start.6
  145.1 38.0 %copy-start.1 = (bf16[4,16,16,256]{3,1,2,0:T(8,128)(2,1)S(1)}, bf16[4,16,16,256]{3,1,2,0:T(8,128)(2,1)}, u32[]{:S(2)}) copy-start(bf16[4,16,16,256]{3,1,2,0:T(8,128)(2,1)} %get-tuple-element.18) | copy-start | bytes 1572868
  146.1 11.5 %collective-permute-start.11 = (bf16[2,16,16,256]{3,1,2,0:T(8,128)(2,1)S(1)}, bf16[2,16,16,256]{3,1,2,0:T(8,128)(2,1)S(1)}, u32[]{:S(2)}, u32[]{:S(2)}) collective-permute-start(bf16[2,16,16,256]{3,1,2,0:T(8,128)(2,1)S(1)} %slice.160), channel_id=1, source_target_pairs={{32,0},{64,32},{96,64},{33,1},{65,33},{97,65},{34,2},{66,34},{98,6... | collective-permute-start | bytes 786440 | tf_op jit(solution)/shard_map/ppermute | solution.py:14
  158.8 6.4 %collective-permute-start.12 = (bf16[6,1,16,256]{3,1,2,0:T(2,128)(2,1)S(1)}, bf16[6,1,16,256]{3,1,2,0:T(2,128)(2,1)S(1)}, u32[]{:S(2)}, u32[]{:S(2)}) collective-permute-start(bf16[6,1,16,256]{3,1,2,0:T(2,128)(2,1)S(1)} %get-tuple-element.32), channel_id=1, source_target_pairs={{0,4},{4,8},{8,12},{12,16},{16,20},{20,24},{24,28},{1,5},{5,9},{9,... | collective-permute-start | bytes 147464 | tf_op jit(solution)/shard_map/ppermute | solution.py:25
  163.6 8.5 %collective-permute-start.13 = (bf16[6,1,16,256]{3,1,2,0:T(2,128)(2,1)S(1)}, bf16[6,1,16,256]{3,1,2,0:T(2,128)(2,1)S(1)}, u32[]{:S(2)}, u32[]{:S(2)}) collective-permute-start(bf16[6,1,16,256]{3,1,2,0:T(2,128)(2,1)S(1)} %get-tuple-element.33), channel_id=1, source_target_pairs={{4,0},{8,4},{12,8},{16,12},{20,16},{24,20},{28,24},{5,1},{9,5},{13... | collective-permute-start | bytes 147464 | tf_op jit(solution)/shard_map/ppermute | solution.py:27
  173.0 6.0 %collective-permute-start.14 = (bf16[6,18,1,256]{3,1,2,0:T(8,128)(2,1)S(1)}, bf16[6,18,1,256]{3,1,2,0:T(8,128)(2,1)S(1)}, u32[]{:S(2)}, u32[]{:S(2)}) collective-permute-start(bf16[6,18,1,256]{3,1,2,0:T(8,128)(2,1)S(1)} %get-tuple-element.26), channel_id=1, source_target_pairs={{0,1},{1,2},{2,3},{4,5},{5,6},{6,7},{8,9},{9,10},{10,11},{12,13},{... | collective-permute-start | bytes 165896 | tf_op jit(solution)/shard_map/ppermute | solution.py:25
  177.3 5.8 %collective-permute-start.15 = (bf16[6,18,1,256]{3,1,2,0:T(8,128)(2,1)S(1)}, bf16[6,18,1,256]{3,1,2,0:T(8,128)(2,1)S(1)}, u32[]{:S(2)}, u32[]{:S(2)}) collective-permute-start(bf16[6,18,1,256]{3,1,2,0:T(8,128)(2,1)S(1)} %get-tuple-element.27), channel_id=1, source_target_pairs={{1,0},{2,1},{3,2},{5,4},{6,5},{7,6},{9,8},{10,9},{11,10},{13,12},{... | collective-permute-start | bytes 165896 | tf_op jit(solution)/shard_map/ppermute | solution.py:27
  330.8 6.9 %copy-start.5 = (f32[3,3,3,256,256]{4,3,2,1,0:T(8,128)S(1)}, f32[3,3,3,256,256]{4,3,2,1,0:T(8,128)}, u32[]{:S(2)}) copy-start(f32[3,3,3,256,256]{4,3,2,1,0:T(8,128)} %get-tuple-element.50) | copy-start | bytes 21233668
  (8 other events, 10.1 us)
Sparse Core Ops, SparseCore 0:
  145.2 185.5 all-reduce.2

commit v6 on v5

--- a/solution.py
+++ b/solution.py
@@ -134,7 +134,7 @@
     )
     dropped = (jax.nn.silu(pre_first) * scaling).astype(jnp.bfloat16)
     dropped_ext = face_cells(with_earlier(dropped))
-    grad_second = weight_gradient(dropped_ext, upstream)
+    grad_second = flipped(weight_gradient(upstream_ext, dropped))
     mixed = (cells_here.astype(jnp.float32) + convolve(dropped_ext, w_second) + b_second).astype(
         jnp.bfloat16
     )

time: 353 us -> 335 us (0.949)
  waiting for transfers between devices: 147 us -> 128 us
  local copies, waits for them, and re-layouts: 52.5 us -> 62 us
  starting transfers between devices: 48.8 us -> 44 us
  other arithmetic: 21.5 us -> 17.9 us
    ppermute x4, waiting for transfers between devices: 14.4 us -> 4.65 us  [shifted(): return lax.ppermute(block, axis, route)]
    ppermute x4, waiting for transfers between devices: 13.1 us -> 5.98 us  [extended_2(): lax.ppermute(head, axis, [((i + 1) % count, i) for i in range(ends)])]
    psum x1, waiting for transfers between devices: 117 us -> 111 us  [local(): grad_first, grad_second = lax.psum((grad_first, grad_second), ALL)]
    unnamed x52 -> x58, local copies, waits for them, and re-layouts: 19.3 us -> 24.3 us
    ppermute x4, starting transfers between devices: 17.7 us -> 13.3 us  [extended_2(): lax.ppermute(tail, axis, [(i, (i + 1) % count) for i in range(ends)])]
    ppermute x2, waiting for transfers between devices: 0.01 us -> 3.76 us  [faces_together(): from_next = lax.ppermute(head, axis, [(i + 1, i) for i in range(ends)])]
  transfers between devices with their start and end apart: 17 -> 17, of which waited for: 10 -> 8; matrix products, arithmetic and copies ran while one was open for 17% -> 12% of each run, Pallas kernels for 0% -> 0%
where the time goes in v6:
time: 335 us; the launch traced here: 330 us
  waiting for transfers between devices  128 us (38%)
  matrix products  62.8 us (19%)
  local copies, waits for them, and re-layouts  62 us (19%)
  starting transfers between devices  44 us (13%)
  other arithmetic  17.9 us (5%)
  between operations  15 us (4%)
    psum x1, waiting for transfers between devices, local(): grad_first, grad_second = lax.psum((grad_first, grad_second), ALL)  111 us
    transpose x2, matrix products, weight_gradient(): return jnp.transpose(summed, (1, 2, 3, 0, 4))  36.7 us
    conv_general_dilated x4, matrix products, convolve(): lax.conv_general_dilated(extended[None], weight, (1, 1, 1), 'VALID', dime...  26.1 us
    unnamed x58, local copies, waits for them, and re-layouts  24.3 us
    ppermute x4, starting transfers between devices, shifted(): return lax.ppermute(block, axis, route)  15.2 us
    ppermute x4, starting transfers between devices, extended_2(): lax.ppermute(tail, axis, [(i, (i + 1) % count) for i in range(ends)])  13.3 us
    conv_general_dilated x13, local copies, waits for them, and re-layouts, convolve(): lax.conv_general_dilated(extended[None], weight, (1, 1, 1), 'VALID', dime...  12 us
    ppermute x2, starting transfers between devices, faces_together(): from_prev = lax.ppermute(tail, axis, [(i, i + 1) for i in range(ends)])  7.3 us
  transfers between devices with their start and end apart: 17, of which 8 were waited for; matrix products, arithmetic and copies ran while one was open for 12% of the time, Pallas kernels for 0%

profile of v6, /device:TPU:1, one launch (start us, length us, event | category | flops | bytes accessed | tf_op | source)
XLA Modules:
  0.0 329.8 jit_solution(8515775649328649379)
XLA Ops:
  8.9 6.2 %collective-permute-start = (bf16[2,8,8,256]{3,2,1,0:T(8,128)(2,1)}, bf16[2,8,8,256]{3,2,1,0:T(8,128)(2,1)}, u32[]{:S(2)}, u32[]{:S(2)}) collective-permute-start(bf16[2,8,8,256]{3,2,1,0:T(8,128)(2,1)} %slice.97), channel_id=1, source_target_pairs={{0,32},{32,64},{64,96},{1,33},{33,65},{65,97},{2,34},{34,66},{66,9... | collective-permute-start | bytes 196616 | tf_op jit(solution)/shard_map/ppermute | solution.py:14
  23.7 2.6 collective-permute-done.1
  30.0 4.2 %collective-permute-start.2 = (bf16[6,1,24,256]{3,2,1,0:T(8,128)(2,1)S(1)}, bf16[6,1,24,256]{3,2,1,0:T(8,128)(2,1)S(1)}, u32[]{:S(2)}, u32[]{:S(2)}) collective-permute-start(bf16[6,1,24,256]{3,2,1,0:T(8,128)(2,1)S(1)} %pad_maximum_fusion.22), channel_id=1, source_target_pairs={{0,4},{4,8},{8,12},{12,16},{16,20},{20,24},{24,28},{1,5},{5,9},{9,... | collective-permute-start | bytes 221192 | tf_op jit(solution)/shard_map/ppermute | solution.py:104
  37.0 3.1 collective-permute-start.4
  42.6 3.8 %collective-permute-done.5 = bf16[6,28,1,256]{3,2,1,0:T(2,128)(2,1)S(1)} collective-permute-done((bf16[6,28,1,256]{3,2,1,0:T(2,128)(2,1)S(1)}, bf16[6,28,1,256]{3,2,1,0:T(2,128)(2,1)S(1)}, u32[]{:S(2)}, u32[]{:S(2)}) %collective-permute-start.5) | collective-permute-done | bytes 86048 | tf_op jit(solution)/shard_map/ppermute | solution.py:105
  48.7 2.7 reshape.81
  53.4 3.1 fusion.80
  57.8 4.9 %reshape.100 = bf16[6,18,1,8,3,256]{5,4,3,1,0,2:T(4,128)(2,1)} reshape(bf16[6,18,1,24,256]{4,3,1,0,2:T(8,128)(2,1)} %pad.4) | data formatting | bytes 2654208 | tf_op jit(solution)/shard_map/conv_general_dilated | solution.py:55
  62.7 2.0 copy.50
  65.3 5.9 %fusion.42 = f32[4,16,8,3,256]{4,2,3,1,0:T(8,128)S(1)} fusion(bf16[3,3,3,256,256]{4,3,2,1,0:T(8,128)(2,1)S(1)} %copy-done.22, bf16[6,18,1,7,2,256]{5,3,4,1,0,2:T(8,128)(2,1)S(1)} %slice.159, bf16[6,18,1,8,3,256]{5,3,4,1,0,2:T(8,128)(2,1)S(1)} %copy.50, pred[8,3]{0,1:T(4,128)(4,1)S(1)} %copy-done.24), kind=kOutput, calls=%fused_computation.44 | convolution fusion | flops 5442846720 | bytes 7213080 | tf_op jit(solution)/shard_map/conv_general_dilated | solution.py:55
  75.2 7.9 %add_multiply_fusion = (f32[4,16,8,3,256]{4,2,3,1,0:T(8,128)S(1)}, f32[4,16,8,3,256]{4,2,3,1,0:T(8,128)S(1)}, f32[4,16,8,3,256]{4,2,3,1,0:T(8,128)S(1)}, f32[4,16,8,3,256]{4,2,3,1,0:T(8,128)}) fusion(f32[256]{0:T(256)S(1)} %copy-done.19, bf16[3,3,3,256,256]{4,3,2,1,0:T(8,128)(2,1)S(1)} %copy-done, bf16[6,18,1,7,2,256]{5,3,4,1,0,2:T(8,128)(2,1)S(1)} %slice.152, ...), kind=kOutput, calls=%fused_computation.46 | convolution fusion | flops 5445992448 | bytes 11932696 | tf_op jit(solution)/shard_map/conv_general_dilated | solution.py:55
  84.6 3.0 fusion.59
  87.6 17.3 %fusion.34 = f32[3,3,3,256,256]{4,3,2,1,0:T(8,128)S(1)} fusion(bf16[1,6,18,18,256]{4,3,2,1,0:T(8,128)(2,1)S(1)} %copy-done.6, bf16[1,4,16,16,256]{4,2,3,1,0:T(8,128)(2,1)S(1)} %get-tuple-element.41), kind=kOutput, calls=%fused_computation.32 | convolution fusion | flops 3623878656 | bytes 8597504 | tf_op jit(solution)/shard_map/transpose | solution.py:78
  105.0 3.4 %reverse_bitcast_fusion = f32[3,3,3,256,256]{3,4,2,1,0:T(8,128)} fusion(f32[3,3,3,256,256]{4,3,2,1,0:T(8,128)S(1)} %fusion.34), kind=kLoop, calls=%fused_computation | loop fusion | bytes 14155776 | tf_op jit(solution)/shard_map/transpose | solution.py:66
  108.4 19.4 %fusion.32 = f32[3,3,3,256,256]{4,3,2,1,0:T(8,128)} fusion(bf16[1,6,18,18,256]{4,2,3,1,0:T(8,128)(2,1)S(1)} %copy-done.7, bf16[1,4,16,16,256]{4,2,3,1,0:T(8,128)(2,1)S(1)} %copy-done.8), kind=kOutput, calls=%fused_computation.30 | convolution fusion | flops 3623878656 | bytes 8597504 | tf_op jit(solution)/shard_map/transpose | solution.py:78
  127.8 2.0 copy.43
  129.9 2.4 fusion.55
  134.3 5.1 %collective-permute-start.6 = (bf16[2,16,16,256]{3,1,2,0:T(8,128)(2,1)S(1)}, bf16[2,16,16,256]{3,1,2,0:T(8,128)(2,1)S(1)}, u32[]{:S(2)}, u32[]{:S(2)}) collective-permute-start(bf16[2,16,16,256]{3,1,2,0:T(8,128)(2,1)S(1)} %slice.154), channel_id=1, source_target_pairs={{0,32},{32,64},{64,96},{1,33},{33,65},{65,97},{2,34},{34,66},{66,9... | collective-permute-start | bytes 786440 | tf_op jit(solution)/shard_map/ppermute | solution.py:14
  139.4 2.1 collective-permute-done.11
  141.7 3.8 %collective-permute-start.12 = (bf16[6,1,16,256]{3,1,2,0:T(2,128)(2,1)S(1)}, bf16[6,1,16,256]{3,1,2,0:T(2,128)(2,1)S(1)}, u32[]{:S(2)}, u32[]{:S(2)}) collective-permute-start(bf16[6,1,16,256]{3,1,2,0:T(2,128)(2,1)S(1)} %get-tuple-element.33), channel_id=1, source_target_pairs={{0,4},{4,8},{8,12},{12,16},{16,20},{20,24},{24,28},{1,5},{5,9},{9,... | collective-permute-start | bytes 147464 | tf_op jit(solution)/shard_map/ppermute | solution.py:25
  147.1 4.2 %collective-permute-start.7 = (bf16[6,1,16,256]{3,1,2,0:T(2,128)(2,1)S(1)}, bf16[6,1,16,256]{3,1,2,0:T(2,128)(2,1)S(1)}, u32[]{:S(2)}, u32[]{:S(2)}) collective-permute-start(bf16[6,1,16,256]{3,1,2,0:T(2,128)(2,1)S(1)} %get-tuple-element.35), channel_id=1, source_target_pairs={{0,4},{4,8},{8,12},{12,16},{16,20},{20,24},{24,28},{1,5},{5,9},{9,... | collective-permute-start | bytes 147464 | tf_op jit(solution)/shard_map/ppermute | solution.py:25
  152.6 3.1 collective-permute-start.14
  157.1 2.9 collective-permute-done.8
  160.0 2.2 collective-permute-start.9
  165.2 3.1 collective-permute-done.10
  171.5 6.2 %fusion.39 = f32[4,16,8,3,256]{4,2,3,1,0:T(8,128)S(1)} fusion(bf16[3,3,3,256,256]{4,3,2,1,0:T(8,128)(2,1)S(1)} %copy-done.23, bf16[6,18,1,7,2,256]{5,3,4,1,0,2:T(8,128)(2,1)S(1)} %slice.155, bf16[6,18,1,8,3,256]{5,3,4,1,0,2:T(8,128)(2,1)S(1)} %copy.46, pred[8,3]{0,1:T(4,128)(4,1)S(1)} %copy-done.25), kind=kOutput, calls=%fused_computation.43 | convolution fusion | flops 5442846720 | bytes 7213080 | tf_op jit(solution)/shard_map/conv_general_dilated | solution.py:55
  181.1 6.1 %fusion.36 = f32[4,16,8,3,256]{4,2,3,1,0:T(8,128)S(1)} fusion(bf16[3,3,3,256,256]{4,3,2,1,0:T(8,128)(2,1)S(1)} %copy-done, bf16[6,18,1,7,2,256]{5,3,4,1,0,2:T(8,128)(2,1)S(1)} %slice.162, bf16[6,18,1,8,3,256]{5,3,4,1,0,2:T(8,128)(2,1)S(1)} %copy.54, pred[8,3]{0,1:T(4,128)(4,1)S(1)} %copy-done.25), kind=kOutput, calls=%fused_computation.42 | convolution fusion | flops 5442846720 | bytes 7213080 | tf_op jit(solution)/shard_map/conv_general_dilated | solution.py:55
  189.4 2.8 reshape.83
  192.2 2.7 reduce_sum.9
  196.6 111.4 %all-reduce.3.cloned.1.call-done = (f32[3,3,3,256,256]{4,3,2,1,0:T(8,128)}, f32[3,3,3,256,256]{3,4,2,1,0:T(8,128)}) async-done(((f32[3,3,3,256,256]{4,3,2,1,0:T(8,128)}, f32[3,3,3,256,256]{3,4,2,1,0:T(8,128)}), (f32[3,3,3,256,256]{4,3,2,1,0:T(8,128)}, f32[3,3,3,256,256]{3,4,2,1,0:T(8,128)})) %all-reduce.3.cloned.1.call-update) | async-done | bytes 14155792 | tf_op jit(solution)/shard_map/psum | solution.py:155
  308.0 8.0 %copy.66 = f32[3,3,3,256,256]{4,3,2,1,0:T(8,128)} copy(f32[3,3,3,256,256]{3,4,2,1,0:T(8,128)} %get-tuple-element.17) | data formatting | bytes 14155776
  316.0 6.7 %copy.88 = f32[3,3,3,256,256]{4,3,2,1,0:T(8,128)} copy(f32[3,3,3,256,256]{4,3,2,1,0:T(8,128)} %get-tuple-element.50) | data formatting | bytes 14155776
  (129 shorter events, 50.4 us)
Async XLA Ops:
  7.2 67.8 %copy-start = (bf16[3,3,3,256,256]{4,3,2,1,0:T(8,128)(2,1)S(1)}, bf16[3,3,3,256,256]{4,3,2,1,0:T(8,128)(2,1)}, u32[]{:S(2)}) copy-start(bf16[3,3,3,256,256]{4,3,2,1,0:T(8,128)(2,1)} %param.8) | copy-start | bytes 10616836
  7.2 300.8 %all-reduce.3.cloned.1.call-start = ((), (), s32[]{:S(2)}) async-start(), calls=%async_computation | async-start | bytes 28311552 | tf_op jit(solution)/shard_map/psum | solution.py:155
  8.9 13.0 %collective-permute-start = (bf16[2,8,8,256]{3,2,1,0:T(8,128)(2,1)}, bf16[2,8,8,256]{3,2,1,0:T(8,128)(2,1)}, u32[]{:S(2)}, u32[]{:S(2)}) collective-permute-start(bf16[2,8,8,256]{3,2,1,0:T(8,128)(2,1)} %slice.97), channel_id=1, source_target_pairs={{0,32},{32,64},{64,96},{1,33},{33,65},{65,97},{2,34},{34,66},{66,9... | collective-permute-start | bytes 196616 | tf_op jit(solution)/shard_map/ppermute | solution.py:14
  16.7 9.5 %collective-permute-start.1 = (bf16[2,16,16,256]{3,2,1,0:T(8,128)(2,1)}, bf16[2,16,16,256]{3,2,1,0:T(8,128)(2,1)}, u32[]{:S(2)}, u32[]{:S(2)}) collective-permute-start(bf16[2,16,16,256]{3,2,1,0:T(8,128)(2,1)} %slice.99), channel_id=1, source_target_pairs={{32,0},{64,32},{96,64},{33,1},{65,33},{97,65},{34,2},{66,34},{98,6... | collective-permute-start | bytes 786440 | tf_op jit(solution)/shard_map/ppermute | solution.py:14
  28.7 5.5 %collective-permute-start.3 = (bf16[6,1,24,256]{3,2,1,0:T(8,128)(2,1)S(1)}, bf16[6,1,24,256]{3,2,1,0:T(8,128)(2,1)S(1)}, u32[]{:S(2)}, u32[]{:S(2)}) collective-permute-start(bf16[6,1,24,256]{3,2,1,0:T(8,128)(2,1)S(1)} %pad_maximum_fusion.23), channel_id=1, source_target_pairs={{4,0},{8,4},{12,8},{16,12},{20,16},{24,20},{28,24},{5,1},{9,5},{13... | collective-permute-start | bytes 221192 | tf_op jit(solution)/shard_map/ppermute | solution.py:105
  30.0 5.6 %collective-permute-start.2 = (bf16[6,1,24,256]{3,2,1,0:T(8,128)(2,1)S(1)}, bf16[6,1,24,256]{3,2,1,0:T(8,128)(2,1)S(1)}, u32[]{:S(2)}, u32[]{:S(2)}) collective-permute-start(bf16[6,1,24,256]{3,2,1,0:T(8,128)(2,1)S(1)} %pad_maximum_fusion.22), channel_id=1, source_target_pairs={{0,4},{4,8},{8,12},{12,16},{16,20},{20,24},{24,28},{1,5},{5,9},{9,... | collective-permute-start | bytes 221192 | tf_op jit(solution)/shard_map/ppermute | solution.py:104
  34.2 50.3 %copy-start.13 = (s32[16]{0:T(128)}, s32[16]{0:T(128)S(1)}, u32[]{:S(2)}) copy-start(s32[16]{0:T(128)S(1)} %get-tuple-element.46) | copy-start | bytes 196
  34.3 50.3 %copy-start.15 = (s32[16]{0:T(128)}, s32[16]{0:T(128)S(1)}, u32[]{:S(2)}) copy-start(s32[16]{0:T(128)S(1)} %get-tuple-element.47) | copy-start | bytes 196
  34.3 13.1 %copy-start.9 = (bf16[6,1,16,256]{3,2,1,0:T(8,128)(2,1)}, bf16[6,1,16,256]{3,2,1,0:T(8,128)(2,1)S(1)}, u32[]{:S(2)}) copy-start(bf16[6,1,16,256]{3,2,1,0:T(8,128)(2,1)S(1)} %slice.147) | copy-start | bytes 147460
  35.6 11.8 %copy-start.10 = (bf16[6,1,16,256]{3,2,1,0:T(8,128)(2,1)}, bf16[6,1,16,256]{3,2,1,0:T(8,128)(2,1)S(1)}, u32[]{:S(2)}) copy-start(bf16[6,1,16,256]{3,2,1,0:T(8,128)(2,1)S(1)} %slice.146) | copy-start | bytes 147460
  37.0 5.5 %collective-permute-start.4 = (bf16[6,28,1,256]{3,2,1,0:T(2,128)(2,1)S(1)}, bf16[6,28,1,256]{3,2,1,0:T(2,128)(2,1)S(1)}, u32[]{:S(2)}, u32[]{:S(2)}) collective-permute-start(bf16[6,28,1,256]{3,2,1,0:T(2,128)(2,1)S(1)} %get-tuple-element.25), channel_id=1, source_target_pairs={{0,1},{1,2},{2,3},{4,5},{5,6},{6,7},{8,9},{9,10},{10,11},{12,13},{... | collective-permute-start | bytes 258056 | tf_op jit(solution)/shard_map/ppermute | solution.py:104
  40.2 6.2 %collective-permute-start.5 = (bf16[6,28,1,256]{3,2,1,0:T(2,128)(2,1)S(1)}, bf16[6,28,1,256]{3,2,1,0:T(2,128)(2,1)S(1)}, u32[]{:S(2)}, u32[]{:S(2)}) collective-permute-start(bf16[6,28,1,256]{3,2,1,0:T(2,128)(2,1)S(1)} %get-tuple-element.26), channel_id=1, source_target_pairs={{1,0},{2,1},{3,2},{5,4},{6,5},{7,6},{9,8},{10,9},{11,10},{13,12},{... | collective-permute-start | bytes 258056 | tf_op jit(solution)/shard_map/ppermute | solution.py:105
  41.5 43.0 %copy-start.17 = (s32[4]{0:T(128)}, s32[4]{0:T(128)S(1)}, u32[]{:S(2)}) copy-start(s32[4]{0:T(128)S(1)} %add_multiply_fusion.1) | copy-start | bytes 52
  42.5 3.8 %copy-start.11 = (bf16[6,28,1,256]{3,2,1,0:T(2,128)(2,1)}, bf16[6,28,1,256]{3,2,1,0:T(2,128)(2,1)S(1)}, u32[]{:S(2)}) copy-start(bf16[6,28,1,256]{3,2,1,0:T(2,128)(2,1)S(1)} %collective-permute-done.4) | copy-start | bytes 258052
  62.7 2.5 copy-start.22
  62.7 2.5 copy-start.24
  72.3 12.3 %copy-start.1 = (f32[4,16,8,3,256]{4,1,3,2,0:T(8,128)}, f32[4,16,8,3,256]{4,1,3,2,0:T(8,128)S(1)}, u32[]{:S(2)}) copy-start(f32[4,16,8,3,256]{4,1,3,2,0:T(8,128)S(1)} %copy.51) | copy-start | bytes 4718596
  84.6 3.0 copy-start.6
  104.9 3.5 %copy-start.7 = (bf16[1,6,18,18,256]{4,2,3,1,0:T(8,128)(2,1)S(1)}, bf16[1,6,18,18,256]{4,2,3,1,0:T(8,128)(2,1)}, u32[]{:S(2)}) copy-start(bf16[1,6,18,18,256]{4,2,3,1,0:T(8,128)(2,1)} %get-tuple-element.23) | copy-start | bytes 2985988
  104.9 3.4 %copy-start.8 = (bf16[1,4,16,16,256]{4,2,3,1,0:T(8,128)(2,1)S(1)}, bf16[1,4,16,16,256]{4,2,3,1,0:T(8,128)(2,1)}, u32[]{:S(2)}) copy-start(bf16[1,4,16,16,256]{4,2,3,1,0:T(8,128)(2,1)} %get-tuple-element.42) | copy-start | bytes 1572868
  132.3 9.2 %collective-permute-start.11 = (bf16[2,16,16,256]{3,1,2,0:T(8,128)(2,1)S(1)}, bf16[2,16,16,256]{3,1,2,0:T(8,128)(2,1)S(1)}, u32[]{:S(2)}, u32[]{:S(2)}) collective-permute-start(bf16[2,16,16,256]{3,1,2,0:T(8,128)(2,1)S(1)} %slice.161), channel_id=1, source_target_pairs={{32,0},{64,32},{96,64},{33,1},{65,33},{97,65},{34,2},{66,34},{98,6... | collective-permute-start | bytes 786440 | tf_op jit(solution)/shard_map/ppermute | solution.py:14
  134.3 12.6 %collective-permute-start.6 = (bf16[2,16,16,256]{3,1,2,0:T(8,128)(2,1)S(1)}, bf16[2,16,16,256]{3,1,2,0:T(8,128)(2,1)S(1)}, u32[]{:S(2)}, u32[]{:S(2)}) collective-permute-start(bf16[2,16,16,256]{3,1,2,0:T(8,128)(2,1)S(1)} %slice.154), channel_id=1, source_target_pairs={{0,32},{32,64},{64,96},{1,33},{33,65},{65,97},{2,34},{34,66},{66,9... | collective-permute-start | bytes 786440 | tf_op jit(solution)/shard_map/ppermute | solution.py:14
  141.7 10.8 %collective-permute-start.12 = (bf16[6,1,16,256]{3,1,2,0:T(2,128)(2,1)S(1)}, bf16[6,1,16,256]{3,1,2,0:T(2,128)(2,1)S(1)}, u32[]{:S(2)}, u32[]{:S(2)}) collective-permute-start(bf16[6,1,16,256]{3,1,2,0:T(2,128)(2,1)S(1)} %get-tuple-element.33), channel_id=1, source_target_pairs={{0,4},{4,8},{8,12},{12,16},{16,20},{20,24},{24,28},{1,5},{5,9},{9,... | collective-permute-start | bytes 147464 | tf_op jit(solution)/shard_map/ppermute | solution.py:25
  145.6 7.0 %collective-permute-start.13 = (bf16[6,1,16,256]{3,1,2,0:T(2,128)(2,1)S(1)}, bf16[6,1,16,256]{3,1,2,0:T(2,128)(2,1)S(1)}, u32[]{:S(2)}, u32[]{:S(2)}) collective-permute-start(bf16[6,1,16,256]{3,1,2,0:T(2,128)(2,1)S(1)} %get-tuple-element.34), channel_id=1, source_target_pairs={{4,0},{8,4},{12,8},{16,12},{20,16},{24,20},{28,24},{5,1},{9,5},{13... | collective-permute-start | bytes 147464 | tf_op jit(solution)/shard_map/ppermute | solution.py:27
  147.1 10.0 %collective-permute-start.7 = (bf16[6,1,16,256]{3,1,2,0:T(2,128)(2,1)S(1)}, bf16[6,1,16,256]{3,1,2,0:T(2,128)(2,1)S(1)}, u32[]{:S(2)}, u32[]{:S(2)}) collective-permute-start(bf16[6,1,16,256]{3,1,2,0:T(2,128)(2,1)S(1)} %get-tuple-element.35), channel_id=1, source_target_pairs={{0,4},{4,8},{8,12},{12,16},{16,20},{20,24},{24,28},{1,5},{5,9},{9,... | collective-permute-start | bytes 147464 | tf_op jit(solution)/shard_map/ppermute | solution.py:25
  151.2 8.7 %collective-permute-start.8 = (bf16[6,1,16,256]{3,1,2,0:T(2,128)(2,1)S(1)}, bf16[6,1,16,256]{3,1,2,0:T(2,128)(2,1)S(1)}, u32[]{:S(2)}, u32[]{:S(2)}) collective-permute-start(bf16[6,1,16,256]{3,1,2,0:T(2,128)(2,1)S(1)} %get-tuple-element.36), channel_id=1, source_target_pairs={{4,0},{8,4},{12,8},{16,12},{20,16},{24,20},{28,24},{5,1},{9,5},{13... | collective-permute-start | bytes 147464 | tf_op jit(solution)/shard_map/ppermute | solution.py:27
  152.6 11.3 %collective-permute-start.14 = (bf16[6,18,1,256]{3,1,2,0:T(8,128)(2,1)S(1)}, bf16[6,18,1,256]{3,1,2,0:T(8,128)(2,1)S(1)}, u32[]{:S(2)}, u32[]{:S(2)}) collective-permute-start(bf16[6,18,1,256]{3,1,2,0:T(8,128)(2,1)S(1)} %get-tuple-element.29), channel_id=1, source_target_pairs={{0,1},{1,2},{2,3},{4,5},{5,6},{6,7},{8,9},{9,10},{10,11},{12,13},{... | collective-permute-start | bytes 165896 | tf_op jit(solution)/shard_map/ppermute | solution.py:25
  155.8 8.2 %collective-permute-start.15 = (bf16[6,18,1,256]{3,1,2,0:T(8,128)(2,1)S(1)}, bf16[6,18,1,256]{3,1,2,0:T(8,128)(2,1)S(1)}, u32[]{:S(2)}, u32[]{:S(2)}) collective-permute-start(bf16[6,18,1,256]{3,1,2,0:T(8,128)(2,1)S(1)} %get-tuple-element.30), channel_id=1, source_target_pairs={{1,0},{2,1},{3,2},{5,4},{6,5},{7,6},{9,8},{10,9},{11,10},{13,12},{... | collective-permute-start | bytes 165896 | tf_op jit(solution)/shard_map/ppermute | solution.py:27
  160.0 5.2 %collective-permute-start.9 = (bf16[6,18,1,256]{3,1,2,0:T(8,128)(2,1)S(1)}, bf16[6,18,1,256]{3,1,2,0:T(8,128)(2,1)S(1)}, u32[]{:S(2)}, u32[]{:S(2)}) collective-permute-start(bf16[6,18,1,256]{3,1,2,0:T(8,128)(2,1)S(1)} %get-tuple-element.31), channel_id=1, source_target_pairs={{0,1},{1,2},{2,3},{4,5},{5,6},{6,7},{8,9},{9,10},{10,11},{12,13},{... | collective-permute-start | bytes 165896 | tf_op jit(solution)/shard_map/ppermute | solution.py:25
  162.2 6.1 %collective-permute-start.10 = (bf16[6,18,1,256]{3,1,2,0:T(8,128)(2,1)S(1)}, bf16[6,18,1,256]{3,1,2,0:T(8,128)(2,1)S(1)}, u32[]{:S(2)}, u32[]{:S(2)}) collective-permute-start(bf16[6,18,1,256]{3,1,2,0:T(8,128)(2,1)S(1)} %get-tuple-element.32), channel_id=1, source_target_pairs={{1,0},{2,1},{3,2},{5,4},{6,5},{7,6},{9,8},{10,9},{11,10},{13,12},{... | collective-permute-start | bytes 165896 | tf_op jit(solution)/shard_map/ppermute | solution.py:27
  169.3 2.2 copy-start.23
  169.3 2.2 copy-start.25
  (11 other events, 16.5 us)
Sparse Core Ops, SparseCore 0:
  127.9 180.0 all-reduce.2

commit v7 on v6

--- a/solution.py
+++ b/solution.py
@@ -134,7 +134,9 @@
     )
     dropped = (jax.nn.silu(pre_first) * scaling).astype(jnp.bfloat16)
     dropped_ext = face_cells(with_earlier(dropped))
-    grad_second = flipped(weight_gradient(upstream_ext, dropped))
+    grad_second = jnp.swapaxes(
+        weight_gradient(upstream_ext[::-1, ::-1, ::-1], dropped[::-1, ::-1, ::-1]), 3, 4
+    )
     mixed = (cells_here.astype(jnp.float32) + convolve(dropped_ext, w_second) + b_second).astype(
         jnp.bfloat16
     )

time: 335 us -> 345 us (1.030)
  local copies, waits for them, and re-layouts: 62 us -> 67.8 us
  waiting for transfers between devices: 128 us -> 123 us
  other arithmetic: 17.9 us -> 22.4 us
    another operation x0 -> x1, matrix products: none -> 19.4 us  [local(): jnp.swapaxes(weight_gradient(upstream_ext[::-1, ::-1, ::-1], dropped[::-1...]
    transpose x2 -> x1, matrix products: 36.7 us -> 19.4 us  [weight_gradient(): return jnp.transpose(summed, (1, 2, 3, 0, 4))]
    rev x0 -> x2, local copies, waits for them, and re-layouts: none -> 6.71 us  [the longest x1 4.85 us: local(): upstream_ext[::-1, ::-1, ::-1]]
    convert_element_type x1 -> x2, other arithmetic: 2.42 us -> 8.31 us  [local(): (grad_dropped * scaling * sigma * (1.0 + pre_first * (1.0 - sigma))).asty...]
    ppermute x2, waiting for transfers between devices: 3.76 us -> 0.01 us  [faces_together(): from_next = lax.ppermute(head, axis, [(i + 1, i) for i in range(ends)])]
    concatenate x1 -> x2, other arithmetic: 0.31 us -> 3.95 us  [faces_together(): placed.append(jnp.concatenate([before, f, after], axis=dim))]
    unnamed x58 -> x44, local copies, waits for them, and re-layouts: 24.3 us -> 23.5 us
  transfers between devices with their start and end apart: 17 -> 17, of which waited for: 8 -> 7; matrix products, arithmetic and copies ran while one was open for 12% -> 11% of each run, Pallas kernels for 0% -> 0%
where the time goes in v7:
time: 345 us; the launch traced here: 339 us
  waiting for transfers between devices  123 us (36%)
  local copies, waits for them, and re-layouts  67.8 us (20%)
  matrix products  63.2 us (18%)
  starting transfers between devices  47.3 us (14%)
  other arithmetic  22.4 us (6%)
  between operations  14.9 us (4%)
    psum x1, waiting for transfers between devices, local(): grad_first, grad_second = lax.psum((grad_first, grad_second), ALL)  113 us
    conv_general_dilated x4, matrix products, convolve(): lax.conv_general_dilated(extended[None], weight, (1, 1, 1), 'VALID', dime...  24.5 us
    unnamed x44, local copies, waits for them, and re-layouts  23.5 us
    transpose x1, matrix products, weight_gradient(): return jnp.transpose(summed, (1, 2, 3, 0, 4))  19.4 us
    another operation x1, matrix products, local(): jnp.swapaxes(weight_gradient(upstream_ext[::-1, ::-1, ::-1], dropped[::-1...  19.4 us
    ppermute x4, starting transfers between devices, extended_2(): lax.ppermute(tail, axis, [(i, (i + 1) % count) for i in range(ends)])  15.8 us
    ppermute x4, starting transfers between devices, shifted(): return lax.ppermute(block, axis, route)  15.2 us
    conv_general_dilated x13, local copies, waits for them, and re-layouts, convolve(): lax.conv_general_dilated(extended[None], weight, (1, 1, 1), 'VALID', dime...  10.7 us
  transfers between devices with their start and end apart: 17, of which 7 were waited for; matrix products, arithmetic and copies ran while one was open for 11% of the time, Pallas kernels for 0%

profile of v7, /device:TPU:1, one launch (start us, length us, event | category | flops | bytes accessed | tf_op | source)
XLA Modules:
  0.0 338.7 jit_solution(622023824185726739)
XLA Ops:
  8.9 6.2 %collective-permute-start = (bf16[2,8,8,256]{3,2,1,0:T(8,128)(2,1)}, bf16[2,8,8,256]{3,2,1,0:T(8,128)(2,1)}, u32[]{:S(2)}, u32[]{:S(2)}) collective-permute-start(bf16[2,8,8,256]{3,2,1,0:T(8,128)(2,1)} %slice.97), channel_id=1, source_target_pairs={{0,32},{32,64},{64,96},{1,33},{33,65},{65,97},{2,34},{34,66},{66,9... | collective-permute-start | bytes 196616 | tf_op jit(solution)/shard_map/ppermute | solution.py:14
  16.7 1.9 collective-permute-start.1
  23.6 2.6 collective-permute-done.1
  30.1 4.2 %collective-permute-start.2 = (bf16[6,1,24,256]{3,2,1,0:T(8,128)(2,1)S(1)}, bf16[6,1,24,256]{3,2,1,0:T(8,128)(2,1)S(1)}, u32[]{:S(2)}, u32[]{:S(2)}) collective-permute-start(bf16[6,1,24,256]{3,2,1,0:T(8,128)(2,1)S(1)} %pad_maximum_fusion.19), channel_id=1, source_target_pairs={{0,4},{4,8},{8,12},{12,16},{16,20},{20,24},{24,28},{1,5},{5,9},{9,... | collective-permute-start | bytes 221192 | tf_op jit(solution)/shard_map/ppermute | solution.py:104
  38.6 4.0 %collective-permute-start.4 = (bf16[6,28,1,256]{3,1,2,0:T(8,128)(2,1)S(1)}, bf16[6,28,1,256]{3,1,2,0:T(8,128)(2,1)S(1)}, u32[]{:S(2)}, u32[]{:S(2)}) collective-permute-start(bf16[6,28,1,256]{3,1,2,0:T(8,128)(2,1)S(1)} %pad_maximum_fusion.9), channel_id=1, source_target_pairs={{0,1},{1,2},{2,3},{4,5},{5,6},{6,7},{8,9},{9,10},{10,11},{12,13},{... | collective-permute-start | bytes 258056 | tf_op jit(solution)/shard_map/ppermute | solution.py:104
  46.6 2.6 reshape.80
  49.3 3.6 %pad_maximum_fusion = (bf16[6,18,18,256]{3,2,1,0:T(8,128)(2,1)}, bf16[6,18,1,18,256]{4,3,1,0,2:T(8,128)(2,1)}) fusion(bf16[6,18,1,256]{3,2,1,0:T(2,128)(2,1)} %copy.90, bf16[6,1,16,256]{3,2,1,0:T(8,128)(2,1)} %copy-done.11, bf16[6,16,16,256]{3,2,1,0:T(8,128)(2,1)} %constant_dynamic-update-slice_fusion.2, bf16[6,1,16,256]{3,2,1,0:T(8,128)(2,1)} %copy-done.12, ...), kind=kLoop, calls=%fused_computation.48 | loop fusion | flops 4976640 | bytes 2985984 | tf_op jit(solution)/shard_map/concatenate | solution.py:112
  52.9 4.9 %rev.8 = bf16[6,18,18,256]{3,2,1,0:T(8,128)(2,1)} reverse(bf16[6,18,18,256]{3,2,1,0:T(8,128)(2,1)} %get-tuple-element.28), dimensions={0,1,2} | reverse | bytes 1990656 | tf_op jit(solution)/shard_map/rev | solution.py:138
  57.8 2.6 pad.4
  60.3 5.1 %reshape.99 = bf16[6,18,1,8,3,256]{5,4,3,1,0,2:T(4,128)(2,1)} reshape(bf16[6,18,1,24,256]{4,3,1,0,2:T(8,128)(2,1)} %pad.4) | data formatting | bytes 2654208 | tf_op jit(solution)/shard_map/conv_general_dilated | solution.py:55
  65.5 2.0 copy.92
  68.0 5.9 %fusion.42 = f32[4,16,8,3,256]{4,2,3,1,0:T(8,128)S(1)} fusion(bf16[3,3,3,256,256]{4,3,2,1,0:T(8,128)(2,1)S(1)} %copy-done.15, bf16[6,18,1,7,2,256]{5,3,4,1,0,2:T(8,128)(2,1)S(1)} %slice.158, bf16[6,18,1,8,3,256]{5,3,4,1,0,2:T(8,128)(2,1)S(1)} %copy.92, pred[8,3]{0,1:T(4,128)(4,1)S(1)} %copy-done.17), kind=kOutput, calls=%fused_computation.43 | convolution fusion | flops 5442846720 | bytes 7213080 | tf_op jit(solution)/shard_map/conv_general_dilated | solution.py:55
  75.1 1.9 slice_bitcast_fusion.1
  77.9 6.3 %add_divide_fusion = (f32[4,16,8,3,256]{4,2,3,1,0:T(8,128)S(1)}, f32[4,16,8,3,256]{4,2,3,1,0:T(8,128)S(1)}, f32[4,16,8,3,256]{4,2,3,1,0:T(8,128)S(1)}) fusion(f32[256]{0:T(256)S(1)} %copy-done.13, bf16[3,3,3,256,256]{4,3,2,1,0:T(8,128)(2,1)S(1)} %copy-done, bf16[6,18,1,7,2,256]{5,3,4,1,0,2:T(8,128)(2,1)S(1)} %slice.151, ...), kind=kOutput, calls=%fused_computation.34 | convolution fusion | flops 5445599232 | bytes 10359832 | tf_op jit(solution)/shard_map/conv_general_dilated | solution.py:55
  87.9 3.4 %fusion.55 = (bf16[4,16,16,256]{3,1,2,0:T(8,128)(2,1)}, bf16[4,16,16,256]{3,1,2,0:T(8,128)(2,1)}) fusion(f32[4,16,1,24,256]{4,1,3,0,2:T(8,128)S(1)} %bitcast.98, f32[4,16,1,24,256]{4,1,3,0,2:T(8,128)S(1)} %bitcast.107, s32[]{:T(128)} %bitcast.7, s32[]{:T(128)} %bitcast.6, s32[16]{0:T(128)S(1)} %get-tuple-element.49, s32[16]{0:T(128)S(1)} %get-tuple-element.50, ...), kind=kLoop, calls=%fused_computation.59 | loop fusion | flops 8650752 | bytes 3146904 | tf_op jit(solution)/shard_map/convert_element_type | solution.py:145
  93.2 4.9 %fusion.67 = bf16[1,4,16,16,256]{4,2,3,1,0:T(8,128)(2,1)} fusion(f32[4,16,1,24,256]{4,1,3,0,2:T(8,128)} %bitcast.106, f32[4,16,1,24,256]{4,1,3,0,2:T(8,128)} %bitcast.105, f32[4,16,1,24,256]{4,1,3,0,2:T(8,128)} %bitcast.99, s32[]{:T(128)} %bitcast.7, s32[]{:T(128)} %bitcast.6, s32[16]{0:T(128)S(1)} %get-tuple-element.49, s32[16]{0:T(128)S(1)} %get-tuple-element.50, ...), kind=kLoop, calls=%fused_computation.72 | loop fusion | flops 6029312 | bytes 3670168 | tf_op jit(solution)/shard_map/convert_element_type | solution.py:145
  98.1 19.4 %fusion.34 = f32[3,3,3,256,256]{3,4,2,1,0:T(8,128)} fusion(bf16[1,6,18,18,256]{4,3,2,1,0:T(8,128)(2,1)S(1)} %bitcast.110, bf16[1,4,16,16,256]{4,2,3,1,0:T(8,128)(2,1)S(1)} %bitcast.111), kind=kOutput, calls=%fused_computation.31 | convolution fusion | flops 3623878656 | bytes 8597504 | tf_op jit(solution)/shard_map/transpose;transpose | solution.py:137
  117.5 19.4 %fusion.32 = f32[3,3,3,256,256]{4,3,2,1,0:T(8,128)} fusion(bf16[1,6,18,18,256]{4,2,3,1,0:T(8,128)(2,1)S(1)} %copy-done.8, bf16[1,4,16,16,256]{4,2,3,1,0:T(8,128)(2,1)S(1)} %copy-done.9), kind=kOutput, calls=%fused_computation.29 | convolution fusion | flops 3623878656 | bytes 8597504 | tf_op jit(solution)/shard_map/transpose | solution.py:78
  138.0 1.9 collective-permute-start.11
  140.9 5.1 %collective-permute-start.6 = (bf16[2,16,16,256]{3,1,2,0:T(8,128)(2,1)S(1)}, bf16[2,16,16,256]{3,1,2,0:T(8,128)(2,1)S(1)}, u32[]{:S(2)}, u32[]{:S(2)}) collective-permute-start(bf16[2,16,16,256]{3,1,2,0:T(8,128)(2,1)S(1)} %slice.153), channel_id=1, source_target_pairs={{0,32},{32,64},{64,96},{1,33},{33,65},{65,97},{2,34},{34,66},{66,9... | collective-permute-start | bytes 786440 | tf_op jit(solution)/shard_map/ppermute | solution.py:14
  148.4 3.7 %collective-permute-start.12 = (bf16[6,1,16,256]{3,1,2,0:T(2,128)(2,1)S(1)}, bf16[6,1,16,256]{3,1,2,0:T(2,128)(2,1)S(1)}, u32[]{:S(2)}, u32[]{:S(2)}) collective-permute-start(bf16[6,1,16,256]{3,1,2,0:T(2,128)(2,1)S(1)} %get-tuple-element.36), channel_id=1, source_target_pairs={{0,4},{4,8},{8,12},{12,16},{16,20},{20,24},{24,28},{1,5},{5,9},{9,... | collective-permute-start | bytes 147464 | tf_op jit(solution)/shard_map/ppermute | solution.py:25
  153.6 4.2 %collective-permute-start.7 = (bf16[6,1,16,256]{3,1,2,0:T(2,128)(2,1)S(1)}, bf16[6,1,16,256]{3,1,2,0:T(2,128)(2,1)S(1)}, u32[]{:S(2)}, u32[]{:S(2)}) collective-permute-start(bf16[6,1,16,256]{3,1,2,0:T(2,128)(2,1)S(1)} %get-tuple-element.38), channel_id=1, source_target_pairs={{0,4},{4,8},{8,12},{12,16},{16,20},{20,24},{24,28},{1,5},{5,9},{9,... | collective-permute-start | bytes 147464 | tf_op jit(solution)/shard_map/ppermute | solution.py:25
  159.2 3.8 %collective-permute-start.14 = (bf16[6,18,1,256]{3,1,2,0:T(8,128)(2,1)S(1)}, bf16[6,18,1,256]{3,1,2,0:T(8,128)(2,1)S(1)}, u32[]{:S(2)}, u32[]{:S(2)}) collective-permute-start(bf16[6,18,1,256]{3,1,2,0:T(8,128)(2,1)S(1)} %get-tuple-element.30), channel_id=1, source_target_pairs={{0,1},{1,2},{2,3},{4,5},{5,6},{6,7},{8,9},{9,10},{10,11},{12,13},{... | collective-permute-start | bytes 165896 | tf_op jit(solution)/shard_map/ppermute | solution.py:25
  166.1 4.1 %collective-permute-start.9 = (bf16[6,18,1,256]{3,1,2,0:T(8,128)(2,1)S(1)}, bf16[6,18,1,256]{3,1,2,0:T(8,128)(2,1)S(1)}, u32[]{:S(2)}, u32[]{:S(2)}) collective-permute-start(bf16[6,18,1,256]{3,1,2,0:T(8,128)(2,1)S(1)} %get-tuple-element.32), channel_id=1, source_target_pairs={{0,1},{1,2},{2,3},{4,5},{5,6},{6,7},{8,9},{9,10},{10,11},{12,13},{... | collective-permute-start | bytes 165896 | tf_op jit(solution)/shard_map/ppermute | solution.py:25
  173.2 3.0 collective-permute-done.10
  179.3 6.2 %fusion.39 = f32[4,16,8,3,256]{4,2,3,1,0:T(8,128)S(1)} fusion(bf16[3,3,3,256,256]{4,3,2,1,0:T(8,128)(2,1)S(1)} %copy-done.16, bf16[6,18,1,7,2,256]{5,3,4,1,0,2:T(8,128)(2,1)S(1)} %slice.154, bf16[6,18,1,8,3,256]{5,3,4,1,0,2:T(8,128)(2,1)S(1)} %copy.86, pred[8,3]{0,1:T(4,128)(4,1)S(1)} %copy-done.18), kind=kOutput, calls=%fused_computation.42 | convolution fusion | flops 5442846720 | bytes 7213080 | tf_op jit(solution)/shard_map/conv_general_dilated | solution.py:55
  188.8 6.1 %fusion.36 = f32[4,16,8,3,256]{4,2,3,1,0:T(8,128)S(1)} fusion(bf16[3,3,3,256,256]{4,3,2,1,0:T(8,128)(2,1)S(1)} %copy-done, bf16[6,18,1,7,2,256]{5,3,4,1,0,2:T(8,128)(2,1)S(1)} %slice.161, bf16[6,18,1,8,3,256]{5,3,4,1,0,2:T(8,128)(2,1)S(1)} %copy.96, pred[8,3]{0,1:T(4,128)(4,1)S(1)} %copy-done.18), kind=kOutput, calls=%fused_computation.41 | convolution fusion | flops 5442846720 | bytes 7213080 | tf_op jit(solution)/shard_map/conv_general_dilated | solution.py:55
  197.2 2.8 reshape.82
  200.0 2.7 reduce_sum.9
  204.3 112.6 %all-reduce.3.cloned.1.call-done = (f32[3,3,3,256,256]{4,3,2,1,0:T(8,128)}, f32[3,3,3,256,256]{3,4,2,1,0:T(8,128)}) async-done(((f32[3,3,3,256,256]{4,3,2,1,0:T(8,128)}, f32[3,3,3,256,256]{3,4,2,1,0:T(8,128)}), (f32[3,3,3,256,256]{4,3,2,1,0:T(8,128)}, f32[3,3,3,256,256]{3,4,2,1,0:T(8,128)})) %all-reduce.3.cloned.1.call-update) | async-done | bytes 14155792 | tf_op jit(solution)/shard_map/psum | solution.py:157
  316.9 8.0 %copy.108 = f32[3,3,3,256,256]{4,3,2,1,0:T(8,128)} copy(f32[3,3,3,256,256]{3,4,2,1,0:T(8,128)} %get-tuple-element.21) | data formatting | bytes 14155776
  324.9 6.7 %copy.132 = f32[3,3,3,256,256]{4,3,2,1,0:T(8,128)} copy(f32[3,3,3,256,256]{4,3,2,1,0:T(8,128)} %get-tuple-element.53) | data formatting | bytes 14155776
  (126 shorter events, 51.9 us)
Async XLA Ops:
  7.2 70.6 %copy-start = (bf16[3,3,3,256,256]{4,3,2,1,0:T(8,128)(2,1)S(1)}, bf16[3,3,3,256,256]{4,3,2,1,0:T(8,128)(2,1)}, u32[]{:S(2)}) copy-start(bf16[3,3,3,256,256]{4,3,2,1,0:T(8,128)(2,1)} %param.8) | copy-start | bytes 10616836
  7.2 309.7 %all-reduce.3.cloned.1.call-start = ((), (), s32[]{:S(2)}) async-start(), calls=%async_computation | async-start | bytes 28311552 | tf_op jit(solution)/shard_map/psum | solution.py:157
  8.9 13.0 %collective-permute-start = (bf16[2,8,8,256]{3,2,1,0:T(8,128)(2,1)}, bf16[2,8,8,256]{3,2,1,0:T(8,128)(2,1)}, u32[]{:S(2)}, u32[]{:S(2)}) collective-permute-start(bf16[2,8,8,256]{3,2,1,0:T(8,128)(2,1)} %slice.97), channel_id=1, source_target_pairs={{0,32},{32,64},{64,96},{1,33},{33,65},{65,97},{2,34},{34,66},{66,9... | collective-permute-start | bytes 196616 | tf_op jit(solution)/shard_map/ppermute | solution.py:14
  16.7 9.5 %collective-permute-start.1 = (bf16[2,16,16,256]{3,2,1,0:T(8,128)(2,1)}, bf16[2,16,16,256]{3,2,1,0:T(8,128)(2,1)}, u32[]{:S(2)}, u32[]{:S(2)}) collective-permute-start(bf16[2,16,16,256]{3,2,1,0:T(8,128)(2,1)} %slice.99), channel_id=1, source_target_pairs={{32,0},{64,32},{96,64},{33,1},{65,33},{97,65},{34,2},{66,34},{98,6... | collective-permute-start | bytes 786440 | tf_op jit(solution)/shard_map/ppermute | solution.py:14
  28.8 5.5 %collective-permute-start.3 = (bf16[6,1,24,256]{3,2,1,0:T(8,128)(2,1)S(1)}, bf16[6,1,24,256]{3,2,1,0:T(8,128)(2,1)S(1)}, u32[]{:S(2)}, u32[]{:S(2)}) collective-permute-start(bf16[6,1,24,256]{3,2,1,0:T(8,128)(2,1)S(1)} %pad_maximum_fusion.20), channel_id=1, source_target_pairs={{4,0},{8,4},{12,8},{16,12},{20,16},{24,20},{28,24},{5,1},{9,5},{13... | collective-permute-start | bytes 221192 | tf_op jit(solution)/shard_map/ppermute | solution.py:105
  30.1 5.6 %collective-permute-start.2 = (bf16[6,1,24,256]{3,2,1,0:T(8,128)(2,1)S(1)}, bf16[6,1,24,256]{3,2,1,0:T(8,128)(2,1)S(1)}, u32[]{:S(2)}, u32[]{:S(2)}) collective-permute-start(bf16[6,1,24,256]{3,2,1,0:T(8,128)(2,1)S(1)} %pad_maximum_fusion.19), channel_id=1, source_target_pairs={{0,4},{4,8},{8,12},{12,16},{16,20},{20,24},{24,28},{1,5},{5,9},{9,... | collective-permute-start | bytes 221192 | tf_op jit(solution)/shard_map/ppermute | solution.py:104
  35.8 9.5 %copy-start.11 = (bf16[6,1,16,256]{3,2,1,0:T(8,128)(2,1)}, bf16[6,1,16,256]{3,2,1,0:T(8,128)(2,1)S(1)}, u32[]{:S(2)}) copy-start(bf16[6,1,16,256]{3,2,1,0:T(8,128)(2,1)S(1)} %slice.146) | copy-start | bytes 147460
  35.8 9.5 %copy-start.12 = (bf16[6,1,16,256]{3,2,1,0:T(8,128)(2,1)}, bf16[6,1,16,256]{3,2,1,0:T(8,128)(2,1)S(1)}, u32[]{:S(2)}) copy-start(bf16[6,1,16,256]{3,2,1,0:T(8,128)(2,1)S(1)} %slice.145) | copy-start | bytes 147460
  37.2 5.4 %collective-permute-start.5 = (bf16[6,28,1,256]{3,1,2,0:T(8,128)(2,1)S(1)}, bf16[6,28,1,256]{3,1,2,0:T(8,128)(2,1)S(1)}, u32[]{:S(2)}, u32[]{:S(2)}) collective-permute-start(bf16[6,28,1,256]{3,1,2,0:T(8,128)(2,1)S(1)} %pad_maximum_fusion.10), channel_id=1, source_target_pairs={{1,0},{2,1},{3,2},{5,4},{6,5},{7,6},{9,8},{10,9},{11,10},{13,12},{... | collective-permute-start | bytes 258056 | tf_op jit(solution)/shard_map/ppermute | solution.py:105
  38.6 5.6 %collective-permute-start.4 = (bf16[6,28,1,256]{3,1,2,0:T(8,128)(2,1)S(1)}, bf16[6,28,1,256]{3,1,2,0:T(8,128)(2,1)S(1)}, u32[]{:S(2)}, u32[]{:S(2)}) collective-permute-start(bf16[6,28,1,256]{3,1,2,0:T(8,128)(2,1)S(1)} %pad_maximum_fusion.9), channel_id=1, source_target_pairs={{0,1},{1,2},{2,3},{4,5},{5,6},{6,7},{8,9},{9,10},{10,11},{12,13},{... | collective-permute-start | bytes 258056 | tf_op jit(solution)/shard_map/ppermute | solution.py:104
  65.5 2.5 copy-start.15
  65.5 2.5 copy-start.17
  75.0 12.9 %copy-start.3 = (f32[4,16,8,3,256]{4,1,3,2,0:T(8,128)}, f32[4,16,8,3,256]{4,1,3,2,0:T(8,128)S(1)}, u32[]{:S(2)}) copy-start(f32[4,16,8,3,256]{4,1,3,2,0:T(8,128)S(1)} %copy.93) | copy-start | bytes 4718596
  75.1 2.0 copy-start.4
  93.2 4.9 %copy-start.7 = (bf16[6,18,18,256]{3,2,1,0:T(8,128)(2,1)S(1)}, bf16[6,18,18,256]{3,2,1,0:T(8,128)(2,1)}, u32[]{:S(2)}) copy-start(bf16[6,18,18,256]{3,2,1,0:T(8,128)(2,1)} %rev.8) | copy-start | bytes 2985988
  93.2 4.9 %copy-start.10 = (bf16[4,16,16,256]{3,1,2,0:T(8,128)(2,1)S(1)}, bf16[4,16,16,256]{3,1,2,0:T(8,128)(2,1)}, u32[]{:S(2)}) copy-start(bf16[4,16,16,256]{3,1,2,0:T(8,128)(2,1)} %rev.9) | copy-start | bytes 1572868
  98.1 19.4 %copy-start.8 = (bf16[1,6,18,18,256]{4,2,3,1,0:T(8,128)(2,1)S(1)}, bf16[1,6,18,18,256]{4,2,3,1,0:T(8,128)(2,1)}, u32[]{:S(2)}) copy-start(bf16[1,6,18,18,256]{4,2,3,1,0:T(8,128)(2,1)} %get-tuple-element.26) | copy-start | bytes 2985988
  98.1 19.4 %copy-start.9 = (bf16[1,4,16,16,256]{4,2,3,1,0:T(8,128)(2,1)S(1)}, bf16[1,4,16,16,256]{4,2,3,1,0:T(8,128)(2,1)}, u32[]{:S(2)}) copy-start(bf16[1,4,16,16,256]{4,2,3,1,0:T(8,128)(2,1)} %fusion.67) | copy-start | bytes 1572868
  136.9 16.5 %copy-start.1 = (bf16[4,16,16,256]{3,1,2,0:T(8,128)(2,1)S(1)}, bf16[4,16,16,256]{3,1,2,0:T(8,128)(2,1)}, u32[]{:S(2)}) copy-start(bf16[4,16,16,256]{3,1,2,0:T(8,128)(2,1)} %get-tuple-element.23) | copy-start | bytes 1572868
  136.9 22.2 %copy-start.2 = (bf16[4,16,16,256]{3,1,2,0:T(8,128)(2,1)S(1)}, bf16[4,16,16,256]{3,1,2,0:T(8,128)(2,1)}, u32[]{:S(2)}) copy-start(bf16[4,16,16,256]{3,1,2,0:T(8,128)(2,1)} %get-tuple-element.22) | copy-start | bytes 1572868
  138.0 9.2 %collective-permute-start.11 = (bf16[2,16,16,256]{3,1,2,0:T(8,128)(2,1)S(1)}, bf16[2,16,16,256]{3,1,2,0:T(8,128)(2,1)S(1)}, u32[]{:S(2)}, u32[]{:S(2)}) collective-permute-start(bf16[2,16,16,256]{3,1,2,0:T(8,128)(2,1)S(1)} %slice.160), channel_id=1, source_target_pairs={{32,0},{64,32},{96,64},{33,1},{65,33},{97,65},{34,2},{66,34},{98,6... | collective-permute-start | bytes 786440 | tf_op jit(solution)/shard_map/ppermute | solution.py:14
  140.9 12.5 %collective-permute-start.6 = (bf16[2,16,16,256]{3,1,2,0:T(8,128)(2,1)S(1)}, bf16[2,16,16,256]{3,1,2,0:T(8,128)(2,1)S(1)}, u32[]{:S(2)}, u32[]{:S(2)}) collective-permute-start(bf16[2,16,16,256]{3,1,2,0:T(8,128)(2,1)S(1)} %slice.153), channel_id=1, source_target_pairs={{0,32},{32,64},{64,96},{1,33},{33,65},{65,97},{2,34},{34,66},{66,9... | collective-permute-start | bytes 786440 | tf_op jit(solution)/shard_map/ppermute | solution.py:14
  148.4 10.7 %collective-permute-start.12 = (bf16[6,1,16,256]{3,1,2,0:T(2,128)(2,1)S(1)}, bf16[6,1,16,256]{3,1,2,0:T(2,128)(2,1)S(1)}, u32[]{:S(2)}, u32[]{:S(2)}) collective-permute-start(bf16[6,1,16,256]{3,1,2,0:T(2,128)(2,1)S(1)} %get-tuple-element.36), channel_id=1, source_target_pairs={{0,4},{4,8},{8,12},{12,16},{16,20},{20,24},{24,28},{1,5},{5,9},{9,... | collective-permute-start | bytes 147464 | tf_op jit(solution)/shard_map/ppermute | solution.py:25
  152.1 7.0 %collective-permute-start.13 = (bf16[6,1,16,256]{3,1,2,0:T(2,128)(2,1)S(1)}, bf16[6,1,16,256]{3,1,2,0:T(2,128)(2,1)S(1)}, u32[]{:S(2)}, u32[]{:S(2)}) collective-permute-start(bf16[6,1,16,256]{3,1,2,0:T(2,128)(2,1)S(1)} %get-tuple-element.37), channel_id=1, source_target_pairs={{4,0},{8,4},{12,8},{16,12},{20,16},{24,20},{28,24},{5,1},{9,5},{13... | collective-permute-start | bytes 147464 | tf_op jit(solution)/shard_map/ppermute | solution.py:27
  153.6 10.7 %collective-permute-start.7 = (bf16[6,1,16,256]{3,1,2,0:T(2,128)(2,1)S(1)}, bf16[6,1,16,256]{3,1,2,0:T(2,128)(2,1)S(1)}, u32[]{:S(2)}, u32[]{:S(2)}) collective-permute-start(bf16[6,1,16,256]{3,1,2,0:T(2,128)(2,1)S(1)} %get-tuple-element.38), channel_id=1, source_target_pairs={{0,4},{4,8},{8,12},{12,16},{16,20},{20,24},{24,28},{1,5},{5,9},{9,... | collective-permute-start | bytes 147464 | tf_op jit(solution)/shard_map/ppermute | solution.py:25
  157.8 8.2 %collective-permute-start.8 = (bf16[6,1,16,256]{3,1,2,0:T(2,128)(2,1)S(1)}, bf16[6,1,16,256]{3,1,2,0:T(2,128)(2,1)S(1)}, u32[]{:S(2)}, u32[]{:S(2)}) collective-permute-start(bf16[6,1,16,256]{3,1,2,0:T(2,128)(2,1)S(1)} %get-tuple-element.39), channel_id=1, source_target_pairs={{4,0},{8,4},{12,8},{16,12},{20,16},{24,20},{28,24},{5,1},{9,5},{13... | collective-permute-start | bytes 147464 | tf_op jit(solution)/shard_map/ppermute | solution.py:27
  159.2 12.7 %collective-permute-start.14 = (bf16[6,18,1,256]{3,1,2,0:T(8,128)(2,1)S(1)}, bf16[6,18,1,256]{3,1,2,0:T(8,128)(2,1)S(1)}, u32[]{:S(2)}, u32[]{:S(2)}) collective-permute-start(bf16[6,18,1,256]{3,1,2,0:T(8,128)(2,1)S(1)} %get-tuple-element.30), channel_id=1, source_target_pairs={{0,1},{1,2},{2,3},{4,5},{5,6},{6,7},{8,9},{9,10},{10,11},{12,13},{... | collective-permute-start | bytes 165896 | tf_op jit(solution)/shard_map/ppermute | solution.py:25
  163.0 8.9 %collective-permute-start.15 = (bf16[6,18,1,256]{3,1,2,0:T(8,128)(2,1)S(1)}, bf16[6,18,1,256]{3,1,2,0:T(8,128)(2,1)S(1)}, u32[]{:S(2)}, u32[]{:S(2)}) collective-permute-start(bf16[6,18,1,256]{3,1,2,0:T(8,128)(2,1)S(1)} %get-tuple-element.31), channel_id=1, source_target_pairs={{1,0},{2,1},{3,2},{5,4},{6,5},{7,6},{9,8},{10,9},{11,10},{13,12},{... | collective-permute-start | bytes 165896 | tf_op jit(solution)/shard_map/ppermute | solution.py:27
  166.1 7.1 %collective-permute-start.9 = (bf16[6,18,1,256]{3,1,2,0:T(8,128)(2,1)S(1)}, bf16[6,18,1,256]{3,1,2,0:T(8,128)(2,1)S(1)}, u32[]{:S(2)}, u32[]{:S(2)}) collective-permute-start(bf16[6,18,1,256]{3,1,2,0:T(8,128)(2,1)S(1)} %get-tuple-element.32), channel_id=1, source_target_pairs={{0,1},{1,2},{2,3},{4,5},{5,6},{6,7},{8,9},{9,10},{10,11},{12,13},{... | collective-permute-start | bytes 165896 | tf_op jit(solution)/shard_map/ppermute | solution.py:25
  170.2 6.0 %collective-permute-start.10 = (bf16[6,18,1,256]{3,1,2,0:T(8,128)(2,1)S(1)}, bf16[6,18,1,256]{3,1,2,0:T(8,128)(2,1)S(1)}, u32[]{:S(2)}, u32[]{:S(2)}) collective-permute-start(bf16[6,18,1,256]{3,1,2,0:T(8,128)(2,1)S(1)} %get-tuple-element.33), channel_id=1, source_target_pairs={{1,0},{2,1},{3,2},{5,4},{6,5},{7,6},{9,8},{10,9},{11,10},{13,12},{... | collective-permute-start | bytes 165896 | tf_op jit(solution)/shard_map/ppermute | solution.py:27
  177.1 2.1 copy-start.16
  177.2 2.1 copy-start.18
  (4 other events, 3.5 us)
Sparse Core Ops, SparseCore 0:
  137.0 179.8 all-reduce.2
